TPU v7x, 256 devices: a whole 4x4x8 slice. The times are simulated.
256 devices in a mesh: dp: 8 (over x, core), expert: 32 (over z, y).
Axes of the slice: x: 4, y: 4, z: 8, core: 2. Of those that a mesh axis runs over, the one named last changes fastest.
Arguments:
- tokens: bfloat16 [32768, 2048], P(('dp', 'expert')), may hold values from -6 to 6
- cotangent: bfloat16 [32768, 2048], P(('dp', 'expert')), may hold values from -0.875 to 0.875
- expert_ids: int32 [32768, 8], P(('dp', 'expert')), may hold values from 0 to 31, all different within a row; in each aligned block of 128 rows (0 to 127, 128 to 255, ...) at most 36 rows name the same one
- combine: float32 [32768, 8], P(('dp', 'expert')), may hold values from 0.02 to 0.5
- w_gate: bfloat16 [32, 2048, 512], P('expert'), may hold values from -0.125 to 0.125
- w_up: bfloat16 [32, 2048, 512], P('expert'), may hold values from -0.125 to 0.125
- w_down: bfloat16 [32, 512, 2048], P('expert'), may hold values from -0.25 to 0.25
- tangent_gate: bfloat16 [32, 2048, 512], P('expert'), may hold values from -0.125 to 0.125
Outputs:
- hvp_gate: float32 [32, 2048, 512], P('expert', 'dp')
- output_tangent: bfloat16 [32768, 2048], P(('dp', 'expert'))
Inputs may be any that keep to these rules, and one draw needn't show every extreme that they name: `expert_ids`: A row names 8 different experts; among the 128 rows of one device no expert is named by more than 36 rows, and in every draw some expert is named by exactly 36 rows of some device.
All inputs are finite; a program needn't handle non-finite values.
Results may differ from a plain program's by a relative error of at most 0.0057.
Values may be sent and summed in bfloat16 or wider, within the bound.
No kernel may reach another device: no remote copies, remote signals or barrier semaphores. Data moves between devices by JAX's collectives and lax.ppermute only.
A program may use at most 128 MiB of HBM per device.

v0:
```python
import jax
import jax.numpy as jnp
import numpy as np
from jax import lax
from jax.sharding import Mesh
from jax.sharding import PartitionSpec as P


def silu_derivs(gate_act):
    squash = jax.nn.sigmoid(gate_act)
    first = squash * (1.0 + gate_act * (1.0 - squash))
    second = squash * (1.0 - squash) * (2.0 + gate_act * (1.0 - 2.0 * squash))
    return (first, second)


def forward_part(rows_flat, gate_e, up_e, down_e, tangent_e):
    gate_act = jnp.dot(rows_flat, gate_e, preferred_element_type=jnp.float32)
    up_act = jnp.dot(rows_flat, up_e, preferred_element_type=jnp.float32)
    gate_dot = jnp.dot(rows_flat, tangent_e, preferred_element_type=jnp.float32)
    first, second = silu_derivs(gate_act)
    lifted = (first * gate_dot * up_act).astype(jnp.bfloat16)
    term = jnp.dot(lifted, down_e, preferred_element_type=jnp.float32).astype(jnp.bfloat16)
    return (term, up_act * second * gate_dot)


def backward_part(scaled_flat, down_e, factor):
    back_hidden = lax.dot_general(
        scaled_flat, down_e, (((1,), (1,)), ((), ())), preferred_element_type=jnp.float32
    )
    return (back_hidden * factor).astype(jnp.bfloat16)


def per_device(tokens, cotangent, expert_ids, combine, w_gate, w_up, w_down, tangent_gate):
    n_z = lax.axis_size("ez")
    n_y = lax.axis_size("ey")
    expert_count = n_z * n_y
    rows_dev, top_count = expert_ids.shape
    model_width = tokens.shape[1]
    capacity = rows_dev * top_count * 9 // (8 * expert_count)
    owners = jnp.arange(expert_count, dtype=jnp.int32)
    matches = (expert_ids[:, :, None] == owners[None, None, :]).astype(jnp.int32)
    named_count = jnp.sum(matches, axis=1)
    before = jnp.cumsum(named_count, axis=0) - named_count
    slot_pos = jnp.sum(before[:, None, :] * matches, axis=2)
    target = (expert_ids * capacity + slot_pos).reshape(-1)
    slots = expert_count * capacity
    token_index = jnp.repeat(jnp.arange(rows_dev, dtype=jnp.float32), top_count)
    src_of = jnp.full((slots,), -1.0, jnp.float32).at[target].set(token_index)
    w_of = jnp.zeros((slots,), jnp.float32).at[target].set(combine.reshape(-1))
    w_hi = lax.reduce_precision(w_of, exponent_bits=8, mantissa_bits=7)
    rest = w_of - w_hi
    w_mid = lax.reduce_precision(rest, exponent_bits=8, mantissa_bits=7)
    w_lo = rest - w_mid
    table = jnp.stack([src_of, w_hi, w_mid, w_lo]).astype(jnp.bfloat16)
    extra = 16
    table = jnp.pad(table.reshape(-1), (0, extra * model_width - 4 * slots))
    packed = jnp.concatenate([tokens, table.reshape(extra, model_width)], axis=0)

    tok_g = lax.all_gather(packed, "ez", axis=0)
    cot_g = lax.all_gather(cotangent, "ez", axis=0, tiled=True)
    table_g = tok_g[:, rows_dev:].reshape(n_z, -1)[:, : 4 * slots].reshape(n_z, 4, expert_count, capacity)
    tok_g = tok_g[:, :rows_dev].reshape(n_z * rows_dev, model_width)
    z_me = lax.axis_index("ez")
    mine = lax.dynamic_slice_in_dim(table_g, z_me * n_y, n_y, axis=2).astype(jnp.float32)
    mine = jnp.transpose(mine, (1, 2, 0, 3))
    src_tok = mine[0]
    src_w = (mine[1] + mine[2]) + mine[3]
    gidx = jnp.maximum(
        src_tok.astype(jnp.int32) + (jnp.arange(n_z, dtype=jnp.int32) * rows_dev)[None, :, None], 0
    ).reshape(-1)
    send_rows = tok_g[gidx]
    send_scaled = (src_w.reshape(-1)[:, None] * cot_g[gidx].astype(jnp.float32)).astype(jnp.bfloat16)

    rows_flat = lax.all_to_all(send_rows, "ey", split_axis=0, concat_axis=0, tiled=True)
    scaled_flat = lax.all_to_all(send_scaled, "ey", split_axis=0, concat_axis=0, tiled=True)
    gate_e = w_gate[0]
    up_e = w_up[0]
    down_e = w_down[0]
    tangent_e = tangent_gate[0]
    term, factor = forward_part(rows_flat, gate_e, up_e, down_e, tangent_e)
    returned = lax.all_to_all(term, ("ey", "ez"), split_axis=0, concat_axis=0, tiled=True)
    coeff = backward_part(scaled_flat, down_e, factor)
    partial_hvp = lax.dot_general(
        rows_flat, coeff, (((0,), (0,)), ((), ())), preferred_element_type=jnp.float32
    )
    hvp_gate = lax.psum_scatter(partial_hvp, "dp", scatter_dimension=0, tiled=True)
    back_at = (((expert_ids % n_y) * n_z + expert_ids // n_y) * capacity + slot_pos).reshape(-1)
    picked = returned[back_at].reshape(rows_dev, top_count, model_width)
    output_tangent = jnp.sum(combine[:, :, None] * picked.astype(jnp.float32), axis=1).astype(
        jnp.bfloat16
    )
    return (hvp_gate[None], output_tangent)


def y_size(mesh):
    column = mesh.devices[0]
    try:
        return len({int(d.coords[1]) for d in column})
    except Exception:
        return 4


def solution(mesh):
    n_dp, n_expert = mesh.devices.shape
    n_y = y_size(mesh)
    mesh3 = Mesh(mesh.devices.reshape(n_dp, n_expert // n_y, n_y), ("dp", "ez", "ey"))
    rows = P(("dp", "ez", "ey"), None)
    weights = P(("ez", "ey"), None, None)
    placed = (rows, rows, rows, rows, weights, weights, weights, weights)
    return jax.shard_map(
        per_device,
        mesh=mesh3,
        in_specs=placed,
        out_specs=(P(("ez", "ey"), "dp", None), rows),
        check_vma=False,
    )
```

profile of v0, /device:TPU:32, one launch (start us, length us, event | category | flops | bytes accessed | tf_op | source)
XLA Modules:
  0.0 376.6 jit_solution(12889950200578065263)
XLA Ops:
  7.2 0.8 convert_reduce_fusion
  8.1 0.1 copy.40
  8.2 0.8 copy.44
  9.0 0.1 reshape.208
  9.1 0.2 reduce_window_sum.11
  9.2 0.1 copy.42
  9.3 0.7 select_reduce_fusion
  10.0 0.7 fusion.28
  10.7 0.1 copy.43
  10.8 0.1 reshape.162
  10.9 4.3 %scatter_custom_fusion.1 = f32[1152]{0:T(1024)S(1)} fusion(s32[1024]{0:T(1024)S(1)} %bitcast.52, f32[1024]{0:T(1024)S(1)} %reshape.208, f32[]{:T(128)} %constant.51.clone.1), kind=kCustom, calls=%fused_computation.64 | custom fusion | bytes 4612 | tf_op jit(solution)/shard_map/scatter | solution.py:49
  15.4 0.1 reshape.200
  15.4 4.3 %scatter_custom_fusion = f32[1152]{0:T(1024)S(1)} fusion(s32[1024]{0:T(1024)S(1)} %bitcast.53, f32[1024]{0:T(1024)S(1)} %reshape.200, f32[]{:T(128)} %constant.27.clone.1), kind=kCustom, calls=%fused_computation.67 | custom fusion | bytes 4612 | tf_op jit(solution)/shard_map/scatter | solution.py:48
  19.9 2.0 pad_maximum_fusion
  21.9 0.0 all-gather.4.cloned.1.call-start
  21.9 0.7 all-gather.4.cloned.1.call-update
  22.7 0.1 add.95
  22.7 0.1 add.96
  22.8 59.8 %all-gather.6.cloned.1.call-done = bf16[1152,2048]{1,0:T(8,128)(2,1)} async-done(((bf16[144,2048]{1,0:T(8,128)(2,1)}), bf16[1152,2048]{1,0:T(8,128)(2,1)}) %all-gather.6.cloned.1.call-update) | async-done | bytes 4718608 | tf_op jit(solution)/shard_map/all_gather | solution.py:59
  82.6 4.8 %slice.34 = bf16[8,128,2048]{2,1,0:T(8,128)(2,1)} slice(bf16[8,144,2048]{2,1,0:T(8,128)(2,1)} %bitcast.48), slice={[0:8], [0:128], [0:2048]} | slice | bytes 8388608 | tf_op jit(solution)/shard_map/slice | solution.py:62
  87.4 1.1 slice_bitcast_fusion
  88.5 0.3 copy.49
  88.8 0.6 reshape.168
  89.5 0.1 convert_element_type.57
  89.6 13.4 %gather_fusion = bf16[1152,2048]{1,0:T(8,128)(2,1)} fusion(bf16[1024,2048]{1,0:T(8,128)(2,1)} %bitcast.45, s32[2048]{0:T(1024)S(1)} %pad_clamp_fusion), kind=kCustom, calls=%fused_computation | custom fusion | bytes 9441792 | tf_op jit(solution)/shard_map/gather | solution.py:71
  103.0 5.0 %all-to-all-start = ((bf16[4,288,2048]{2,1,0:T(8,128)(2,1)}), bf16[4,288,2048]{2,1,0:T(8,128)(2,1)}, u32[]{:S(2)}, u32[]{:S(2)}) async-start(bf16[4,288,2048]{2,1,0:T(8,128)(2,1)} %bitcast.46), calls=%async_computation | async-start | bytes 9437184 | tf_op jit(solution)/shard_map/all_to_all | solution.py:74
  108.0 0.1 add.100
  108.1 29.8 %all-gather.4.cloned.1.call-done = bf16[1024,2048]{1,0:T(8,128)(2,1)} async-done(((bf16[128,2048]{1,0:T(8,128)(2,1)}), bf16[1024,2048]{1,0:T(8,128)(2,1)}) %all-gather.4.cloned.1.call-update) | async-done | bytes 4194320 | tf_op jit(solution)/shard_map/all_gather | solution.py:60
  137.8 13.4 %gather_fusion.1 = bf16[1152,2048]{1,0:T(8,128)(2,1)} fusion(bf16[1024,2048]{1,0:T(8,128)(2,1)} %all-gather.4.cloned.1.call-done, s32[2048]{0:T(1024)S(1)} %pad_clamp_fusion), kind=kCustom, calls=%fused_computation.1 | custom fusion | bytes 9441792 | tf_op jit(solution)/shard_map/gather | solution.py:72
  151.2 5.4 %fusion = bf16[4,288,2048]{2,1,0:T(8,128)(2,1)} fusion(bf16[4,288,2048]{2,1,0:T(8,128)(2,1)} %bitcast.47, f32[4,288]{1,0:T(4,128)S(1)} %add.100), kind=kLoop, calls=%fused_computation.6 | loop fusion | flops 7077888 | bytes 9441792 | tf_op jit(solution)/shard_map/convert_element_type | solution.py:72
  156.6 6.1 %all-to-all-done = bf16[4,288,2048]{2,1,0:T(8,128)(2,1)} async-done(((bf16[4,288,2048]{2,1,0:T(8,128)(2,1)}), bf16[4,288,2048]{2,1,0:T(8,128)(2,1)}, u32[]{:S(2)}, u32[]{:S(2)}) %all-to-all-start) | async-done | bytes 4718624 | tf_op jit(solution)/shard_map/all_to_all | solution.py:74
  162.7 5.1 %all-to-all-start.1 = ((bf16[4,288,2048]{2,1,0:T(8,128)(2,1)}), bf16[4,288,2048]{2,1,0:T(8,128)(2,1)}, u32[]{:S(2)}, u32[]{:S(2)}) async-start(bf16[4,288,2048]{2,1,0:T(8,128)(2,1)} %fusion), calls=%async_computation.1 | async-start | bytes 9437184 | tf_op jit(solution)/shard_map/all_to_all | solution.py:75
  167.9 5.2 %fusion.11 = f32[1152,512]{1,0:T(8,128)S(1)} fusion(bf16[1152,2048]{1,0:T(8,128)(2,1)} %bitcast.5, bf16[1,2048,512]{2,1,0:T(8,128)(2,1)} %param.15), kind=kOutput, calls=%fused_computation.23 | convolution fusion | flops 2415919104 | bytes 9175040 | tf_op jit(solution)/shard_map/dot_general | solution.py:19
  173.2 5.3 %fusion.13 = f32[1152,512]{1,0:T(8,128)S(1)} fusion(bf16[1152,2048]{1,0:T(8,128)(2,1)} %bitcast.5, bf16[1,2048,512]{2,1,0:T(8,128)(2,1)S(1)} %copy-done.1), kind=kOutput, calls=%fused_computation.25 | convolution fusion | flops 2415919104 | bytes 9175040 | tf_op jit(solution)/shard_map/dot_general | solution.py:17
  178.5 5.3 %fusion.15 = f32[1152,512]{1,0:T(8,128)S(1)} fusion(bf16[1152,2048]{1,0:T(8,128)(2,1)} %bitcast.5, bf16[1,2048,512]{2,1,0:T(8,128)(2,1)S(1)} %copy-done.2), kind=kOutput, calls=%fused_computation.27 | convolution fusion | flops 2415919104 | bytes 9175040 | tf_op jit(solution)/shard_map/dot_general | solution.py:18
  183.9 1.4 copy-done.5
  185.2 4.8 %convolution_convert_fusion = bf16[1152,2048]{1,0:T(8,128)(2,1)} fusion(bf16[1,512,2048]{2,1,0:T(8,128)(2,1)S(1)} %copy-done, f32[1152,512]{1,0:T(8,128)S(1)} %fusion.15, f32[1152,512]{1,0:T(8,128)S(1)} %fusion.11, f32[1152,512]{1,0:T(8,128)S(1)} %fusion.13), kind=kOutput, calls=%fused_computation.9 | convolution fusion | flops 2424176640 | bytes 13893632 | tf_op jit(solution)/shard_map/dot_general | solution.py:22
  190.1 7.2 %all_to_all.27 = bf16[32,36,2048]{2,1,0:T(8,128)(2,1)} reshape(bf16[1152,2048]{1,0:T(8,128)(2,1)} %convolution_convert_fusion) | data formatting | bytes 9437184 | tf_op jit(solution)/shard_map/all_to_all | solution.py:81
  197.3 24.3 %all-to-all-done.1 = bf16[4,288,2048]{2,1,0:T(8,128)(2,1)} async-done(((bf16[4,288,2048]{2,1,0:T(8,128)(2,1)}), bf16[4,288,2048]{2,1,0:T(8,128)(2,1)}, u32[]{:S(2)}, u32[]{:S(2)}) %all-to-all-start.1) | async-done | bytes 4718624 | tf_op jit(solution)/shard_map/all_to_all | solution.py:75
  221.6 7.4 %all-to-all-start.2 = ((bf16[32,36,2048]{2,1,0:T(8,128)(2,1)}), bf16[32,36,2048]{2,1,0:T(8,128)(2,1)}, u32[]{:S(2)}, u32[]{:S(2)}) async-start(bf16[32,36,2048]{2,1,0:T(8,128)(2,1)} %all_to_all.27), calls=%async_computation.3 | async-start | bytes 10485760 | tf_op jit(solution)/shard_map/all_to_all | solution.py:81
  229.0 0.0 reduce-scatter.2.cloned.1.call-start
  229.0 14.0 %fusion.22 = f32[2048,512]{1,0:T(8,128)} fusion(bf16[1152,2048]{1,0:T(8,128)(2,1)} %bitcast.5, bf16[1152,2048]{1,0:T(8,128)(2,1)} %bitcast.7, f32[1152,512]{1,0:T(8,128)} %copy-done.3, f32[1152,512]{1,0:T(8,128)} %copy-done.5, f32[1152,512]{1,0:T(8,128)} %copy-done.4, bf16[1,512,2048]{2,1,0:T(8,128)(2,1)S(1)} %copy-done), kind=kOutput, calls=%fused_computation.40 | convolution fusion | flops 4840095744 | bytes 22806528 | tf_op jit(solution)/shard_map/dot_general | solution.py:83
  243.1 0.1 copy.47
  243.2 0.1 reshape.169
  243.3 100.4 %all-to-all-done.2 = bf16[32,36,2048]{2,1,0:T(8,128)(2,1)} async-done(((bf16[32,36,2048]{2,1,0:T(8,128)(2,1)}), bf16[32,36,2048]{2,1,0:T(8,128)(2,1)}, u32[]{:S(2)}, u32[]{:S(2)}) %all-to-all-start.2) | async-done | bytes 4718624 | tf_op jit(solution)/shard_map/all_to_all | solution.py:81
  343.7 7.3 %all_to_all.29 = bf16[1152,2048]{1,0:T(8,128)(2,1)} reshape(bf16[32,36,2048]{2,1,0:T(8,128)(2,1)} %all-to-all-done.2) | data formatting | bytes 9437184 | tf_op jit(solution)/shard_map/all_to_all | solution.py:81
  351.0 11.8 %gather_fusion.2 = bf16[1024,2048]{1,0:T(8,128)(2,1)} fusion(bf16[1152,2048]{1,0:T(8,128)(2,1)} %all_to_all.29, s32[1024]{0:T(1024)S(1)} %broadcast_clamp_fusion), kind=kCustom, calls=%fused_computation.2 | custom fusion | bytes 8392704 | tf_op jit(solution)/shard_map/gather | solution.py:88
  362.8 7.3 %fusion.1 = bf16[128,2048]{1,0:T(8,128)(2,1)} fusion(bf16[1024,2048]{1,0:T(8,128)(2,1)} %gather_fusion.2, f32[128,8]{1,0:T(8,128)S(1)} %copy.44), kind=kLoop, calls=%fused_computation.8 | loop fusion | flops 6029312 | bytes 4722688 | tf_op jit(solution)/shard_map/reduce_sum | solution.py:89
  (37 shorter events, 0.4 us)
Async XLA Ops:
  7.2 178.1 %copy-start = (bf16[1,512,2048]{2,1,0:T(8,128)(2,1)S(1)}, bf16[1,512,2048]{2,1,0:T(8,128)(2,1)}, u32[]{:S(2)}) copy-start(bf16[1,512,2048]{2,1,0:T(8,128)(2,1)} %param.14) | copy-start | bytes 6291460
  7.2 75.4 %all-gather.6.cloned.1.call-start = ((), (), s32[]{:S(2)}) async-start(), calls=%async_computation.6 | async-start | bytes 5308416 | tf_op jit(solution)/shard_map/all_gather | solution.py:59
  21.9 115.9 %all-gather.4.cloned.1.call-start = ((), (), s32[]{:S(2)}) async-start(), calls=%async_computation.4 | async-start | bytes 4718592 | tf_op jit(solution)/shard_map/all_gather | solution.py:60
  103.0 59.7 %all-to-all-start = ((bf16[4,288,2048]{2,1,0:T(8,128)(2,1)}), bf16[4,288,2048]{2,1,0:T(8,128)(2,1)}, u32[]{:S(2)}, u32[]{:S(2)}) async-start(bf16[4,288,2048]{2,1,0:T(8,128)(2,1)} %bitcast.46), calls=%async_computation | async-start | bytes 9437184 | tf_op jit(solution)/shard_map/all_to_all | solution.py:74
  162.7 58.8 %all-to-all-start.1 = ((bf16[4,288,2048]{2,1,0:T(8,128)(2,1)}), bf16[4,288,2048]{2,1,0:T(8,128)(2,1)}, u32[]{:S(2)}, u32[]{:S(2)}) async-start(bf16[4,288,2048]{2,1,0:T(8,128)(2,1)} %fusion), calls=%async_computation.1 | async-start | bytes 9437184 | tf_op jit(solution)/shard_map/all_to_all | solution.py:75
  167.9 5.3 %copy-start.1 = (bf16[1,2048,512]{2,1,0:T(8,128)(2,1)S(1)}, bf16[1,2048,512]{2,1,0:T(8,128)(2,1)}, u32[]{:S(2)}) copy-start(bf16[1,2048,512]{2,1,0:T(8,128)(2,1)} %param.12) | copy-start | bytes 6291460
  173.1 10.7 %copy-start.3 = (f32[1152,512]{1,0:T(8,128)}, f32[1152,512]{1,0:T(8,128)S(1)}, u32[]{:S(2)}) copy-start(f32[1152,512]{1,0:T(8,128)S(1)} %fusion.11) | copy-start | bytes 7077892
  173.2 5.4 %copy-start.2 = (bf16[1,2048,512]{2,1,0:T(8,128)(2,1)S(1)}, bf16[1,2048,512]{2,1,0:T(8,128)(2,1)}, u32[]{:S(2)}) copy-start(bf16[1,2048,512]{2,1,0:T(8,128)(2,1)} %param.13) | copy-start | bytes 6291460
  178.5 5.3 %copy-start.4 = (f32[1152,512]{1,0:T(8,128)}, f32[1152,512]{1,0:T(8,128)S(1)}, u32[]{:S(2)}) copy-start(f32[1152,512]{1,0:T(8,128)S(1)} %fusion.13) | copy-start | bytes 7077892
  183.9 1.4 copy-start.5
  221.6 122.1 %all-to-all-start.2 = ((bf16[32,36,2048]{2,1,0:T(8,128)(2,1)}), bf16[32,36,2048]{2,1,0:T(8,128)(2,1)}, u32[]{:S(2)}, u32[]{:S(2)}) async-start(bf16[32,36,2048]{2,1,0:T(8,128)(2,1)} %all_to_all.27), calls=%async_computation.3 | async-start | bytes 10485760 | tf_op jit(solution)/shard_map/all_to_all | solution.py:81
  229.0 141.1 %reduce-scatter.2.cloned.1.call-start = ((), (), s32[]{:S(2)}) async-start(), calls=%async_computation.5 | async-start | bytes 4718592 | tf_op jit(solution)/shard_map/reduce_scatter | solution.py:86
Sparse Core Ops, SparseCore 0:
  22.0 60.5 all-gather.5
  84.4 53.4 all-gather.3
  243.2 42.1 reduce-scatter.1
where the time goes:
time: 381 us; the launch traced here: 377 us
  waiting for transfers between devices  221 us (58%)
  local copies, waits for them, and re-layouts  71.9 us (19%)
  matrix products  34.7 us (9%)
  starting transfers between devices  17.6 us (5%)
  other arithmetic  17.2 us (5%)
  between operations  14.1 us (4%)
    all_to_all x1, waiting for transfers between devices, per_device(): lax.all_to_all(term, ('ey', 'ez'), split_axis=0, concat_axis=0, tiled=True)  100 us
    all_gather x1, waiting for transfers between devices, per_device(): tok_g = lax.all_gather(packed, 'ez', axis=0)  59.8 us
    all_gather x1, waiting for transfers between devices, per_device(): cot_g = lax.all_gather(cotangent, 'ez', axis=0, tiled=True)  29.8 us
    all_to_all x1, waiting for transfers between devices, per_device(): lax.all_to_all(send_scaled, 'ey', split_axis=0, concat_axis=0, tiled=True)  24.3 us
    all_to_all x2, local copies, waits for them, and re-layouts, per_device(): lax.all_to_all(term, ('ey', 'ez'), split_axis=0, concat_axis=0, tiled=True)  14.5 us
    dot_general x1, matrix products, per_device(): lax.dot_general(rows_flat, coeff, (((0,), (0,)), ((), ())), preferred_ele...  14 us
    gather x1, local copies, waits for them, and re-layouts, per_device(): cot_g[gidx].astype(jnp.float32)  13.4 us
    gather x1, local copies, waits for them, and re-layouts, per_device(): send_rows = tok_g[gidx]  13.4 us
  transfers between devices with their start and end apart: 6, of which 5 were waited for; matrix products, arithmetic and copies ran while one was open for 25% of the time, Pallas kernels for 0%

commit v1 on v0

--- a/solution.py
+++ b/solution.py
@@ -30,6 +30,18 @@
     return (back_hidden * factor).astype(jnp.bfloat16)
 
 
+def split3(value):
+    hi = lax.reduce_precision(value, exponent_bits=8, mantissa_bits=7)
+    rest = value - hi
+    mid = lax.reduce_precision(rest, exponent_bits=8, mantissa_bits=7)
+    return (hi, mid, rest - mid)
+
+
+def select_rows(index, source):
+    picks = (index[:, None] == jnp.arange(source.shape[0], dtype=jnp.int32)[None, :]).astype(source.dtype)
+    return jnp.dot(picks, source, preferred_element_type=jnp.float32)
+
+
 def per_device(tokens, cotangent, expert_ids, combine, w_gate, w_up, w_down, tangent_gate):
     n_z = lax.axis_size("ez")
     n_y = lax.axis_size("ey")
@@ -38,38 +50,40 @@
     model_width = tokens.shape[1]
     capacity = rows_dev * top_count * 9 // (8 * expert_count)
     owners = jnp.arange(expert_count, dtype=jnp.int32)
-    matches = (expert_ids[:, :, None] == owners[None, None, :]).astype(jnp.int32)
+    chosen = expert_ids[:, :, None] == owners[None, None, :]
+    matches = chosen.astype(jnp.int32)
     named_count = jnp.sum(matches, axis=1)
     before = jnp.cumsum(named_count, axis=0) - named_count
     slot_pos = jnp.sum(before[:, None, :] * matches, axis=2)
-    target = (expert_ids * capacity + slot_pos).reshape(-1)
     slots = expert_count * capacity
-    token_index = jnp.repeat(jnp.arange(rows_dev, dtype=jnp.float32), top_count)
-    src_of = jnp.full((slots,), -1.0, jnp.float32).at[target].set(token_index)
-    w_of = jnp.zeros((slots,), jnp.float32).at[target].set(combine.reshape(-1))
-    w_hi = lax.reduce_precision(w_of, exponent_bits=8, mantissa_bits=7)
-    rest = w_of - w_hi
-    w_mid = lax.reduce_precision(rest, exponent_bits=8, mantissa_bits=7)
-    w_lo = rest - w_mid
-    table = jnp.stack([src_of, w_hi, w_mid, w_lo]).astype(jnp.bfloat16)
+    in_slot = (named_count[:, :, None] > 0) & (
+        before[:, :, None] == jnp.arange(capacity, dtype=jnp.int32)[None, None, :]
+    )
+    token_no = jnp.arange(rows_dev, dtype=jnp.float32)[:, None, None]
+    src_of = jnp.sum(jnp.where(in_slot, token_no + 1.0, 0.0), axis=0) - 1.0
+    weight_te = jnp.sum(jnp.where(chosen, combine[:, :, None], 0.0), axis=1)
+    w_of = jnp.sum(jnp.where(in_slot, weight_te[:, :, None], 0.0), axis=0)
+    table = jnp.stack((src_of,) + split3(w_of)).astype(jnp.bfloat16)
     extra = 16
     table = jnp.pad(table.reshape(-1), (0, extra * model_width - 4 * slots))
     packed = jnp.concatenate([tokens, table.reshape(extra, model_width)], axis=0)
+    block = rows_dev + extra
 
-    tok_g = lax.all_gather(packed, "ez", axis=0)
+    tok_g = lax.all_gather(packed, "ez", axis=0, tiled=True)
     cot_g = lax.all_gather(cotangent, "ez", axis=0, tiled=True)
-    table_g = tok_g[:, rows_dev:].reshape(n_z, -1)[:, : 4 * slots].reshape(n_z, 4, expert_count, capacity)
-    tok_g = tok_g[:, :rows_dev].reshape(n_z * rows_dev, model_width)
+    table_g = tok_g.reshape(n_z, block, model_width)[:, rows_dev:].reshape(n_z, -1)
+    table_g = table_g[:, : 4 * slots].reshape(n_z, 4, expert_count, capacity)
     z_me = lax.axis_index("ez")
     mine = lax.dynamic_slice_in_dim(table_g, z_me * n_y, n_y, axis=2).astype(jnp.float32)
     mine = jnp.transpose(mine, (1, 2, 0, 3))
-    src_tok = mine[0]
+    src_tok = mine[0].astype(jnp.int32)
     src_w = (mine[1] + mine[2]) + mine[3]
-    gidx = jnp.maximum(
-        src_tok.astype(jnp.int32) + (jnp.arange(n_z, dtype=jnp.int32) * rows_dev)[None, :, None], 0
-    ).reshape(-1)
-    send_rows = tok_g[gidx]
-    send_scaled = (src_w.reshape(-1)[:, None] * cot_g[gidx].astype(jnp.float32)).astype(jnp.bfloat16)
+    valid = src_tok >= 0
+    z_of = jnp.arange(n_z, dtype=jnp.int32)[None, :, None]
+    at_packed = jnp.where(valid, src_tok + z_of * block, -1).reshape(-1)
+    at_cot = jnp.where(valid, src_tok + z_of * rows_dev, -1).reshape(-1)
+    send_rows = select_rows(at_packed, tok_g).astype(jnp.bfloat16)
+    send_scaled = (src_w.reshape(-1)[:, None] * select_rows(at_cot, cot_g)).astype(jnp.bfloat16)
 
     rows_flat = lax.all_to_all(send_rows, "ey", split_axis=0, concat_axis=0, tiled=True)
     scaled_flat = lax.all_to_all(send_scaled, "ey", split_axis=0, concat_axis=0, tiled=True)
@@ -84,12 +98,13 @@
         rows_flat, coeff, (((0,), (0,)), ((), ())), preferred_element_type=jnp.float32
     )
     hvp_gate = lax.psum_scatter(partial_hvp, "dp", scatter_dimension=0, tiled=True)
-    back_at = (((expert_ids % n_y) * n_z + expert_ids // n_y) * capacity + slot_pos).reshape(-1)
-    picked = returned[back_at].reshape(rows_dev, top_count, model_width)
-    output_tangent = jnp.sum(combine[:, :, None] * picked.astype(jnp.float32), axis=1).astype(
-        jnp.bfloat16
-    )
-    return (hvp_gate[None], output_tangent)
+    back_at = ((expert_ids % n_y) * n_z + expert_ids // n_y) * capacity + slot_pos
+    at_slot = back_at[:, :, None] == jnp.arange(slots, dtype=jnp.int32)[None, None, :]
+    output_tangent = jnp.zeros((rows_dev, model_width), jnp.float32)
+    for piece in split3(combine):
+        spread = jnp.sum(jnp.where(at_slot, piece[:, :, None], 0.0), axis=1).astype(jnp.bfloat16)
+        output_tangent = output_tangent + jnp.dot(spread, returned, preferred_element_type=jnp.float32)
+    return (hvp_gate[None], output_tangent.astype(jnp.bfloat16))
 
 
 def y_size(mesh):

time: 381 us -> 350 us (0.919)
  local copies, waits for them, and re-layouts: 71.9 us -> 20.3 us
  matrix products: 34.7 us -> 60.4 us
  other arithmetic: 17.2 us -> 8.99 us
  waiting for transfers between devices: 221 us -> 225 us
    gather x3 -> x0, local copies, waits for them, and re-layouts: 38.6 us -> none  [the longest x1 13.4 us: per_device(): cot_g[gidx].astype(jnp.float32)]
    dot_general x0 -> x5, matrix products: none -> 25.6 us  [the longest x2 19.7 us: select_rows(): return jnp.dot(picks, source, preferred_element_type=jnp.float32)]
    scatter x2 -> x0, local copies, waits for them, and re-layouts: 8.63 us -> none  [the longest x1 4.32 us: per_device(): w_of = jnp.zeros((slots,), jnp.float32).at[target].set(combine.reshape(-1))]
    all_gather x1, waiting for transfers between devices: 29.8 us -> 37.5 us  [per_device(): cot_g = lax.all_gather(cotangent, 'ez', axis=0, tiled=True)]
    all_to_all x1, waiting for transfers between devices: 100 us -> 94.9 us  [per_device(): lax.all_to_all(term, ('ey', 'ez'), split_axis=0, concat_axis=0, tiled=True)]
    convert_element_type x1 -> x0, other arithmetic: 5.36 us -> none  [per_device(): (src_w.reshape(-1)[:, None] * cot_g[gidx].astype(jnp.float32)).astype(jnp...]
    slice x2 -> x1, local copies, waits for them, and re-layouts: 4.78 us -> 0.01 us  [per_device(): table_g = table_g[:, :4 * slots].reshape(n_z, 4, expert_count, capacity)]
  transfers between devices with their start and end apart: 6 -> 6, of which waited for: 5 -> 5; matrix products, arithmetic and copies ran while one was open for 25% -> 20% of each run, Pallas kernels for 0% -> 0%
where the time goes in v1:
time: 350 us; the launch traced here: 347 us
  waiting for transfers between devices  225 us (64%)
  matrix products  60.4 us (17%)
  local copies, waits for them, and re-layouts  20.3 us (6%)
  starting transfers between devices  17.7 us (5%)
  between operations  14.1 us (4%)
  other arithmetic  8.99 us (3%)
    all_to_all x1, waiting for transfers between devices, per_device(): lax.all_to_all(term, ('ey', 'ez'), split_axis=0, concat_axis=0, tiled=True)  94.9 us
    all_gather x1, waiting for transfers between devices, per_device(): tok_g = lax.all_gather(packed, 'ez', axis=0, tiled=True)  59.6 us
    all_gather x1, waiting for transfers between devices, per_device(): cot_g = lax.all_gather(cotangent, 'ez', axis=0, tiled=True)  37.5 us
    all_to_all x1, waiting for transfers between devices, per_device(): lax.all_to_all(send_scaled, 'ey', split_axis=0, concat_axis=0, tiled=True)  24.4 us
    dot_general x2, matrix products, select_rows(): return jnp.dot(picks, source, preferred_element_type=jnp.float32)  19.7 us
    all_to_all x2, local copies, waits for them, and re-layouts, per_device(): lax.all_to_all(term, ('ey', 'ez'), split_axis=0, concat_axis=0, tiled=True)  14.4 us
    dot_general x1, matrix products, per_device(): lax.dot_general(rows_flat, coeff, (((0,), (0,)), ((), ())), preferred_ele...  14 us
    all_to_all x1, waiting for transfers between devices, per_device(): lax.all_to_all(send_rows, 'ey', split_axis=0, concat_axis=0, tiled=True)  7.92 us
  transfers between devices with their start and end apart: 6, of which 5 were waited for; matrix products, arithmetic and copies ran while one was open for 20% of the time, Pallas kernels for 0%

profile of v1, /device:TPU:32, one launch (start us, length us, event | category | flops | bytes accessed | tf_op | source)
XLA Modules:
  0.0 346.5 jit_solution(554096132738252504)
XLA Ops:
  7.2 0.8 convert_reduce_fusion
  8.1 0.1 copy.51
  8.2 0.2 reduce_window_sum.11
  8.4 0.1 copy.53
  8.4 0.7 select_reduce_fusion.6
  9.2 0.4 select_reduce_fusion.4
  9.6 0.1 copy.54
  9.7 0.1 convert_element_type.54
  9.9 2.0 pad_maximum_fusion
  12.0 0.7 all-gather.5.cloned.1.call-update
  12.7 0.1 add.110
  12.8 0.1 add.111
  12.9 0.1 add.104
  13.0 0.1 add.105
  13.1 59.6 %all-gather.3.cloned.1.call-done = bf16[1152,2048]{1,0:T(8,128)(2,1)} async-done(((bf16[144,2048]{1,0:T(8,128)(2,1)}), bf16[1152,2048]{1,0:T(8,128)(2,1)}) %all-gather.3.cloned.1.call-update) | async-done | bytes 4718608 | tf_op jit(solution)/shard_map/all_gather | solution.py:72
  72.6 1.1 slice_bitcast_fusion
  73.7 0.3 copy.62
  74.0 0.6 reshape.140
  74.8 0.1 convert_element_type.56
  74.9 10.4 %convolution_convert_fusion = bf16[1152,2048]{1,0:T(8,128)(2,1)} fusion(bf16[1152,2048]{1,0:T(8,128)(2,1)} %all-gather.3.cloned.1.call-done, s32[1152]{0:T(1024)S(1)} %get-tuple-element.13), kind=kOutput, calls=%fused_computation.1 | convolution fusion | flops 5439504384 | bytes 9441792 | tf_op jit(solution)/shard_map/dot_general | solution.py:42
  85.3 4.9 %all-to-all-start = ((bf16[4,288,2048]{2,1,0:T(8,128)(2,1)}), bf16[4,288,2048]{2,1,0:T(8,128)(2,1)}, u32[]{:S(2)}, u32[]{:S(2)}) async-start(bf16[4,288,2048]{2,1,0:T(8,128)(2,1)} %bitcast.54), calls=%async_computation | async-start | bytes 9437184 | tf_op jit(solution)/shard_map/all_to_all | solution.py:88
  90.3 0.1 add.109
  90.4 37.5 %all-gather.5.cloned.1.call-done = bf16[1024,2048]{1,0:T(8,128)(2,1)} async-done(((bf16[128,2048]{1,0:T(8,128)(2,1)}), bf16[1024,2048]{1,0:T(8,128)(2,1)}) %all-gather.5.cloned.1.call-update) | async-done | bytes 4194320 | tf_op jit(solution)/shard_map/all_gather | solution.py:73
  127.9 9.2 %fusion = bf16[1152,2048]{1,0:T(8,128)(2,1)} fusion(bf16[1024,2048]{1,0:T(8,128)(2,1)} %all-gather.5.cloned.1.call-done, f32[1152]{0:T(1024)S(1)} %add.109, s32[1152]{0:T(1024)S(1)} %get-tuple-element.12), kind=kOutput, calls=%fused_computation.2 | convolution fusion | flops 4837736448 | bytes 8922112 | tf_op jit(solution)/shard_map/dot_general | solution.py:42
  137.1 7.9 %all-to-all-done = bf16[4,288,2048]{2,1,0:T(8,128)(2,1)} async-done(((bf16[4,288,2048]{2,1,0:T(8,128)(2,1)}), bf16[4,288,2048]{2,1,0:T(8,128)(2,1)}, u32[]{:S(2)}, u32[]{:S(2)}) %all-to-all-start) | async-done | bytes 4718624 | tf_op jit(solution)/shard_map/all_to_all | solution.py:88
  145.0 5.0 %all-to-all-start.1 = ((bf16[4,288,2048]{2,1,0:T(8,128)(2,1)}), bf16[4,288,2048]{2,1,0:T(8,128)(2,1)}, u32[]{:S(2)}, u32[]{:S(2)}) async-start(bf16[4,288,2048]{2,1,0:T(8,128)(2,1)} %bitcast.53), calls=%async_computation.1 | async-start | bytes 9437184 | tf_op jit(solution)/shard_map/all_to_all | solution.py:89
  150.0 5.2 %fusion.13 = f32[1152,512]{1,0:T(8,128)S(1)} fusion(bf16[1152,2048]{1,0:T(8,128)(2,1)} %bitcast.5, bf16[1,2048,512]{2,1,0:T(8,128)(2,1)} %param.15), kind=kOutput, calls=%fused_computation.28 | convolution fusion | flops 2415919104 | bytes 9175040 | tf_op jit(solution)/shard_map/dot_general | solution.py:19
  155.3 5.3 %fusion.17 = f32[1152,512]{1,0:T(8,128)S(1)} fusion(bf16[1152,2048]{1,0:T(8,128)(2,1)} %bitcast.5, bf16[1,2048,512]{2,1,0:T(8,128)(2,1)S(1)} %copy-done.4), kind=kOutput, calls=%fused_computation.32 | convolution fusion | flops 2415919104 | bytes 9175040 | tf_op jit(solution)/shard_map/dot_general | solution.py:18
  160.6 5.3 %fusion.15 = f32[1152,512]{1,0:T(8,128)S(1)} fusion(bf16[1152,2048]{1,0:T(8,128)(2,1)} %bitcast.5, bf16[1,2048,512]{2,1,0:T(8,128)(2,1)S(1)} %copy-done.5), kind=kOutput, calls=%fused_computation.30 | convolution fusion | flops 2415919104 | bytes 9175040 | tf_op jit(solution)/shard_map/dot_general | solution.py:17
  166.0 1.4 copy-done.8
  167.4 4.9 %convolution_convert_fusion.1 = bf16[1152,2048]{1,0:T(8,128)(2,1)} fusion(bf16[1,512,2048]{2,1,0:T(8,128)(2,1)S(1)} %copy-done, f32[1152,512]{1,0:T(8,128)S(1)} %fusion.17, f32[1152,512]{1,0:T(8,128)S(1)} %fusion.13, f32[1152,512]{1,0:T(8,128)S(1)} %fusion.15), kind=kOutput, calls=%fused_computation.3 | convolution fusion | flops 2424176640 | bytes 13893632 | tf_op jit(solution)/shard_map/dot_general | solution.py:22
  172.3 7.2 %all_to_all.30 = bf16[32,36,2048]{2,1,0:T(8,128)(2,1)} reshape(bf16[1152,2048]{1,0:T(8,128)(2,1)} %convolution_convert_fusion.1) | data formatting | bytes 9437184 | tf_op jit(solution)/shard_map/all_to_all | solution.py:95
  179.5 24.4 %all-to-all-done.1 = bf16[4,288,2048]{2,1,0:T(8,128)(2,1)} async-done(((bf16[4,288,2048]{2,1,0:T(8,128)(2,1)}), bf16[4,288,2048]{2,1,0:T(8,128)(2,1)}, u32[]{:S(2)}, u32[]{:S(2)}) %all-to-all-start.1) | async-done | bytes 4718624 | tf_op jit(solution)/shard_map/all_to_all | solution.py:89
  203.9 7.5 %all-to-all-start.2 = ((bf16[32,36,2048]{2,1,0:T(8,128)(2,1)}), bf16[32,36,2048]{2,1,0:T(8,128)(2,1)}, u32[]{:S(2)}, u32[]{:S(2)}) async-start(bf16[32,36,2048]{2,1,0:T(8,128)(2,1)} %all_to_all.30), calls=%async_computation.3 | async-start | bytes 10485760 | tf_op jit(solution)/shard_map/all_to_all | solution.py:95
  211.4 0.2 reduce-scatter.2.cloned.1.call-start
  211.6 14.0 %fusion.29 = f32[2048,512]{1,0:T(8,128)} fusion(bf16[1152,2048]{1,0:T(8,128)(2,1)} %bitcast.5, bf16[1152,2048]{1,0:T(8,128)(2,1)} %bitcast.7, f32[1152,512]{1,0:T(8,128)} %copy-done.6, f32[1152,512]{1,0:T(8,128)} %copy-done.7, f32[1152,512]{1,0:T(8,128)} %copy-done.8, bf16[1,512,2048]{2,1,0:T(8,128)(2,1)S(1)} %copy-done), kind=kOutput, calls=%fused_computation.57 | convolution fusion | flops 4840095744 | bytes 22806528 | tf_op jit(solution)/shard_map/dot_general | solution.py:97
  225.6 0.7 copy-done.3
  226.3 0.1 copy.60
  226.5 0.1 copy.57
  226.6 0.1 copy.59
  226.7 0.1 copy.58
  226.8 4.7 %select_reduce_fusion = (bf16[128,1152]{1,0:T(8,128)(2,1)S(1)}, bf16[128,1152]{1,0:T(8,128)(2,1)S(1)}, bf16[128,1152]{1,0:T(8,128)(2,1)S(1)}) fusion(f32[128,8]{1,0:T(8,128)S(1)} %copy.60, s32[128,8]{1,0:T(8,128)S(1)} %copy.57, f32[128,8]{1,0:T(8,128)S(1)} %copy.59, f32[128,8]{1,0:T(8,128)S(1)} %copy.58), kind=kLoop, calls=%fused_computation.5 | loop fusion | flops 7815168 | bytes 901120 | tf_op jit(solution)/shard_map/reduce_sum | solution.py:105
  231.5 94.9 %all-to-all-done.2 = bf16[32,36,2048]{2,1,0:T(8,128)(2,1)} async-done(((bf16[32,36,2048]{2,1,0:T(8,128)(2,1)}), bf16[32,36,2048]{2,1,0:T(8,128)(2,1)}, u32[]{:S(2)}, u32[]{:S(2)}) %all-to-all-start.2) | async-done | bytes 4718624 | tf_op jit(solution)/shard_map/all_to_all | solution.py:95
  326.4 7.2 %all_to_all.32 = bf16[1152,2048]{1,0:T(8,128)(2,1)} reshape(bf16[32,36,2048]{2,1,0:T(8,128)(2,1)} %all-to-all-done.2) | data formatting | bytes 9437184 | tf_op jit(solution)/shard_map/all_to_all | solution.py:95
  333.6 3.3 fusion.45
  337.0 0.4 copy-done.1
  337.4 0.9 convolution_add_fusion.1
  338.3 1.7 fusion.3
  (38 shorter events, 0.4 us)
Async XLA Ops:
  7.2 160.2 %copy-start = (bf16[1,512,2048]{2,1,0:T(8,128)(2,1)S(1)}, bf16[1,512,2048]{2,1,0:T(8,128)(2,1)}, u32[]{:S(2)}) copy-start(bf16[1,512,2048]{2,1,0:T(8,128)(2,1)} %param.14) | copy-start | bytes 6291460
  7.2 65.5 %all-gather.3.cloned.1.call-start = ((), (), s32[]{:S(2)}) async-start(), calls=%async_computation.4 | async-start | bytes 5308416 | tf_op jit(solution)/shard_map/all_gather | solution.py:72
  11.9 115.9 %all-gather.5.cloned.1.call-start = ((), (), s32[]{:S(2)}) async-start(), calls=%async_computation.5 | async-start | bytes 4718592 | tf_op jit(solution)/shard_map/all_gather | solution.py:73
  85.3 59.7 %all-to-all-start = ((bf16[4,288,2048]{2,1,0:T(8,128)(2,1)}), bf16[4,288,2048]{2,1,0:T(8,128)(2,1)}, u32[]{:S(2)}, u32[]{:S(2)}) async-start(bf16[4,288,2048]{2,1,0:T(8,128)(2,1)} %bitcast.54), calls=%async_computation | async-start | bytes 9437184 | tf_op jit(solution)/shard_map/all_to_all | solution.py:88
  145.0 58.9 %all-to-all-start.1 = ((bf16[4,288,2048]{2,1,0:T(8,128)(2,1)}), bf16[4,288,2048]{2,1,0:T(8,128)(2,1)}, u32[]{:S(2)}, u32[]{:S(2)}) async-start(bf16[4,288,2048]{2,1,0:T(8,128)(2,1)} %bitcast.53), calls=%async_computation.1 | async-start | bytes 9437184 | tf_op jit(solution)/shard_map/all_to_all | solution.py:89
  150.0 5.3 %copy-start.4 = (bf16[1,2048,512]{2,1,0:T(8,128)(2,1)S(1)}, bf16[1,2048,512]{2,1,0:T(8,128)(2,1)}, u32[]{:S(2)}) copy-start(bf16[1,2048,512]{2,1,0:T(8,128)(2,1)} %param.13) | copy-start | bytes 6291460
  155.3 10.7 %copy-start.6 = (f32[1152,512]{1,0:T(8,128)}, f32[1152,512]{1,0:T(8,128)S(1)}, u32[]{:S(2)}) copy-start(f32[1152,512]{1,0:T(8,128)S(1)} %fusion.13) | copy-start | bytes 7077892
  155.3 5.4 %copy-start.5 = (bf16[1,2048,512]{2,1,0:T(8,128)(2,1)S(1)}, bf16[1,2048,512]{2,1,0:T(8,128)(2,1)}, u32[]{:S(2)}) copy-start(bf16[1,2048,512]{2,1,0:T(8,128)(2,1)} %param.12) | copy-start | bytes 6291460
  160.6 5.3 %copy-start.7 = (f32[1152,512]{1,0:T(8,128)}, f32[1152,512]{1,0:T(8,128)S(1)}, u32[]{:S(2)}) copy-start(f32[1152,512]{1,0:T(8,128)S(1)} %fusion.17) | copy-start | bytes 7077892
  166.0 1.4 copy-start.8
  203.9 122.5 %all-to-all-start.2 = ((bf16[32,36,2048]{2,1,0:T(8,128)(2,1)}), bf16[32,36,2048]{2,1,0:T(8,128)(2,1)}, u32[]{:S(2)}, u32[]{:S(2)}) async-start(bf16[32,36,2048]{2,1,0:T(8,128)(2,1)} %all_to_all.30), calls=%async_computation.3 | async-start | bytes 10485760 | tf_op jit(solution)/shard_map/all_to_all | solution.py:95
  211.4 128.6 %reduce-scatter.2.cloned.1.call-start = ((), (), s32[]{:S(2)}) async-start(), calls=%async_computation.6 | async-start | bytes 4718592 | tf_op jit(solution)/shard_map/reduce_scatter | solution.py:100
  225.6 0.7 copy-start.3
  225.6 0.8 copy-start.2
  333.6 3.8 %copy-start.1 = (bf16[1152,2048]{1,0:T(8,128)(2,1)S(1)}, bf16[1152,2048]{1,0:T(8,128)(2,1)}, u32[]{:S(2)}) copy-start(bf16[1152,2048]{1,0:T(8,128)(2,1)} %all_to_all.32) | copy-start | bytes 14155780
Sparse Core Ops, SparseCore 0:
  12.0 60.5 all-gather.2
  74.4 53.4 all-gather.4
  225.8 42.2 reduce-scatter.1

commit v2 on v1

--- a/solution.py
+++ b/solution.py
@@ -42,6 +42,18 @@
     return jnp.dot(picks, source, preferred_element_type=jnp.float32)
 
 
+def shift_along_y(send, n_y):
+    chunks = send.reshape(n_y, -1, send.shape[-1])
+    me = lax.axis_index("ey")
+    got = jnp.zeros_like(chunks)
+    got = lax.dynamic_update_index_in_dim(got, lax.dynamic_index_in_dim(chunks, me, 0, False), me, 0)
+    for shift in range(1, n_y):
+        out = lax.dynamic_index_in_dim(chunks, (me + shift) % n_y, 0, False)
+        moved = lax.ppermute(out, "ey", perm=[(i, (i + shift) % n_y) for i in range(n_y)])
+        got = lax.dynamic_update_index_in_dim(got, moved, (me + n_y - shift) % n_y, 0)
+    return got.reshape(send.shape)
+
+
 def per_device(tokens, cotangent, expert_ids, combine, w_gate, w_up, w_down, tangent_gate):
     n_z = lax.axis_size("ez")
     n_y = lax.axis_size("ey")
@@ -83,16 +95,17 @@
     at_packed = jnp.where(valid, src_tok + z_of * block, -1).reshape(-1)
     at_cot = jnp.where(valid, src_tok + z_of * rows_dev, -1).reshape(-1)
     send_rows = select_rows(at_packed, tok_g).astype(jnp.bfloat16)
-    send_scaled = (src_w.reshape(-1)[:, None] * select_rows(at_cot, cot_g)).astype(jnp.bfloat16)
 
     rows_flat = lax.all_to_all(send_rows, "ey", split_axis=0, concat_axis=0, tiled=True)
-    scaled_flat = lax.all_to_all(send_scaled, "ey", split_axis=0, concat_axis=0, tiled=True)
     gate_e = w_gate[0]
     up_e = w_up[0]
     down_e = w_down[0]
     tangent_e = tangent_gate[0]
     term, factor = forward_part(rows_flat, gate_e, up_e, down_e, tangent_e)
     returned = lax.all_to_all(term, ("ey", "ez"), split_axis=0, concat_axis=0, tiled=True)
+    _, cot_g = lax.optimization_barrier((term, cot_g))
+    send_scaled = (src_w.reshape(-1)[:, None] * select_rows(at_cot, cot_g)).astype(jnp.bfloat16)
+    scaled_flat = shift_along_y(send_scaled, n_y)
     coeff = backward_part(scaled_flat, down_e, factor)
     partial_hvp = lax.dot_general(
         rows_flat, coeff, (((0,), (0,)), ((), ())), preferred_element_type=jnp.float32

time: 350 us -> 339 us (0.969)
  waiting for transfers between devices: 225 us -> 206 us
  local copies, waits for them, and re-layouts: 20.3 us -> 32.4 us
    all_to_all x1, waiting for transfers between devices: 94.9 us -> 14.6 us  [per_device(): lax.all_to_all(term, ('ey', 'ez'), split_axis=0, concat_axis=0, tiled=True)]
    ppermute x0 -> x3, waiting for transfers between devices: none -> 70.6 us  [shift_along_y(): lax.ppermute(out, 'ey', perm=[(i, (i + shift) % n_y) for i in range(n_y)])]
    all_to_all x1, waiting for transfers between devices: 7.92 us -> 54.6 us  [per_device(): lax.all_to_all(send_rows, 'ey', split_axis=0, concat_axis=0, tiled=True)]
    all_gather x1, waiting for transfers between devices: 37.5 us -> 0.01 us  [per_device(): cot_g = lax.all_gather(cotangent, 'ez', axis=0, tiled=True)]
    all_to_all x1 -> x0, waiting for transfers between devices: 24.4 us -> none  [per_device(): lax.all_to_all(send_scaled, 'ey', split_axis=0, concat_axis=0, tiled=True)]
    dynamic_update_slice x0 -> x3, local copies, waits for them, and re-layouts: none -> 7.32 us  [shift_along_y(): lax.dynamic_update_index_in_dim(got, moved, (me + n_y - shift) % n_y, 0)]
    reduce_scatter x1, waiting for transfers between devices: 0.01 us -> 6.13 us  [per_device(): lax.psum_scatter(partial_hvp, 'dp', scatter_dimension=0, tiled=True)]
    all_to_all x1 -> x0, starting transfers between devices: 4.97 us -> none  [per_device(): lax.all_to_all(send_scaled, 'ey', split_axis=0, concat_axis=0, tiled=True)]
  transfers between devices with their start and end apart: 6 -> 8, of which waited for: 5 -> 5; matrix products, arithmetic and copies ran while one was open for 20% -> 20% of each run, Pallas kernels for 0% -> 0%
where the time goes in v2:
time: 339 us; the launch traced here: 338 us
  waiting for transfers between devices  206 us (61%)
  matrix products  59 us (17%)
  local copies, waits for them, and re-layouts  32.4 us (10%)
  starting transfers between devices  17.5 us (5%)
  between operations  14.1 us (4%)
  other arithmetic  8.93 us (3%)
    ppermute x3, waiting for transfers between devices, shift_along_y(): lax.ppermute(out, 'ey', perm=[(i, (i + shift) % n_y) for i in range(n_y)])  70.6 us
    all_gather x1, waiting for transfers between devices, per_device(): tok_g = lax.all_gather(packed, 'ez', axis=0, tiled=True)  59.6 us
    all_to_all x1, waiting for transfers between devices, per_device(): lax.all_to_all(send_rows, 'ey', split_axis=0, concat_axis=0, tiled=True)  54.6 us
    dot_general x2, matrix products, select_rows(): return jnp.dot(picks, source, preferred_element_type=jnp.float32)  18.2 us
    all_to_all x1, waiting for transfers between devices, per_device(): lax.all_to_all(term, ('ey', 'ez'), split_axis=0, concat_axis=0, tiled=True)  14.6 us
    all_to_all x2, local copies, waits for them, and re-layouts, per_device(): lax.all_to_all(term, ('ey', 'ez'), split_axis=0, concat_axis=0, tiled=True)  14.5 us
    dot_general x1, matrix products, per_device(): lax.dot_general(rows_flat, coeff, (((0,), (0,)), ((), ())), preferred_ele...  14.1 us
    all_to_all x1, starting transfers between devices, per_device(): lax.all_to_all(term, ('ey', 'ez'), split_axis=0, concat_axis=0, tiled=True)  9.18 us
  transfers between devices with their start and end apart: 8, of which 5 were waited for; matrix products, arithmetic and copies ran while one was open for 20% of the time, Pallas kernels for 0%

profile of v2, /device:TPU:32, one launch (start us, length us, event | category | flops | bytes accessed | tf_op | source)
XLA Modules:
  0.0 338.2 jit_solution(14234625373344032425)
XLA Ops:
  7.2 0.8 convert_reduce_fusion
  8.2 0.2 reduce_window_sum.11
  8.4 0.8 select_reduce_fusion.6
  9.2 0.4 select_reduce_fusion.4
  9.6 0.1 copy.54
  9.8 0.1 convert_element_type.54
  9.9 1.9 pad_maximum_fusion
  11.9 0.7 all-gather.5.cloned.1.call-update
  12.7 0.1 add.155
  13.0 59.6 %all-gather.3.cloned.1.call-done = bf16[1152,2048]{1,0:T(8,128)(2,1)} async-done(((bf16[144,2048]{1,0:T(8,128)(2,1)}), bf16[1152,2048]{1,0:T(8,128)(2,1)}) %all-gather.3.cloned.1.call-update) | async-done | bytes 4718608 | tf_op jit(solution)/shard_map/all_gather | solution.py:84
  72.6 1.1 slice_bitcast_fusion
  73.7 0.3 copy.62
  74.0 0.6 reshape.144
  74.8 10.4 %convolution_convert_fusion = bf16[1152,2048]{1,0:T(8,128)(2,1)} fusion(bf16[1152,2048]{1,0:T(8,128)(2,1)} %all-gather.3.cloned.1.call-done, s32[1152]{0:T(1024)S(1)} %get-tuple-element.19), kind=kOutput, calls=%fused_computation.1 | convolution fusion | flops 5439504384 | bytes 9441792 | tf_op jit(solution)/shard_map/dot_general | solution.py:42
  85.3 4.9 %all-to-all-start = ((bf16[4,288,2048]{2,1,0:T(8,128)(2,1)}), bf16[4,288,2048]{2,1,0:T(8,128)(2,1)}, u32[]{:S(2)}, u32[]{:S(2)}) async-start(bf16[4,288,2048]{2,1,0:T(8,128)(2,1)} %bitcast.66), calls=%async_computation | async-start | bytes 9437184 | tf_op jit(solution)/shard_map/all_to_all | solution.py:99
  90.4 54.6 %all-to-all-done = bf16[4,288,2048]{2,1,0:T(8,128)(2,1)} async-done(((bf16[4,288,2048]{2,1,0:T(8,128)(2,1)}), bf16[4,288,2048]{2,1,0:T(8,128)(2,1)}, u32[]{:S(2)}, u32[]{:S(2)}) %all-to-all-start) | async-done | bytes 4718624 | tf_op jit(solution)/shard_map/all_to_all | solution.py:99
  145.0 5.2 %fusion.15 = f32[1152,512]{1,0:T(8,128)S(1)} fusion(bf16[1152,2048]{1,0:T(8,128)(2,1)} %bitcast.5, bf16[1,2048,512]{2,1,0:T(8,128)(2,1)} %param.13), kind=kOutput, calls=%fused_computation.30 | convolution fusion | flops 2415919104 | bytes 9175040 | tf_op jit(solution)/shard_map/dot_general | solution.py:18
  150.3 5.3 %fusion.17 = f32[1152,512]{1,0:T(8,128)S(1)} fusion(bf16[1152,2048]{1,0:T(8,128)(2,1)} %bitcast.5, bf16[1,2048,512]{2,1,0:T(8,128)(2,1)S(1)} %copy-done.5), kind=kOutput, calls=%fused_computation.32 | convolution fusion | flops 2415919104 | bytes 9175040 | tf_op jit(solution)/shard_map/dot_general | solution.py:19
  155.6 5.3 %fusion.19 = f32[1152,512]{1,0:T(8,128)S(1)} fusion(bf16[1152,2048]{1,0:T(8,128)(2,1)} %bitcast.5, bf16[1,2048,512]{2,1,0:T(8,128)(2,1)S(1)} %copy-done.6), kind=kOutput, calls=%fused_computation.34 | convolution fusion | flops 2415919104 | bytes 9175040 | tf_op jit(solution)/shard_map/dot_general | solution.py:17
  161.0 1.4 copy-done.9
  162.3 4.9 %convolution_convert_fusion.1 = bf16[1152,2048]{1,0:T(8,128)(2,1)} fusion(bf16[1,512,2048]{2,1,0:T(8,128)(2,1)S(1)} %copy-done, f32[1152,512]{1,0:T(8,128)S(1)} %fusion.15, f32[1152,512]{1,0:T(8,128)S(1)} %fusion.17, f32[1152,512]{1,0:T(8,128)S(1)} %fusion.19), kind=kOutput, calls=%fused_computation.3 | convolution fusion | flops 2424176640 | bytes 13893632 | tf_op jit(solution)/shard_map/dot_general | solution.py:22
  167.2 7.8 %fusion = bf16[1152,2048]{1,0:T(8,128)(2,1)S(1)} fusion(bf16[1024,2048]{1,0:T(8,128)(2,1)} %all-gather.5.cloned.1.call-done, f32[1152]{0:T(1024)S(1)} %add.159, s32[1152]{0:T(1024)S(1)} %get-tuple-element.18), kind=kOutput, calls=%fused_computation.2 | convolution fusion | flops 4837736448 | bytes 8922112 | tf_op jit(solution)/shard_map/dot_general | solution.py:42
  175.0 0.6 broadcast_in_dim.103
  175.6 2.0 dynamic-slice_bitcast_fusion
  177.6 2.1 copy-done.2
  179.7 0.6 collective-permute-start
  180.2 2.0 collective-permute-start.1
  182.2 0.7 collective-permute-start.2
  182.9 7.2 %all_to_all.19 = bf16[32,36,2048]{2,1,0:T(8,128)(2,1)} reshape(bf16[1152,2048]{1,0:T(8,128)(2,1)} %convolution_convert_fusion.1) | data formatting | bytes 9437184 | tf_op jit(solution)/shard_map/all_to_all | solution.py:105
  190.1 9.2 %all-to-all-start.1 = ((bf16[32,36,2048]{2,1,0:T(8,128)(2,1)}), bf16[32,36,2048]{2,1,0:T(8,128)(2,1)}, u32[]{:S(2)}, u32[]{:S(2)}) async-start(bf16[32,36,2048]{2,1,0:T(8,128)(2,1)} %all_to_all.19), calls=%async_computation.2 | async-start | bytes 10485760 | tf_op jit(solution)/shard_map/all_to_all | solution.py:105
  199.3 70.6 %collective-permute-done = bf16[288,2048]{1,0:T(8,128)(2,1)} collective-permute-done((bf16[288,2048]{1,0:T(8,128)(2,1)}, bf16[288,2048]{1,0:T(8,128)(2,1)}, u32[]{:S(2)}, u32[]{:S(2)}) %collective-permute-start) | collective-permute-done | bytes 1179680 | tf_op jit(solution)/shard_map/ppermute | solution.py:52
  269.9 2.4 bitcast_dynamic-update-slice_fusion.2
  272.3 2.4 bitcast_dynamic-update-slice_fusion.1
  274.8 2.5 bitcast_dynamic-update-slice_fusion
  277.2 14.1 %fusion.29 = f32[2048,512]{1,0:T(8,128)} fusion(bf16[1152,2048]{1,0:T(8,128)(2,1)} %bitcast.5, bf16[1152,2048]{1,0:T(8,128)(2,1)} %bitcast.67, f32[1152,512]{1,0:T(8,128)} %copy-done.8, f32[1152,512]{1,0:T(8,128)} %copy-done.7, f32[1152,512]{1,0:T(8,128)} %copy-done.9, bf16[1,512,2048]{2,1,0:T(8,128)(2,1)S(1)} %copy-done), kind=kOutput, calls=%fused_computation.64 | convolution fusion | flops 4840095744 | bytes 22806528 | tf_op jit(solution)/shard_map/dot_general | solution.py:110
  291.3 0.7 copy-done.3
  292.1 0.1 copy.57
  292.2 0.1 copy.58
  292.3 0.1 copy.59
  292.4 0.1 copy.60
  292.5 4.7 %select_reduce_fusion = (bf16[128,1152]{1,0:T(8,128)(2,1)S(1)}, bf16[128,1152]{1,0:T(8,128)(2,1)S(1)}, bf16[128,1152]{1,0:T(8,128)(2,1)S(1)}) fusion(f32[128,8]{1,0:T(8,128)S(1)} %copy.60, s32[128,8]{1,0:T(8,128)S(1)} %copy.57, f32[128,8]{1,0:T(8,128)S(1)} %copy.59, f32[128,8]{1,0:T(8,128)S(1)} %copy.58), kind=kLoop, calls=%fused_computation.5 | loop fusion | flops 7815168 | bytes 901120 | tf_op jit(solution)/shard_map/reduce_sum | solution.py:118
  297.2 14.6 %all-to-all-done.1 = bf16[32,36,2048]{2,1,0:T(8,128)(2,1)} async-done(((bf16[32,36,2048]{2,1,0:T(8,128)(2,1)}), bf16[32,36,2048]{2,1,0:T(8,128)(2,1)}, u32[]{:S(2)}, u32[]{:S(2)}) %all-to-all-start.1) | async-done | bytes 4718624 | tf_op jit(solution)/shard_map/all_to_all | solution.py:105
  311.8 7.3 %all_to_all.21 = bf16[1152,2048]{1,0:T(8,128)(2,1)} reshape(bf16[32,36,2048]{2,1,0:T(8,128)(2,1)} %all-to-all-done.1) | data formatting | bytes 9437184 | tf_op jit(solution)/shard_map/all_to_all | solution.py:105
  319.1 3.4 fusion.45
  322.5 0.5 copy-done.1
  322.9 0.9 convolution_add_fusion.1
  323.9 1.7 fusion.3
  325.6 6.1 %reduce-scatter.2.cloned.1.call-done = f32[256,512]{1,0:T(8,128)} async-done(((f32[2048,512]{1,0:T(8,128)}), f32[256,512]{1,0:T(8,128)}) %reduce-scatter.2.cloned.1.call-update) | async-done | bytes 524304 | tf_op jit(solution)/shard_map/reduce_scatter | solution.py:113
  (49 shorter events, 1.0 us)
Async XLA Ops:
  7.2 155.2 %copy-start = (bf16[1,512,2048]{2,1,0:T(8,128)(2,1)S(1)}, bf16[1,512,2048]{2,1,0:T(8,128)(2,1)}, u32[]{:S(2)}) copy-start(bf16[1,512,2048]{2,1,0:T(8,128)(2,1)} %param.14) | copy-start | bytes 6291460
  7.2 65.4 %all-gather.3.cloned.1.call-start = ((), (), s32[]{:S(2)}) async-start(), calls=%async_computation.3 | async-start | bytes 5308416 | tf_op jit(solution)/shard_map/all_gather | solution.py:84
  11.9 155.4 %all-gather.5.cloned.1.call-start = ((), (), s32[]{:S(2)}) async-start(), calls=%async_computation.4 | async-start | bytes 4718592 | tf_op jit(solution)/shard_map/all_gather | solution.py:85
  85.3 59.7 %all-to-all-start = ((bf16[4,288,2048]{2,1,0:T(8,128)(2,1)}), bf16[4,288,2048]{2,1,0:T(8,128)(2,1)}, u32[]{:S(2)}, u32[]{:S(2)}) async-start(bf16[4,288,2048]{2,1,0:T(8,128)(2,1)} %bitcast.66), calls=%async_computation | async-start | bytes 9437184 | tf_op jit(solution)/shard_map/all_to_all | solution.py:99
  145.0 5.2 %copy-start.5 = (bf16[1,2048,512]{2,1,0:T(8,128)(2,1)S(1)}, bf16[1,2048,512]{2,1,0:T(8,128)(2,1)}, u32[]{:S(2)}) copy-start(bf16[1,2048,512]{2,1,0:T(8,128)(2,1)} %param.15) | copy-start | bytes 6291460
  150.2 10.7 %copy-start.7 = (f32[1152,512]{1,0:T(8,128)}, f32[1152,512]{1,0:T(8,128)S(1)}, u32[]{:S(2)}) copy-start(f32[1152,512]{1,0:T(8,128)S(1)} %fusion.15) | copy-start | bytes 7077892
  150.2 5.4 %copy-start.6 = (bf16[1,2048,512]{2,1,0:T(8,128)(2,1)S(1)}, bf16[1,2048,512]{2,1,0:T(8,128)(2,1)}, u32[]{:S(2)}) copy-start(bf16[1,2048,512]{2,1,0:T(8,128)(2,1)} %param.12) | copy-start | bytes 6291460
  155.6 5.3 %copy-start.8 = (f32[1152,512]{1,0:T(8,128)}, f32[1152,512]{1,0:T(8,128)S(1)}, u32[]{:S(2)}) copy-start(f32[1152,512]{1,0:T(8,128)S(1)} %fusion.17) | copy-start | bytes 7077892
  160.9 1.4 copy-start.9
  177.6 2.1 copy-start.2
  179.7 90.2 %collective-permute-start = (bf16[288,2048]{1,0:T(8,128)(2,1)}, bf16[288,2048]{1,0:T(8,128)(2,1)}, u32[]{:S(2)}, u32[]{:S(2)}) collective-permute-start(bf16[288,2048]{1,0:T(8,128)(2,1)} %get-tuple-element.11), channel_id=1, source_target_pairs={{0,1},{1,2},{2,3},{3,0},{4,5},{5,6},{6,7},{7,4},{8,9},{9,10},{10,1... | collective-permute-start | bytes 3538952 | tf_op jit(solution)/shard_map/ppermute | solution.py:52
  180.2 92.1 %collective-permute-start.1 = (bf16[288,2048]{1,0:T(8,128)(2,1)}, bf16[288,2048]{1,0:T(8,128)(2,1)}, u32[]{:S(2)}, u32[]{:S(2)}) collective-permute-start(bf16[288,2048]{1,0:T(8,128)(2,1)} %get-tuple-element.10), channel_id=1, source_target_pairs={{0,2},{1,3},{2,0},{3,1},{4,6},{5,7},{6,4},{7,5},{8,10},{9,11},{10,... | collective-permute-start | bytes 3538952 | tf_op jit(solution)/shard_map/ppermute | solution.py:52
  182.2 92.6 %collective-permute-start.2 = (bf16[288,2048]{1,0:T(8,128)(2,1)S(1)}, bf16[288,2048]{1,0:T(8,128)(2,1)}, u32[]{:S(2)}, u32[]{:S(2)}) collective-permute-start(bf16[288,2048]{1,0:T(8,128)(2,1)S(1)} %get-tuple-element.9), channel_id=1, source_target_pairs={{0,3},{1,0},{2,1},{3,2},{4,7},{5,4},{6,5},{7,6},{8,11},{9,8},{10,9... | collective-permute-start | bytes 3538952 | tf_op jit(solution)/shard_map/ppermute | solution.py:52
  190.1 121.7 %all-to-all-start.1 = ((bf16[32,36,2048]{2,1,0:T(8,128)(2,1)}), bf16[32,36,2048]{2,1,0:T(8,128)(2,1)}, u32[]{:S(2)}, u32[]{:S(2)}) async-start(bf16[32,36,2048]{2,1,0:T(8,128)(2,1)} %all_to_all.19), calls=%async_computation.2 | async-start | bytes 10485760 | tf_op jit(solution)/shard_map/all_to_all | solution.py:105
  199.3 132.4 %reduce-scatter.2.cloned.1.call-start = ((), (), s32[]{:S(2)}) async-start(), calls=%async_computation.5 | async-start | bytes 4718592 | tf_op jit(solution)/shard_map/reduce_scatter | solution.py:113
  291.3 0.7 copy-start.3
  291.3 0.8 copy-start.4
  319.1 3.8 %copy-start.1 = (bf16[1152,2048]{1,0:T(8,128)(2,1)S(1)}, bf16[1152,2048]{1,0:T(8,128)(2,1)}, u32[]{:S(2)}) copy-start(bf16[1152,2048]{1,0:T(8,128)(2,1)} %all_to_all.21) | copy-start | bytes 14155780
Sparse Core Ops, SparseCore 0:
  12.0 60.5 all-gather.2
  74.4 53.4 all-gather.4
  291.5 40.1 reduce-scatter.1

commit v3 on v2

--- a/solution.py
+++ b/solution.py
@@ -13,13 +13,18 @@
     return (first, second)
 
 
-def forward_part(rows_flat, gate_e, up_e, down_e, tangent_e):
+def forward_part(rows_flat, gate_e, up_e, down_e, tangent_e, blocks):
     gate_act = jnp.dot(rows_flat, gate_e, preferred_element_type=jnp.float32)
     up_act = jnp.dot(rows_flat, up_e, preferred_element_type=jnp.float32)
     gate_dot = jnp.dot(rows_flat, tangent_e, preferred_element_type=jnp.float32)
     first, second = silu_derivs(gate_act)
     lifted = (first * gate_dot * up_act).astype(jnp.bfloat16)
-    term = jnp.dot(lifted, down_e, preferred_element_type=jnp.float32).astype(jnp.bfloat16)
+    term = lax.dot_general(
+        lifted.reshape(blocks + (lifted.shape[-1],)),
+        down_e,
+        (((2,), (0,)), ((), ())),
+        preferred_element_type=jnp.float32,
+    ).astype(jnp.bfloat16)
     return (term, up_act * second * gate_dot)
 
 
@@ -101,10 +106,10 @@
     up_e = w_up[0]
     down_e = w_down[0]
     tangent_e = tangent_gate[0]
-    term, factor = forward_part(rows_flat, gate_e, up_e, down_e, tangent_e)
+    send_scaled = (src_w.reshape(-1)[:, None] * select_rows(at_cot, cot_g)).astype(jnp.bfloat16)
+    term, factor = forward_part(rows_flat, gate_e, up_e, down_e, tangent_e, (expert_count, capacity))
     returned = lax.all_to_all(term, ("ey", "ez"), split_axis=0, concat_axis=0, tiled=True)
-    _, cot_g = lax.optimization_barrier((term, cot_g))
-    send_scaled = (src_w.reshape(-1)[:, None] * select_rows(at_cot, cot_g)).astype(jnp.bfloat16)
+    _, send_scaled = lax.optimization_barrier((term, send_scaled))
     scaled_flat = shift_along_y(send_scaled, n_y)
     coeff = backward_part(scaled_flat, down_e, factor)
     partial_hvp = lax.dot_general(
@@ -116,7 +121,12 @@
     output_tangent = jnp.zeros((rows_dev, model_width), jnp.float32)
     for piece in split3(combine):
         spread = jnp.sum(jnp.where(at_slot, piece[:, :, None], 0.0), axis=1).astype(jnp.bfloat16)
-        output_tangent = output_tangent + jnp.dot(spread, returned, preferred_element_type=jnp.float32)
+        output_tangent = output_tangent + lax.dot_general(
+            spread.reshape(rows_dev, expert_count, capacity),
+            returned,
+            (((1, 2), (0, 1)), ((), ())),
+            preferred_element_type=jnp.float32,
+        )
     return (hvp_gate[None], output_tangent.astype(jnp.bfloat16))
 
 

time: 339 us -> 342 us (level)
  local copies, waits for them, and re-layouts: 32.4 us -> 18.4 us
  matrix products: 59 us -> 69.6 us
  waiting for transfers between devices: 206 us -> 212 us
    all_to_all x1, waiting for transfers between devices: 54.6 us -> 7.96 us  [per_device(): lax.all_to_all(send_rows, 'ey', split_axis=0, concat_axis=0, tiled=True)]
    all_gather x1, waiting for transfers between devices: 0.01 us -> 37.3 us  [per_device(): cot_g = lax.all_gather(cotangent, 'ez', axis=0, tiled=True)]
    reduce_scatter x1, waiting for transfers between devices: 6.13 us -> 21.2 us  [per_device(): lax.psum_scatter(partial_hvp, 'dp', scatter_dimension=0, tiled=True)]
    all_to_all x2 -> x0, local copies, waits for them, and re-layouts: 14.5 us -> none  [per_device(): lax.all_to_all(term, ('ey', 'ez'), split_axis=0, concat_axis=0, tiled=True)]
    ppermute x3, waiting for transfers between devices: 70.6 us -> 82.3 us  [shift_along_y(): lax.ppermute(out, 'ey', perm=[(i, (i + shift) % n_y) for i in range(n_y)])]
    all_to_all x1, waiting for transfers between devices: 14.6 us -> 3.14 us  [per_device(): lax.all_to_all(term, ('ey', 'ez'), split_axis=0, concat_axis=0, tiled=True)]
    dot_general x4, matrix products: 10.9 us -> 17.1 us  [the longest x3 11 us: per_device(): lax.dot_general(spread.reshape(rows_dev, expert_count, capacity), returne...]
  transfers between devices with their start and end apart: 8 -> 8, of which waited for: 5 -> 6; matrix products, arithmetic and copies ran while one was open for 20% -> 17% of each run, Pallas kernels for 0% -> 0%
where the time goes in v3:
time: 342 us; the launch traced here: 341 us
  waiting for transfers between devices  212 us (62%)
  matrix products  69.6 us (20%)
  local copies, waits for them, and re-layouts  18.4 us (5%)
  starting transfers between devices  17.9 us (5%)
  between operations  14.1 us (4%)
  other arithmetic  9 us (3%)
    ppermute x3, waiting for transfers between devices, shift_along_y(): lax.ppermute(out, 'ey', perm=[(i, (i + shift) % n_y) for i in range(n_y)])  82.3 us
    all_gather x1, waiting for transfers between devices, per_device(): tok_g = lax.all_gather(packed, 'ez', axis=0, tiled=True)  59.6 us
    all_gather x1, waiting for transfers between devices, per_device(): cot_g = lax.all_gather(cotangent, 'ez', axis=0, tiled=True)  37.3 us
    reduce_scatter x1, waiting for transfers between devices, per_device(): lax.psum_scatter(partial_hvp, 'dp', scatter_dimension=0, tiled=True)  21.2 us
    dot_general x2, matrix products, select_rows(): return jnp.dot(picks, source, preferred_element_type=jnp.float32)  19.6 us
    dot_general x1, matrix products, per_device(): lax.dot_general(rows_flat, coeff, (((0,), (0,)), ((), ())), preferred_ele...  14 us
    dot_general x3, matrix products, per_device(): lax.dot_general(spread.reshape(rows_dev, expert_count, capacity), returne...  11 us
    all_to_all x1, starting transfers between devices, per_device(): lax.all_to_all(term, ('ey', 'ez'), split_axis=0, concat_axis=0, tiled=True)  9.18 us
  transfers between devices with their start and end apart: 8, of which 6 were waited for; matrix products, arithmetic and copies ran while one was open for 17% of the time, Pallas kernels for 0%

profile of v3, /device:TPU:32, one launch (start us, length us, event | category | flops | bytes accessed | tf_op | source)
XLA Modules:
  0.0 341.3 jit_solution(8645760763138743053)
XLA Ops:
  7.2 0.8 convert_reduce_fusion
  8.2 0.7 select_reduce_fusion.6
  8.9 0.2 reduce_window_sum.11
  9.2 0.4 select_reduce_fusion.4
  9.6 0.1 copy.60
  9.8 0.1 convert_element_type.66
  9.9 2.0 pad_maximum_fusion
  12.0 0.7 all-gather.5.cloned.1.call-update
  13.1 59.6 %all-gather.3.cloned.1.call-done = bf16[1152,2048]{1,0:T(8,128)(2,1)} async-done(((bf16[144,2048]{1,0:T(8,128)(2,1)}), bf16[1152,2048]{1,0:T(8,128)(2,1)}) %all-gather.3.cloned.1.call-update) | async-done | bytes 4718608 | tf_op jit(solution)/shard_map/all_gather | solution.py:89
  72.6 1.1 slice_bitcast_fusion
  73.7 0.3 copy.71
  74.0 0.6 reshape.154
  74.9 10.4 %convolution_convert_fusion = bf16[1152,2048]{1,0:T(8,128)(2,1)} fusion(bf16[1152,2048]{1,0:T(8,128)(2,1)} %all-gather.3.cloned.1.call-done, s32[1152]{0:T(1024)S(1)} %get-tuple-element.19), kind=kOutput, calls=%fused_computation.1 | convolution fusion | flops 5439504384 | bytes 9441792 | tf_op jit(solution)/shard_map/dot_general | solution.py:47
  85.3 5.1 %all-to-all-start = ((bf16[4,288,2048]{2,1,0:T(8,128)(2,1)}), bf16[4,288,2048]{2,1,0:T(8,128)(2,1)}, u32[]{:S(2)}, u32[]{:S(2)}) async-start(bf16[4,288,2048]{2,1,0:T(8,128)(2,1)} %bitcast.90), calls=%async_computation | async-start | bytes 9437184 | tf_op jit(solution)/shard_map/all_to_all | solution.py:104
  90.6 37.3 %all-gather.5.cloned.1.call-done = bf16[1024,2048]{1,0:T(8,128)(2,1)} async-done(((bf16[128,2048]{1,0:T(8,128)(2,1)}), bf16[1024,2048]{1,0:T(8,128)(2,1)}) %all-gather.5.cloned.1.call-update) | async-done | bytes 4194320 | tf_op jit(solution)/shard_map/all_gather | solution.py:90
  127.9 9.2 %fusion = bf16[1152,2048]{1,0:T(8,128)(2,1)} fusion(bf16[1024,2048]{1,0:T(8,128)(2,1)} %all-gather.5.cloned.1.call-done, f32[1152]{0:T(1024)S(1)} %add.161, s32[1152]{0:T(1024)S(1)} %get-tuple-element.18), kind=kOutput, calls=%fused_computation.2 | convolution fusion | flops 4837736448 | bytes 8922112 | tf_op jit(solution)/shard_map/dot_general | solution.py:47
  137.1 8.0 %all-to-all-done = bf16[4,288,2048]{2,1,0:T(8,128)(2,1)} async-done(((bf16[4,288,2048]{2,1,0:T(8,128)(2,1)}), bf16[4,288,2048]{2,1,0:T(8,128)(2,1)}, u32[]{:S(2)}, u32[]{:S(2)}) %all-to-all-start) | async-done | bytes 4718624 | tf_op jit(solution)/shard_map/all_to_all | solution.py:104
  145.0 5.2 %fusion.19 = f32[1152,512]{1,0:T(8,128)S(1)} fusion(bf16[1152,2048]{1,0:T(8,128)(2,1)} %bitcast.5, bf16[1,2048,512]{2,1,0:T(8,128)(2,1)} %param.15), kind=kOutput, calls=%fused_computation.35 | convolution fusion | flops 2415919104 | bytes 9175040 | tf_op jit(solution)/shard_map/dot_general | solution.py:19
  150.3 5.3 %fusion.21 = f32[1152,512]{1,0:T(8,128)S(1)} fusion(bf16[1152,2048]{1,0:T(8,128)(2,1)} %bitcast.5, bf16[1,2048,512]{2,1,0:T(8,128)(2,1)S(1)} %copy-done.4), kind=kOutput, calls=%fused_computation.37 | convolution fusion | flops 2415919104 | bytes 9175040 | tf_op jit(solution)/shard_map/dot_general | solution.py:17
  155.7 8.2 %fusion.10 = (bf16[1152,512]{1,0:T(8,128)(2,1)}, f32[1152,512]{1,0:T(8,128)}) fusion(f32[1152,512]{1,0:T(8,128)S(1)} %fusion.19, f32[1152,512]{1,0:T(8,128)S(1)} %fusion.21, bf16[1152,2048]{1,0:T(8,128)(2,1)} %bitcast.5, bf16[1,2048,512]{2,1,0:T(8,128)(2,1)S(1)} %copy-done.5), kind=kOutput, calls=%fused_computation.25 | convolution fusion | flops 2421817344 | bytes 15073280 | tf_op jit(solution)/shard_map/dot_general | solution.py:18
  163.9 3.0 reshape.155
  166.9 6.1 %convolution_convert_fusion.1 = bf16[32,36,2048]{2,1,0:T(8,128)(2,1)} fusion(bf16[32,36,512]{2,1,0:T(8,128)(2,1)} %reshape.155, bf16[1,512,2048]{2,1,0:T(8,128)(2,1)S(1)} %copy-done), kind=kOutput, calls=%fused_computation.9 | convolution fusion | flops 2418278400 | bytes 7995392 | tf_op jit(solution)/shard_map/dot_general | solution.py:22
  173.0 0.6 broadcast_in_dim.103
  173.6 1.8 dynamic-slice_bitcast_fusion
  175.5 2.1 copy-done.1
  177.6 0.6 collective-permute-start
  178.2 2.0 collective-permute-start.1
  180.2 0.6 collective-permute-start.2
  180.8 9.2 %all-to-all-start.1 = ((bf16[32,36,2048]{2,1,0:T(8,128)(2,1)}), bf16[32,36,2048]{2,1,0:T(8,128)(2,1)}, u32[]{:S(2)}, u32[]{:S(2)}) async-start(bf16[32,36,2048]{2,1,0:T(8,128)(2,1)} %convolution_convert_fusion.1), calls=%async_computation.2 | async-start | bytes 10485760 | tf_op jit(solution)/shard_map/all_to_all | solution.py:111
  190.0 0.3 reduce-scatter.2.cloned.1.call-start
  190.3 82.3 %collective-permute-done = bf16[288,2048]{1,0:T(8,128)(2,1)} collective-permute-done((bf16[288,2048]{1,0:T(8,128)(2,1)}, bf16[288,2048]{1,0:T(8,128)(2,1)}, u32[]{:S(2)}, u32[]{:S(2)}) %collective-permute-start) | collective-permute-done | bytes 1179680 | tf_op jit(solution)/shard_map/ppermute | solution.py:57
  272.6 2.4 bitcast_dynamic-update-slice_fusion.2
  275.0 2.4 bitcast_dynamic-update-slice_fusion.1
  277.5 1.1 bitcast_dynamic-update-slice_fusion
  278.6 14.0 %fusion.25 = f32[2048,512]{1,0:T(8,128)} fusion(bf16[1152,2048]{1,0:T(8,128)(2,1)} %bitcast.5, bf16[1152,2048]{1,0:T(8,128)(2,1)} %bitcast.91, f32[1152,512]{1,0:T(8,128)} %copy-done.6, f32[1152,512]{1,0:T(8,128)} %get-tuple-element.24, f32[1152,512]{1,0:T(8,128)} %copy-done.7, bf16[1,512,2048]{2,1,0:T(8,128)(2,1)S(1)} %copy-done), kind=kOutput, calls=%fused_computation.62 | convolution fusion | flops 4840095744 | bytes 22806528 | tf_op jit(solution)/shard_map/dot_general | solution.py:115
  292.6 0.7 copy-done.3
  293.3 0.1 copy.66
  293.5 0.1 copy.63
  293.6 0.1 copy.68
  293.8 4.7 %select_reduce_fusion.2 = (bf16[128,1152]{1,0:T(8,128)(2,1)S(1)}, bf16[128,1152]{1,0:T(8,128)(2,1)S(1)}, bf16[128,1152]{1,0:T(8,128)(2,1)S(1)}) fusion(f32[128,8]{1,0:T(8,128)S(1)} %copy.64, s32[128,8]{1,0:T(8,128)S(1)} %copy.63, f32[128,8]{1,0:T(8,128)S(1)} %copy.68, f32[128,8]{1,0:T(8,128)S(1)} %copy.66), kind=kLoop, calls=%fused_computation.6 | loop fusion | flops 7815168 | bytes 901120 | tf_op jit(solution)/shard_map/reduce_sum | solution.py:123
  298.5 0.2 copy.65
  298.8 0.2 copy.69
  299.1 0.2 copy.67
  299.3 3.1 all-to-all-done.1
  302.5 3.4 convolution_bitcast_fusion
  305.9 3.4 convolution_bitcast_fusion.1
  309.3 4.3 %fusion.5 = bf16[128,2048]{1,0:T(8,128)(2,1)} fusion(f32[128,2048]{1,0:T(8,128)S(1)} %convolution_bitcast_fusion, f32[128,2048]{1,0:T(8,128)S(1)} %convolution_bitcast_fusion.1, bf16[128,32,36]{0,2,1:T(8,128)(2,1)S(1)} %convert_element_type.75, bf16[32,36,2048]{2,1,0:T(8,128)(2,1)} %all-to-all-done.1), kind=kOutput, calls=%fused_computation.20 | convolution fusion | flops 604766208 | bytes 7634944 | tf_op jit(solution)/shard_map/dot_general | solution.py:124
  313.5 21.2 %reduce-scatter.2.cloned.1.call-done = f32[256,512]{1,0:T(8,128)} async-done(((f32[2048,512]{1,0:T(8,128)}), f32[256,512]{1,0:T(8,128)}) %reduce-scatter.2.cloned.1.call-update) | async-done | bytes 524304 | tf_op jit(solution)/shard_map/reduce_scatter | solution.py:118
  (55 shorter events, 1.3 us)
Async XLA Ops:
  7.2 159.7 %copy-start = (bf16[1,512,2048]{2,1,0:T(8,128)(2,1)S(1)}, bf16[1,512,2048]{2,1,0:T(8,128)(2,1)}, u32[]{:S(2)}) copy-start(bf16[1,512,2048]{2,1,0:T(8,128)(2,1)} %param.14) | copy-start | bytes 6291460
  7.2 65.5 %all-gather.3.cloned.1.call-start = ((), (), s32[]{:S(2)}) async-start(), calls=%async_computation.3 | async-start | bytes 5308416 | tf_op jit(solution)/shard_map/all_gather | solution.py:89
  11.9 115.9 %all-gather.5.cloned.1.call-start = ((), (), s32[]{:S(2)}) async-start(), calls=%async_computation.4 | async-start | bytes 4718592 | tf_op jit(solution)/shard_map/all_gather | solution.py:90
  85.3 59.7 %all-to-all-start = ((bf16[4,288,2048]{2,1,0:T(8,128)(2,1)}), bf16[4,288,2048]{2,1,0:T(8,128)(2,1)}, u32[]{:S(2)}, u32[]{:S(2)}) async-start(bf16[4,288,2048]{2,1,0:T(8,128)(2,1)} %bitcast.90), calls=%async_computation | async-start | bytes 9437184 | tf_op jit(solution)/shard_map/all_to_all | solution.py:104
  145.0 5.2 %copy-start.4 = (bf16[1,2048,512]{2,1,0:T(8,128)(2,1)S(1)}, bf16[1,2048,512]{2,1,0:T(8,128)(2,1)}, u32[]{:S(2)}) copy-start(bf16[1,2048,512]{2,1,0:T(8,128)(2,1)} %param.12) | copy-start | bytes 6291460
  150.3 5.4 %copy-start.6 = (f32[1152,512]{1,0:T(8,128)}, f32[1152,512]{1,0:T(8,128)S(1)}, u32[]{:S(2)}) copy-start(f32[1152,512]{1,0:T(8,128)S(1)} %fusion.19) | copy-start | bytes 7077892
  150.3 5.4 %copy-start.5 = (bf16[1,2048,512]{2,1,0:T(8,128)(2,1)S(1)}, bf16[1,2048,512]{2,1,0:T(8,128)(2,1)}, u32[]{:S(2)}) copy-start(bf16[1,2048,512]{2,1,0:T(8,128)(2,1)} %param.13) | copy-start | bytes 6291460
  155.7 8.2 %copy-start.7 = (f32[1152,512]{1,0:T(8,128)}, f32[1152,512]{1,0:T(8,128)S(1)}, u32[]{:S(2)}) copy-start(f32[1152,512]{1,0:T(8,128)S(1)} %fusion.21) | copy-start | bytes 7077892
  163.9 9.7 %slice-start = ((s8[4718592]{0:T(1024)(128)(4,1)}), s8[524288]{0:T(1024)(128)(4,1)S(1)}, s32[]{:S(2)}) async-start(s8[4718592]{0:T(1024)(128)(4,1)} %bitcast.87), calls=%async_computation.6 | async-start | bytes 1048576
  166.9 6.7 %slice-start.1 = ((s8[4718592]{0:T(1024)(128)(4,1)}), s8[4194304]{0:T(1024)(128)(4,1)S(1)}, s32[]{:S(2)}) async-start(s8[4718592]{0:T(1024)(128)(4,1)} %bitcast.87), calls=%async_computation.7 | async-start | bytes 8388608
  175.5 2.1 copy-start.1
  177.6 95.0 %collective-permute-start = (bf16[288,2048]{1,0:T(8,128)(2,1)}, bf16[288,2048]{1,0:T(8,128)(2,1)}, u32[]{:S(2)}, u32[]{:S(2)}) collective-permute-start(bf16[288,2048]{1,0:T(8,128)(2,1)} %get-tuple-element.11), channel_id=1, source_target_pairs={{0,1},{1,2},{2,3},{3,0},{4,5},{5,6},{6,7},{7,4},{8,9},{9,10},{10,1... | collective-permute-start | bytes 3538952 | tf_op jit(solution)/shard_map/ppermute | solution.py:57
  178.2 96.9 %collective-permute-start.1 = (bf16[288,2048]{1,0:T(8,128)(2,1)}, bf16[288,2048]{1,0:T(8,128)(2,1)}, u32[]{:S(2)}, u32[]{:S(2)}) collective-permute-start(bf16[288,2048]{1,0:T(8,128)(2,1)} %get-tuple-element.10), channel_id=1, source_target_pairs={{0,2},{1,3},{2,0},{3,1},{4,6},{5,7},{6,4},{7,5},{8,10},{9,11},{10,... | collective-permute-start | bytes 3538952 | tf_op jit(solution)/shard_map/ppermute | solution.py:57
  180.2 97.3 %collective-permute-start.2 = (bf16[288,2048]{1,0:T(8,128)(2,1)}, bf16[288,2048]{1,0:T(8,128)(2,1)S(1)}, u32[]{:S(2)}, u32[]{:S(2)}) collective-permute-start(bf16[288,2048]{1,0:T(8,128)(2,1)} %get-tuple-element.9), channel_id=1, source_target_pairs={{0,3},{1,0},{2,1},{3,2},{4,7},{5,4},{6,5},{7,6},{8,11},{9,8},{10,9... | collective-permute-start | bytes 3538952 | tf_op jit(solution)/shard_map/ppermute | solution.py:57
  180.8 121.6 %all-to-all-start.1 = ((bf16[32,36,2048]{2,1,0:T(8,128)(2,1)}), bf16[32,36,2048]{2,1,0:T(8,128)(2,1)}, u32[]{:S(2)}, u32[]{:S(2)}) async-start(bf16[32,36,2048]{2,1,0:T(8,128)(2,1)} %convolution_convert_fusion.1), calls=%async_computation.2 | async-start | bytes 10485760 | tf_op jit(solution)/shard_map/all_to_all | solution.py:111
  190.0 144.7 %reduce-scatter.2.cloned.1.call-start = ((), (), s32[]{:S(2)}) async-start(), calls=%async_computation.5 | async-start | bytes 4718592 | tf_op jit(solution)/shard_map/reduce_scatter | solution.py:118
  292.6 0.7 copy-start.3
  292.6 0.8 copy-start.2
Sparse Core Ops, SparseCore 0:
  12.0 60.5 all-gather.2
  74.4 53.4 all-gather.4
  292.8 41.9 reduce-scatter.1

commit v4 on v3

--- a/solution.py
+++ b/solution.py
@@ -109,7 +109,7 @@
     send_scaled = (src_w.reshape(-1)[:, None] * select_rows(at_cot, cot_g)).astype(jnp.bfloat16)
     term, factor = forward_part(rows_flat, gate_e, up_e, down_e, tangent_e, (expert_count, capacity))
     returned = lax.all_to_all(term, ("ey", "ez"), split_axis=0, concat_axis=0, tiled=True)
-    _, send_scaled = lax.optimization_barrier((term, send_scaled))
+    _, send_scaled = lax.optimization_barrier((rows_flat, send_scaled))
     scaled_flat = shift_along_y(send_scaled, n_y)
     coeff = backward_part(scaled_flat, down_e, factor)
     partial_hvp = lax.dot_general(

time: 342 us -> 321 us (0.939)
  waiting for transfers between devices: 212 us -> 192 us
    all_to_all x1, waiting for transfers between devices: 3.14 us -> 58.4 us  [per_device(): lax.all_to_all(term, ('ey', 'ez'), split_axis=0, concat_axis=0, tiled=True)]
    ppermute x3, waiting for transfers between devices: 82.3 us -> 27.8 us  [shift_along_y(): lax.ppermute(out, 'ey', perm=[(i, (i + shift) % n_y) for i in range(n_y)])]
    reduce_scatter x1, waiting for transfers between devices: 21.2 us -> 0.01 us  [per_device(): lax.psum_scatter(partial_hvp, 'dp', scatter_dimension=0, tiled=True)]
  transfers between devices with their start and end apart: 8 -> 8, of which waited for: 6 -> 7; matrix products, arithmetic and copies ran while one was open for 17% -> 27% of each run, Pallas kernels for 0% -> 0%
where the time goes in v4:
time: 321 us; the launch traced here: 320 us
  waiting for transfers between devices  192 us (60%)
  matrix products  67.4 us (21%)
  local copies, waits for them, and re-layouts  20.4 us (6%)
  starting transfers between devices  17.7 us (6%)
  between operations  14.1 us (4%)
  other arithmetic  8.98 us (3%)
    all_gather x1, waiting for transfers between devices, per_device(): tok_g = lax.all_gather(packed, 'ez', axis=0, tiled=True)  59.6 us
    all_to_all x1, waiting for transfers between devices, per_device(): lax.all_to_all(term, ('ey', 'ez'), split_axis=0, concat_axis=0, tiled=True)  58.4 us
    all_gather x1, waiting for transfers between devices, per_device(): cot_g = lax.all_gather(cotangent, 'ez', axis=0, tiled=True)  37.5 us
    ppermute x3, waiting for transfers between devices, shift_along_y(): lax.ppermute(out, 'ey', perm=[(i, (i + shift) % n_y) for i in range(n_y)])  27.8 us
    dot_general x2, matrix products, select_rows(): return jnp.dot(picks, source, preferred_element_type=jnp.float32)  19.6 us
    dot_general x1, matrix products, per_device(): lax.dot_general(rows_flat, coeff, (((0,), (0,)), ((), ())), preferred_ele...  14.1 us
    dot_general x3, matrix products, per_device(): lax.dot_general(spread.reshape(rows_dev, expert_count, capacity), returne...  10.9 us
    all_to_all x1, starting transfers between devices, per_device(): lax.all_to_all(term, ('ey', 'ez'), split_axis=0, concat_axis=0, tiled=True)  9.14 us
  transfers between devices with their start and end apart: 8, of which 7 were waited for; matrix products, arithmetic and copies ran while one was open for 27% of the time, Pallas kernels for 0%

profile of v4, /device:TPU:32, one launch (start us, length us, event | category | flops | bytes accessed | tf_op | source)
XLA Modules:
  0.0 320.5 jit_solution(4439932288606530066)
XLA Ops:
  7.2 0.8 convert_reduce_fusion
  8.2 0.2 reduce_window_sum.11
  8.4 0.8 select_reduce_fusion.6
  9.2 0.4 select_reduce_fusion.4
  9.6 0.1 copy.60
  9.8 0.1 convert_element_type.66
  9.9 2.0 pad_maximum_fusion
  12.0 0.7 all-gather.5.cloned.1.call-update
  13.1 59.6 %all-gather.3.cloned.1.call-done = bf16[1152,2048]{1,0:T(8,128)(2,1)} async-done(((bf16[144,2048]{1,0:T(8,128)(2,1)}), bf16[1152,2048]{1,0:T(8,128)(2,1)}) %all-gather.3.cloned.1.call-update) | async-done | bytes 4718608 | tf_op jit(solution)/shard_map/all_gather | solution.py:89
  72.6 1.1 slice_bitcast_fusion
  73.7 0.3 copy.71
  74.0 0.6 reshape.154
  74.9 10.4 %convolution_convert_fusion = bf16[1152,2048]{1,0:T(8,128)(2,1)} fusion(bf16[1152,2048]{1,0:T(8,128)(2,1)} %all-gather.3.cloned.1.call-done, s32[1152]{0:T(1024)S(1)} %get-tuple-element.19), kind=kOutput, calls=%fused_computation.1 | convolution fusion | flops 5439504384 | bytes 9441792 | tf_op jit(solution)/shard_map/dot_general | solution.py:47
  85.3 4.9 %all-to-all-start = ((bf16[4,288,2048]{2,1,0:T(8,128)(2,1)}), bf16[4,288,2048]{2,1,0:T(8,128)(2,1)}, u32[]{:S(2)}, u32[]{:S(2)}) async-start(bf16[4,288,2048]{2,1,0:T(8,128)(2,1)} %bitcast.88), calls=%async_computation | async-start | bytes 9437184 | tf_op jit(solution)/shard_map/all_to_all | solution.py:104
  90.4 37.5 %all-gather.5.cloned.1.call-done = bf16[1024,2048]{1,0:T(8,128)(2,1)} async-done(((bf16[128,2048]{1,0:T(8,128)(2,1)}), bf16[1024,2048]{1,0:T(8,128)(2,1)}) %all-gather.5.cloned.1.call-update) | async-done | bytes 4194320 | tf_op jit(solution)/shard_map/all_gather | solution.py:90
  127.9 9.2 %fusion = bf16[1152,2048]{1,0:T(8,128)(2,1)} fusion(bf16[1024,2048]{1,0:T(8,128)(2,1)} %all-gather.5.cloned.1.call-done, f32[1152]{0:T(1024)S(1)} %add.159, s32[1152]{0:T(1024)S(1)} %get-tuple-element.18), kind=kOutput, calls=%fused_computation.2 | convolution fusion | flops 4837736448 | bytes 8922112 | tf_op jit(solution)/shard_map/dot_general | solution.py:47
  137.0 8.0 %all-to-all-done = bf16[4,288,2048]{2,1,0:T(8,128)(2,1)} async-done(((bf16[4,288,2048]{2,1,0:T(8,128)(2,1)}), bf16[4,288,2048]{2,1,0:T(8,128)(2,1)}, u32[]{:S(2)}, u32[]{:S(2)}) %all-to-all-start) | async-done | bytes 4718624 | tf_op jit(solution)/shard_map/all_to_all | solution.py:104
  145.0 0.6 broadcast_in_dim.103
  145.6 1.7 copy-done.1
  147.4 2.0 dynamic-slice_bitcast_fusion
  149.3 0.6 collective-permute-start
  149.9 2.1 collective-permute-start.1
  152.0 0.6 collective-permute-start.2
  152.6 4.5 %fusion.16 = f32[1152,512]{1,0:T(8,128)S(1)} fusion(bf16[1152,2048]{1,0:T(8,128)(2,1)} %bitcast.5, bf16[1,2048,512]{2,1,0:T(8,128)(2,1)S(1)} %copy-done.5), kind=kOutput, calls=%fused_computation.32 | convolution fusion | flops 2415919104 | bytes 9175040 | tf_op jit(solution)/shard_map/dot_general | solution.py:19
  157.1 5.4 %fusion.18 = f32[1152,512]{1,0:T(8,128)S(1)} fusion(bf16[1152,2048]{1,0:T(8,128)(2,1)} %bitcast.5, bf16[1,2048,512]{2,1,0:T(8,128)(2,1)S(1)} %copy-done.6), kind=kOutput, calls=%fused_computation.34 | convolution fusion | flops 2415919104 | bytes 9175040 | tf_op jit(solution)/shard_map/dot_general | solution.py:17
  162.6 8.3 %fusion.13 = (bf16[1152,512]{1,0:T(8,128)(2,1)}, f32[1152,512]{1,0:T(8,128)}) fusion(f32[1152,512]{1,0:T(8,128)S(1)} %fusion.16, f32[1152,512]{1,0:T(8,128)S(1)} %fusion.18, bf16[1152,2048]{1,0:T(8,128)(2,1)} %bitcast.5, bf16[1,2048,512]{2,1,0:T(8,128)(2,1)S(1)} %copy-done.7), kind=kOutput, calls=%fused_computation.28 | convolution fusion | flops 2421817344 | bytes 15073280 | tf_op jit(solution)/shard_map/dot_general | solution.py:18
  170.8 2.1 reshape.157
  173.0 4.6 %convolution_convert_fusion.1 = bf16[32,36,2048]{2,1,0:T(8,128)(2,1)} fusion(bf16[32,36,512]{2,1,0:T(8,128)(2,1)S(1)} %reshape.157, bf16[1,512,2048]{2,1,0:T(8,128)(2,1)S(1)} %copy-done), kind=kOutput, calls=%fused_computation.9 | convolution fusion | flops 2418278400 | bytes 7995392 | tf_op jit(solution)/shard_map/dot_general | solution.py:22
  177.6 9.1 %all-to-all-start.1 = ((bf16[32,36,2048]{2,1,0:T(8,128)(2,1)}), bf16[32,36,2048]{2,1,0:T(8,128)(2,1)}, u32[]{:S(2)}, u32[]{:S(2)}) async-start(bf16[32,36,2048]{2,1,0:T(8,128)(2,1)} %convolution_convert_fusion.1), calls=%async_computation.2 | async-start | bytes 10485760 | tf_op jit(solution)/shard_map/all_to_all | solution.py:111
  186.8 0.3 reduce-scatter.2.cloned.1.call-start
  187.0 24.8 %collective-permute-done = bf16[288,2048]{1,0:T(8,128)(2,1)} collective-permute-done((bf16[288,2048]{1,0:T(8,128)(2,1)}, bf16[288,2048]{1,0:T(8,128)(2,1)}, u32[]{:S(2)}, u32[]{:S(2)}) %collective-permute-start) | collective-permute-done | bytes 1179680 | tf_op jit(solution)/shard_map/ppermute | solution.py:57
  211.8 2.5 bitcast_dynamic-update-slice_fusion.2
  214.3 0.6 collective-permute-done.1
  214.9 2.4 bitcast_dynamic-update-slice_fusion.1
  217.3 2.4 collective-permute-done.2
  219.8 2.4 bitcast_dynamic-update-slice_fusion
  222.2 14.1 %fusion.25 = f32[2048,512]{1,0:T(8,128)} fusion(bf16[1152,2048]{1,0:T(8,128)(2,1)} %bitcast.5, bf16[1152,2048]{1,0:T(8,128)(2,1)} %bitcast.89, f32[1152,512]{1,0:T(8,128)} %copy-done.8, f32[1152,512]{1,0:T(8,128)} %get-tuple-element.24, f32[1152,512]{1,0:T(8,128)} %copy-done.9, bf16[1,512,2048]{2,1,0:T(8,128)(2,1)S(1)} %copy-done), kind=kOutput, calls=%fused_computation.62 | convolution fusion | flops 4840095744 | bytes 22806528 | tf_op jit(solution)/shard_map/dot_general | solution.py:115
  236.3 0.7 copy-done.4
  237.1 0.1 copy.63
  237.4 4.7 %select_reduce_fusion.2 = (bf16[128,1152]{1,0:T(8,128)(2,1)S(1)}, bf16[128,1152]{1,0:T(8,128)(2,1)S(1)}, bf16[128,1152]{1,0:T(8,128)(2,1)S(1)}) fusion(f32[128,8]{1,0:T(8,128)S(1)} %copy.64, s32[128,8]{1,0:T(8,128)S(1)} %copy.63, f32[128,8]{1,0:T(8,128)S(1)} %copy.68, f32[128,8]{1,0:T(8,128)S(1)} %copy.66), kind=kLoop, calls=%fused_computation.6 | loop fusion | flops 7815168 | bytes 901120 | tf_op jit(solution)/shard_map/reduce_sum | solution.py:123
  242.1 0.2 copy.69
  242.4 0.2 copy.67
  242.7 0.9 copy.65
  243.6 1.0 convert_element_type.73
  244.6 58.4 %all-to-all-done.1 = bf16[32,36,2048]{2,1,0:T(8,128)(2,1)} async-done(((bf16[32,36,2048]{2,1,0:T(8,128)(2,1)}), bf16[32,36,2048]{2,1,0:T(8,128)(2,1)}, u32[]{:S(2)}, u32[]{:S(2)}) %all-to-all-start.1) | async-done | bytes 4718624 | tf_op jit(solution)/shard_map/all_to_all | solution.py:111
  303.0 3.4 %convolution_bitcast_fusion = f32[128,2048]{1,0:T(8,128)S(1)} fusion(bf16[128,32,36]{0,2,1:T(8,128)(2,1)S(1)} %convert_element_type.79, bf16[32,36,2048]{2,1,0:T(8,128)(2,1)} %all-to-all-done.1), kind=kOutput, calls=%fused_computation.15 | convolution fusion | flops 603979776 | bytes 6062080 | tf_op jit(solution)/shard_map/dot_general | solution.py:124
  306.4 3.4 %convolution_bitcast_fusion.1 = f32[128,2048]{1,0:T(8,128)S(1)} fusion(bf16[128,32,36]{0,2,1:T(8,128)(2,1)S(1)} %convert_element_type.77, bf16[32,36,2048]{2,1,0:T(8,128)(2,1)} %all-to-all-done.1), kind=kOutput, calls=%fused_computation.16 | convolution fusion | flops 603979776 | bytes 6062080 | tf_op jit(solution)/shard_map/dot_general | solution.py:124
  309.8 4.2 %fusion.5 = bf16[128,2048]{1,0:T(8,128)(2,1)} fusion(f32[128,2048]{1,0:T(8,128)S(1)} %convolution_bitcast_fusion, f32[128,2048]{1,0:T(8,128)S(1)} %convolution_bitcast_fusion.1, bf16[128,32,36]{0,2,1:T(8,128)(2,1)S(1)} %convert_element_type.73, bf16[32,36,2048]{2,1,0:T(8,128)(2,1)} %all-to-all-done.1), kind=kOutput, calls=%fused_computation.20 | convolution fusion | flops 604766208 | bytes 7634944 | tf_op jit(solution)/shard_map/dot_general | solution.py:124
  (54 shorter events, 1.5 us)
Async XLA Ops:
  7.2 165.8 %copy-start = (bf16[1,512,2048]{2,1,0:T(8,128)(2,1)S(1)}, bf16[1,512,2048]{2,1,0:T(8,128)(2,1)}, u32[]{:S(2)}) copy-start(bf16[1,512,2048]{2,1,0:T(8,128)(2,1)} %param.14) | copy-start | bytes 6291460
  7.2 65.4 %all-gather.3.cloned.1.call-start = ((), (), s32[]{:S(2)}) async-start(), calls=%async_computation.3 | async-start | bytes 5308416 | tf_op jit(solution)/shard_map/all_gather | solution.py:89
  11.9 115.9 %all-gather.5.cloned.1.call-start = ((), (), s32[]{:S(2)}) async-start(), calls=%async_computation.4 | async-start | bytes 4718592 | tf_op jit(solution)/shard_map/all_gather | solution.py:90
  85.3 59.7 %all-to-all-start = ((bf16[4,288,2048]{2,1,0:T(8,128)(2,1)}), bf16[4,288,2048]{2,1,0:T(8,128)(2,1)}, u32[]{:S(2)}, u32[]{:S(2)}) async-start(bf16[4,288,2048]{2,1,0:T(8,128)(2,1)} %bitcast.88), calls=%async_computation | async-start | bytes 9437184 | tf_op jit(solution)/shard_map/all_to_all | solution.py:104
  145.0 2.3 copy-start.1
  147.4 5.2 %copy-start.5 = (bf16[1,2048,512]{2,1,0:T(8,128)(2,1)S(1)}, bf16[1,2048,512]{2,1,0:T(8,128)(2,1)}, u32[]{:S(2)}) copy-start(bf16[1,2048,512]{2,1,0:T(8,128)(2,1)} %param.15) | copy-start | bytes 6291460
  149.3 7.8 %copy-start.2 = (bf16[4,288,2048]{2,1,0:T(8,128)(2,1)}, bf16[4,288,2048]{2,1,0:T(8,128)(2,1)S(1)}, u32[]{:S(2)}) copy-start(bf16[4,288,2048]{2,1,0:T(8,128)(2,1)S(1)} %get-tuple-element.12) | copy-start | bytes 14155780
  149.3 62.4 %collective-permute-start = (bf16[288,2048]{1,0:T(8,128)(2,1)}, bf16[288,2048]{1,0:T(8,128)(2,1)}, u32[]{:S(2)}, u32[]{:S(2)}) collective-permute-start(bf16[288,2048]{1,0:T(8,128)(2,1)} %get-tuple-element.11), channel_id=1, source_target_pairs={{0,1},{1,2},{2,3},{3,0},{4,5},{5,6},{6,7},{7,4},{8,9},{9,10},{10,1... | collective-permute-start | bytes 3538952 | tf_op jit(solution)/shard_map/ppermute | solution.py:57
  149.9 65.0 %collective-permute-start.1 = (bf16[288,2048]{1,0:T(8,128)(2,1)}, bf16[288,2048]{1,0:T(8,128)(2,1)}, u32[]{:S(2)}, u32[]{:S(2)}) collective-permute-start(bf16[288,2048]{1,0:T(8,128)(2,1)} %get-tuple-element.10), channel_id=1, source_target_pairs={{0,2},{1,3},{2,0},{3,1},{4,6},{5,7},{6,4},{7,5},{8,10},{9,11},{10,... | collective-permute-start | bytes 3538952 | tf_op jit(solution)/shard_map/ppermute | solution.py:57
  152.0 5.1 %copy-start.6 = (bf16[1,2048,512]{2,1,0:T(8,128)(2,1)S(1)}, bf16[1,2048,512]{2,1,0:T(8,128)(2,1)}, u32[]{:S(2)}) copy-start(bf16[1,2048,512]{2,1,0:T(8,128)(2,1)} %param.12) | copy-start | bytes 6291460
  152.0 67.8 %collective-permute-start.2 = (bf16[288,2048]{1,0:T(8,128)(2,1)}, bf16[288,2048]{1,0:T(8,128)(2,1)}, u32[]{:S(2)}, u32[]{:S(2)}) collective-permute-start(bf16[288,2048]{1,0:T(8,128)(2,1)} %get-tuple-element.9), channel_id=1, source_target_pairs={{0,3},{1,0},{2,1},{3,2},{4,7},{5,4},{6,5},{7,6},{8,11},{9,8},{10,9... | collective-permute-start | bytes 3538952 | tf_op jit(solution)/shard_map/ppermute | solution.py:57
  157.1 5.4 %copy-start.8 = (f32[1152,512]{1,0:T(8,128)}, f32[1152,512]{1,0:T(8,128)S(1)}, u32[]{:S(2)}) copy-start(f32[1152,512]{1,0:T(8,128)S(1)} %fusion.16) | copy-start | bytes 7077892
  157.1 5.4 %copy-start.7 = (bf16[1,2048,512]{2,1,0:T(8,128)(2,1)S(1)}, bf16[1,2048,512]{2,1,0:T(8,128)(2,1)}, u32[]{:S(2)}) copy-start(bf16[1,2048,512]{2,1,0:T(8,128)(2,1)} %param.13) | copy-start | bytes 6291460
  162.5 8.3 %copy-start.9 = (f32[1152,512]{1,0:T(8,128)}, f32[1152,512]{1,0:T(8,128)S(1)}, u32[]{:S(2)}) copy-start(f32[1152,512]{1,0:T(8,128)S(1)} %fusion.18) | copy-start | bytes 7077892
  177.6 125.4 %all-to-all-start.1 = ((bf16[32,36,2048]{2,1,0:T(8,128)(2,1)}), bf16[32,36,2048]{2,1,0:T(8,128)(2,1)}, u32[]{:S(2)}, u32[]{:S(2)}) async-start(bf16[32,36,2048]{2,1,0:T(8,128)(2,1)} %convolution_convert_fusion.1), calls=%async_computation.2 | async-start | bytes 10485760 | tf_op jit(solution)/shard_map/all_to_all | solution.py:111
  186.8 127.2 %reduce-scatter.2.cloned.1.call-start = ((), (), s32[]{:S(2)}) async-start(), calls=%async_computation.5 | async-start | bytes 4718592 | tf_op jit(solution)/shard_map/reduce_scatter | solution.py:118
  236.2 0.7 copy-start.4
  236.3 0.8 copy-start.3
Sparse Core Ops, SparseCore 0:
  12.0 60.5 all-gather.2
  74.4 53.4 all-gather.4
  236.4 43.0 reduce-scatter.1

commit v5 on v4

--- a/solution.py
+++ b/solution.py
@@ -13,10 +13,19 @@
     return (first, second)
 
 
-def forward_part(rows_flat, gate_e, up_e, down_e, tangent_e, blocks):
-    gate_act = jnp.dot(rows_flat, gate_e, preferred_element_type=jnp.float32)
-    up_act = jnp.dot(rows_flat, up_e, preferred_element_type=jnp.float32)
-    gate_dot = jnp.dot(rows_flat, tangent_e, preferred_element_type=jnp.float32)
+def forward_part(halves, gate_e, up_e, down_e, tangent_e, blocks):
+    cut = halves[0].shape[1]
+
+    def project(weight):
+        parts = [
+            jnp.dot(h, weight[i * cut : (i + 1) * cut], preferred_element_type=jnp.float32)
+            for i, h in enumerate(halves)
+        ]
+        return parts[0] + parts[1]
+
+    gate_act = project(gate_e)
+    up_act = project(up_e)
+    gate_dot = project(tangent_e)
     first, second = silu_derivs(gate_act)
     lifted = (first * gate_dot * up_act).astype(jnp.bfloat16)
     term = lax.dot_general(
@@ -82,13 +91,15 @@
     w_of = jnp.sum(jnp.where(in_slot, weight_te[:, :, None], 0.0), axis=0)
     table = jnp.stack((src_of,) + split3(w_of)).astype(jnp.bfloat16)
     extra = 16
-    table = jnp.pad(table.reshape(-1), (0, extra * model_width - 4 * slots))
-    packed = jnp.concatenate([tokens, table.reshape(extra, model_width)], axis=0)
+    cut = model_width // 2
+    table = jnp.pad(table.reshape(-1), (0, extra * cut - 4 * slots))
+    packed = jnp.concatenate([tokens[:, :cut], table.reshape(extra, cut)], axis=0)
     block = rows_dev + extra
 
-    tok_g = lax.all_gather(packed, "ez", axis=0, tiled=True)
+    tok_a = lax.all_gather(packed, "ez", axis=0, tiled=True)
+    tok_b = lax.all_gather(tokens[:, cut:], "ez", axis=0, tiled=True)
     cot_g = lax.all_gather(cotangent, "ez", axis=0, tiled=True)
-    table_g = tok_g.reshape(n_z, block, model_width)[:, rows_dev:].reshape(n_z, -1)
+    table_g = tok_a.reshape(n_z, block, cut)[:, rows_dev:].reshape(n_z, -1)
     table_g = table_g[:, : 4 * slots].reshape(n_z, 4, expert_count, capacity)
     z_me = lax.axis_index("ez")
     mine = lax.dynamic_slice_in_dim(table_g, z_me * n_y, n_y, axis=2).astype(jnp.float32)
@@ -99,21 +110,27 @@
     z_of = jnp.arange(n_z, dtype=jnp.int32)[None, :, None]
     at_packed = jnp.where(valid, src_tok + z_of * block, -1).reshape(-1)
     at_cot = jnp.where(valid, src_tok + z_of * rows_dev, -1).reshape(-1)
-    send_rows = select_rows(at_packed, tok_g).astype(jnp.bfloat16)
+    send_a = select_rows(at_packed, tok_a).astype(jnp.bfloat16)
+    send_b = select_rows(at_cot, tok_b).astype(jnp.bfloat16)
 
-    rows_flat = lax.all_to_all(send_rows, "ey", split_axis=0, concat_axis=0, tiled=True)
+    rows_a = lax.all_to_all(send_a, "ey", split_axis=0, concat_axis=0, tiled=True)
+    rows_b = lax.all_to_all(send_b, "ey", split_axis=0, concat_axis=0, tiled=True)
     gate_e = w_gate[0]
     up_e = w_up[0]
     down_e = w_down[0]
     tangent_e = tangent_gate[0]
     send_scaled = (src_w.reshape(-1)[:, None] * select_rows(at_cot, cot_g)).astype(jnp.bfloat16)
-    term, factor = forward_part(rows_flat, gate_e, up_e, down_e, tangent_e, (expert_count, capacity))
+    term, factor = forward_part((rows_a, rows_b), gate_e, up_e, down_e, tangent_e, (expert_count, capacity))
     returned = lax.all_to_all(term, ("ey", "ez"), split_axis=0, concat_axis=0, tiled=True)
-    _, send_scaled = lax.optimization_barrier((rows_flat, send_scaled))
+    _, send_scaled = lax.optimization_barrier((rows_b, send_scaled))
     scaled_flat = shift_along_y(send_scaled, n_y)
     coeff = backward_part(scaled_flat, down_e, factor)
-    partial_hvp = lax.dot_general(
-        rows_flat, coeff, (((0,), (0,)), ((), ())), preferred_element_type=jnp.float32
+    partial_hvp = jnp.concatenate(
+        [
+            lax.dot_general(h, coeff, (((0,), (0,)), ((), ())), preferred_element_type=jnp.float32)
+            for h in (rows_a, rows_b)
+        ],
+        axis=0,
     )
     hvp_gate = lax.psum_scatter(partial_hvp, "dp", scatter_dimension=0, tiled=True)
     back_at = ((expert_ids % n_y) * n_z + expert_ids // n_y) * capacity + slot_pos

time: 321 us -> 327 us (1.019)
  waiting for transfers between devices: 192 us -> 180 us
  matrix products: 67.4 us -> 78.1 us
  starting transfers between devices: 17.7 us -> 23.7 us
    all_gather x1, waiting for transfers between devices: 37.5 us -> 7.61 us  [per_device(): cot_g = lax.all_gather(cotangent, 'ez', axis=0, tiled=True)]
    ppermute x3, waiting for transfers between devices: 27.8 us -> 47.4 us  [shift_along_y(): lax.ppermute(out, 'ey', perm=[(i, (i + shift) % n_y) for i in range(n_y)])]
    all_to_all x1, waiting for transfers between devices: 58.4 us -> 40.8 us  [per_device(): lax.all_to_all(term, ('ey', 'ez'), split_axis=0, concat_axis=0, tiled=True)]
    all_gather x1 -> x2, waiting for transfers between devices: 59.6 us -> 71.5 us  [the longest x1 42 us: per_device(): tok_a = lax.all_gather(packed, 'ez', axis=0, tiled=True)]
    dot_general x4 -> x9, matrix products: 32.2 us -> 42.6 us  [the longest x6 30.1 us: project(): jnp.dot(h, weight[i * cut:(i + 1) * cut], preferred_element_type=jnp.floa...]
    all_to_all x1 -> x2, starting transfers between devices: 4.94 us -> 9.21 us  [the longest x1 4.69 us: per_device(): lax.all_to_all(send_b, 'ey', split_axis=0, concat_axis=0, tiled=True)]
    ppermute x3, starting transfers between devices: 3.24 us -> 7.25 us  [shift_along_y(): lax.ppermute(out, 'ey', perm=[(i, (i + shift) % n_y) for i in range(n_y)])]
    all_to_all x1 -> x2, waiting for transfers between devices: 8 us -> 11.1 us  [the longest x1 11.1 us: per_device(): lax.all_to_all(send_b, 'ey', split_axis=0, concat_axis=0, tiled=True)]
  transfers between devices with their start and end apart: 8 -> 10, of which waited for: 7 -> 7; matrix products, arithmetic and copies ran while one was open for 27% -> 28% of each run, Pallas kernels for 0% -> 0%
where the time goes in v5:
time: 327 us; the launch traced here: 325 us
  waiting for transfers between devices  180 us (55%)
  matrix products  78.1 us (24%)
  starting transfers between devices  23.7 us (7%)
  local copies, waits for them, and re-layouts  19 us (6%)
  between operations  14.2 us (4%)
  other arithmetic  10.5 us (3%)
    ppermute x3, waiting for transfers between devices, shift_along_y(): lax.ppermute(out, 'ey', perm=[(i, (i + shift) % n_y) for i in range(n_y)])  47.4 us
    all_gather x1, waiting for transfers between devices, per_device(): tok_a = lax.all_gather(packed, 'ez', axis=0, tiled=True)  42 us
    all_to_all x1, waiting for transfers between devices, per_device(): lax.all_to_all(term, ('ey', 'ez'), split_axis=0, concat_axis=0, tiled=True)  40.8 us
    dot_general x6, matrix products, project(): jnp.dot(h, weight[i * cut:(i + 1) * cut], preferred_element_type=jnp.floa...  30.1 us
    all_gather x1, waiting for transfers between devices, per_device(): tok_b = lax.all_gather(tokens[:, cut:], 'ez', axis=0, tiled=True)  29.5 us
    dot_general x3, matrix products, select_rows(): return jnp.dot(picks, source, preferred_element_type=jnp.float32)  19.8 us
    all_to_all x1, waiting for transfers between devices, per_device(): lax.all_to_all(send_b, 'ey', split_axis=0, concat_axis=0, tiled=True)  11.1 us
    dot_general x3, matrix products, per_device(): lax.dot_general(spread.reshape(rows_dev, expert_count, capacity), returne...  11 us
  transfers between devices with their start and end apart: 10, of which 7 were waited for; matrix products, arithmetic and copies ran while one was open for 28% of the time, Pallas kernels for 0%

profile of v5, /device:TPU:32, one launch (start us, length us, event | category | flops | bytes accessed | tf_op | source)
XLA Modules:
  0.0 325.2 jit_solution(2913989461486959157)
XLA Ops:
  7.2 0.8 convert_reduce_fusion
  8.2 1.8 fusion.48
  10.2 0.7 select_reduce_fusion.6
  10.9 0.4 select_reduce_fusion.4
  11.7 0.7 pad_maximum_fusion.1
  12.5 0.7 all-gather.6.cloned.1.call-update
  13.2 0.7 all-gather.8.cloned.1.call-update
  14.3 42.0 %all-gather.4.cloned.1.call-done = bf16[1152,1024]{1,0:T(8,128)(2,1)} async-done(((bf16[144,1024]{1,0:T(8,128)(2,1)}), bf16[1152,1024]{1,0:T(8,128)(2,1)}) %all-gather.4.cloned.1.call-update) | async-done | bytes 2359312 | tf_op jit(solution)/shard_map/all_gather | solution.py:99
  56.3 1.0 slice_bitcast_fusion
  57.5 0.6 reshape.162
  58.3 6.3 %fusion.4 = bf16[1152,1024]{1,0:T(8,128)(2,1)} fusion(bf16[1152,1024]{1,0:T(8,128)(2,1)} %all-gather.4.cloned.1.call-done, s32[1152]{0:T(1024)S(1)} %get-tuple-element.20), kind=kOutput, calls=%fused_computation.13 | convolution fusion | flops 2720415744 | bytes 4723200 | tf_op jit(solution)/shard_map/dot_general | solution.py:56
  64.7 4.5 %all-to-all-start = ((bf16[4,288,1024]{2,1,0:T(8,128)(2,1)}), bf16[4,288,1024]{2,1,0:T(8,128)(2,1)}, u32[]{:S(2)}, u32[]{:S(2)}) async-start(bf16[4,288,1024]{2,1,0:T(8,128)(2,1)} %bitcast.106), calls=%async_computation | async-start | bytes 4718592 | tf_op jit(solution)/shard_map/all_to_all | solution.py:116
  69.2 29.5 %all-gather.6.cloned.1.call-done = bf16[1024,1024]{1,0:T(8,128)(2,1)} async-done(((bf16[128,1024]{1,0:T(8,128)(2,1)}), bf16[1024,1024]{1,0:T(8,128)(2,1)}) %all-gather.6.cloned.1.call-update) | async-done | bytes 2097168 | tf_op jit(solution)/shard_map/all_gather | solution.py:100
  98.7 5.7 %fusion.3 = bf16[1152,1024]{1,0:T(8,128)(2,1)} fusion(bf16[1024,1024]{1,0:T(8,128)(2,1)} %all-gather.6.cloned.1.call-done, s32[1152]{0:T(1024)S(1)} %get-tuple-element.21), kind=kOutput, calls=%fused_computation.12 | convolution fusion | flops 2418278400 | bytes 4461056 | tf_op jit(solution)/shard_map/dot_general | solution.py:56
  104.4 4.7 %all-to-all-start.1 = ((bf16[4,288,1024]{2,1,0:T(8,128)(2,1)}), bf16[4,288,1024]{2,1,0:T(8,128)(2,1)}, u32[]{:S(2)}, u32[]{:S(2)}) async-start(bf16[4,288,1024]{2,1,0:T(8,128)(2,1)} %bitcast.105), calls=%async_computation.1 | async-start | bytes 4718592 | tf_op jit(solution)/shard_map/all_to_all | solution.py:117
  109.3 5.1 %fusion.23 = f32[1152,512]{1,0:T(8,128)} fusion(bf16[1152,1024]{1,0:T(8,128)(2,1)} %bitcast.5, bf16[1,2048,512]{2,1,0:T(8,128)(2,1)} %param.15), kind=kOutput, calls=%fused_computation.49 | convolution fusion | flops 1207959552 | bytes 5767168 | tf_op jit(solution)/shard_map/dot_general | solution.py:21
  114.3 4.7 %fusion.26 = f32[1152,512]{1,0:T(8,128)} fusion(bf16[1152,1024]{1,0:T(8,128)(2,1)} %bitcast.5, bf16[1,2048,512]{2,1,0:T(8,128)(2,1)S(1)} %copy-done.4), kind=kOutput, calls=%fused_computation.52 | convolution fusion | flops 1207959552 | bytes 5767168 | tf_op jit(solution)/shard_map/dot_general | solution.py:21
  119.0 4.5 %fusion.29 = f32[1152,512]{1,0:T(8,128)} fusion(bf16[1152,1024]{1,0:T(8,128)(2,1)} %bitcast.5, bf16[1,2048,512]{2,1,0:T(8,128)(2,1)S(1)} %copy-done.6), kind=kOutput, calls=%fused_computation.55 | convolution fusion | flops 1207959552 | bytes 5767168 | tf_op jit(solution)/shard_map/dot_general | solution.py:21
  123.5 11.1 %all-to-all-done.1 = bf16[4,288,1024]{2,1,0:T(8,128)(2,1)} async-done(((bf16[4,288,1024]{2,1,0:T(8,128)(2,1)}), bf16[4,288,1024]{2,1,0:T(8,128)(2,1)}, u32[]{:S(2)}, u32[]{:S(2)}) %all-to-all-start.1) | async-done | bytes 2359328 | tf_op jit(solution)/shard_map/all_to_all | solution.py:117
  134.6 5.8 %convolution_add_fusion = f32[1152,512]{1,0:T(8,128)} fusion(f32[1152,512]{1,0:T(8,128)} %fusion.23, bf16[1152,1024]{1,0:T(8,128)(2,1)} %bitcast.7, bf16[1,2048,512]{2,1,0:T(8,128)(2,1)} %param.15), kind=kOutput, calls=%fused_computation.17 | convolution fusion | flops 1208549376 | bytes 8126464 | tf_op jit(solution)/shard_map/dot_general | solution.py:21
  140.4 4.6 %convolution_add_fusion.1 = f32[1152,512]{1,0:T(8,128)} fusion(f32[1152,512]{1,0:T(8,128)S(1)} %copy-done.12, bf16[1152,1024]{1,0:T(8,128)(2,1)} %bitcast.7, bf16[1,2048,512]{2,1,0:T(8,128)(2,1)S(1)} %copy-done.5), kind=kOutput, calls=%fused_computation.18 | convolution fusion | flops 1208549376 | bytes 8126464 | tf_op jit(solution)/shard_map/dot_general | solution.py:21
  145.0 7.6 %all-gather.8.cloned.1.call-done = bf16[1024,2048]{1,0:T(8,128)(2,1)} async-done(((bf16[128,2048]{1,0:T(8,128)(2,1)}), bf16[1024,2048]{1,0:T(8,128)(2,1)}) %all-gather.8.cloned.1.call-update) | async-done | bytes 4194320 | tf_op jit(solution)/shard_map/all_gather | solution.py:101
  152.6 7.8 %fusion = bf16[1152,2048]{1,0:T(8,128)(2,1)S(1)} fusion(bf16[1024,2048]{1,0:T(8,128)(2,1)} %all-gather.8.cloned.1.call-done, f32[1152]{0:T(1024)S(1)} %add.171, s32[1152]{0:T(1024)S(1)} %get-tuple-element.21), kind=kOutput, calls=%fused_computation.1 | convolution fusion | flops 4837736448 | bytes 8922112 | tf_op jit(solution)/shard_map/dot_general | solution.py:56
  160.3 0.6 broadcast_in_dim.104
  161.0 2.0 dynamic-slice_bitcast_fusion
  163.0 1.5 collective-permute-start
  164.5 2.7 collective-permute-start.1
  167.2 0.4 copy-done.13
  167.6 5.5 %fusion.17 = (bf16[1152,512]{1,0:T(8,128)(2,1)}, f32[1152,512]{1,0:T(8,128)}) fusion(f32[1152,512]{1,0:T(8,128)S(1)} %copy-done.8, f32[1152,512]{1,0:T(8,128)S(1)} %copy-done.10, f32[1152,512]{1,0:T(8,128)S(1)} %copy-done.13, bf16[1152,1024]{1,0:T(8,128)(2,1)} %bitcast.7, bf16[1,2048,512]{2,1,0:T(8,128)(2,1)S(1)} %copy-done.7), kind=kOutput, calls=%fused_computation.35 | convolution fusion | flops 1214447616 | bytes 14024704 | tf_op jit(solution)/shard_map/dot_general | solution.py:21
  173.1 2.1 reshape.165
  175.2 3.0 collective-permute-start.2
  178.2 4.6 %convolution_convert_fusion = bf16[32,36,2048]{2,1,0:T(8,128)(2,1)} fusion(bf16[32,36,512]{2,1,0:T(8,128)(2,1)S(1)} %reshape.165, bf16[1,512,2048]{2,1,0:T(8,128)(2,1)S(1)} %copy-done), kind=kOutput, calls=%fused_computation.11 | convolution fusion | flops 2418278400 | bytes 7995392 | tf_op jit(solution)/shard_map/dot_general | solution.py:31
  182.9 7.1 %all-to-all-start.2 = ((bf16[32,36,2048]{2,1,0:T(8,128)(2,1)}), bf16[32,36,2048]{2,1,0:T(8,128)(2,1)}, u32[]{:S(2)}, u32[]{:S(2)}) async-start(bf16[32,36,2048]{2,1,0:T(8,128)(2,1)} %convolution_convert_fusion), calls=%async_computation.3 | async-start | bytes 10485760 | tf_op jit(solution)/shard_map/all_to_all | solution.py:124
  190.0 2.4 collective-permute-done
  192.4 2.6 bitcast_dynamic-update-slice_fusion.2
  195.0 45.0 %collective-permute-done.1 = bf16[288,2048]{1,0:T(8,128)(2,1)} collective-permute-done((bf16[288,2048]{1,0:T(8,128)(2,1)}, bf16[288,2048]{1,0:T(8,128)(2,1)}, u32[]{:S(2)}, u32[]{:S(2)}) %collective-permute-start.1) | collective-permute-done | bytes 1179680 | tf_op jit(solution)/shard_map/ppermute | solution.py:66
  240.0 2.4 bitcast_dynamic-update-slice_fusion.1
  242.4 2.4 bitcast_dynamic-update-slice_fusion
  244.9 6.1 %fusion.5 = bf16[1152,512]{1,0:T(8,128)(2,1)S(1)} fusion(bf16[1152,2048]{1,0:T(8,128)(2,1)} %bitcast.104, f32[1152,512]{1,0:T(8,128)S(1)} %copy-done.9, f32[1152,512]{1,0:T(8,128)S(1)} %copy-done.14, f32[1152,512]{1,0:T(8,128)S(1)} %copy-done.11, bf16[1,512,2048]{2,1,0:T(8,128)(2,1)S(1)} %copy-done), kind=kOutput, calls=%fused_computation.20 | convolution fusion | flops 2424176640 | bytes 15073280 | tf_op jit(solution)/shard_map/dot_general | solution.py:41
  251.0 3.2 fusion.50
  254.2 3.2 fusion.49
  257.4 2.5 pad_maximum_fusion
  260.0 0.7 copy-done.3
  261.1 5.0 %select_reduce_fusion.2 = (bf16[128,1152]{1,0:T(8,128)(2,1)S(1)}, bf16[128,1152]{1,0:T(8,128)(2,1)S(1)}, bf16[128,1152]{1,0:T(8,128)(2,1)S(1)}) fusion(f32[128,8]{1,0:T(8,128)S(1)} %copy.64, s32[128,8]{1,0:T(8,128)S(1)} %copy.63, f32[128,8]{1,0:T(8,128)S(1)} %copy.68, f32[128,8]{1,0:T(8,128)S(1)} %copy.66), kind=kLoop, calls=%fused_computation.6 | loop fusion | flops 7815168 | bytes 901120 | tf_op jit(solution)/shard_map/reduce_sum | solution.py:140
  266.9 40.8 %all-to-all-done.2 = bf16[32,36,2048]{2,1,0:T(8,128)(2,1)} async-done(((bf16[32,36,2048]{2,1,0:T(8,128)(2,1)}), bf16[32,36,2048]{2,1,0:T(8,128)(2,1)}, u32[]{:S(2)}, u32[]{:S(2)}) %all-to-all-start.2) | async-done | bytes 4718624 | tf_op jit(solution)/shard_map/all_to_all | solution.py:124
  307.7 3.4 %convolution_bitcast_fusion = f32[128,2048]{1,0:T(8,128)S(1)} fusion(bf16[128,32,36]{0,2,1:T(8,128)(2,1)S(1)} %convert_element_type.84, bf16[32,36,2048]{2,1,0:T(8,128)(2,1)} %all-to-all-done.2), kind=kOutput, calls=%fused_computation.22 | convolution fusion | flops 603979776 | bytes 6062080 | tf_op jit(solution)/shard_map/dot_general | solution.py:141
  311.1 3.5 %convolution_bitcast_fusion.1 = f32[128,2048]{1,0:T(8,128)S(1)} fusion(bf16[128,32,36]{0,2,1:T(8,128)(2,1)S(1)} %convert_element_type.82, bf16[32,36,2048]{2,1,0:T(8,128)(2,1)} %all-to-all-done.2), kind=kOutput, calls=%fused_computation.23 | convolution fusion | flops 603979776 | bytes 6062080 | tf_op jit(solution)/shard_map/dot_general | solution.py:141
  314.5 4.2 %fusion.9 = bf16[128,2048]{1,0:T(8,128)(2,1)} fusion(f32[128,2048]{1,0:T(8,128)S(1)} %convolution_bitcast_fusion, f32[128,2048]{1,0:T(8,128)S(1)} %convolution_bitcast_fusion.1, bf16[128,32,36]{0,2,1:T(8,128)(2,1)S(1)} %convert_element_type.78, bf16[32,36,2048]{2,1,0:T(8,128)(2,1)} %all-to-all-done.2), kind=kOutput, calls=%fused_computation.27 | convolution fusion | flops 604766208 | bytes 7634944 | tf_op jit(solution)/shard_map/dot_general | solution.py:141
  (77 shorter events, 2.9 us)
Async XLA Ops:
  7.2 171.1 %copy-start = (bf16[1,512,2048]{2,1,0:T(8,128)(2,1)S(1)}, bf16[1,512,2048]{2,1,0:T(8,128)(2,1)}, u32[]{:S(2)}) copy-start(bf16[1,512,2048]{2,1,0:T(8,128)(2,1)} %param.14) | copy-start | bytes 6291460
  7.2 49.2 %all-gather.4.cloned.1.call-start = ((), (), s32[]{:S(2)}) async-start(), calls=%async_computation.4 | async-start | bytes 2654208 | tf_op jit(solution)/shard_map/all_gather | solution.py:99
  12.4 86.2 %all-gather.6.cloned.1.call-start = ((), (), s32[]{:S(2)}) async-start(), calls=%async_computation.5 | async-start | bytes 2359296 | tf_op jit(solution)/shard_map/all_gather | solution.py:100
  13.2 139.4 %all-gather.8.cloned.1.call-start = ((), (), s32[]{:S(2)}) async-start(), calls=%async_computation.6 | async-start | bytes 4718592 | tf_op jit(solution)/shard_map/all_gather | solution.py:101
  64.7 39.7 %all-to-all-start = ((bf16[4,288,1024]{2,1,0:T(8,128)(2,1)}), bf16[4,288,1024]{2,1,0:T(8,128)(2,1)}, u32[]{:S(2)}, u32[]{:S(2)}) async-start(bf16[4,288,1024]{2,1,0:T(8,128)(2,1)} %bitcast.106), calls=%async_computation | async-start | bytes 4718592 | tf_op jit(solution)/shard_map/all_to_all | solution.py:116
  104.4 30.2 %all-to-all-start.1 = ((bf16[4,288,1024]{2,1,0:T(8,128)(2,1)}), bf16[4,288,1024]{2,1,0:T(8,128)(2,1)}, u32[]{:S(2)}, u32[]{:S(2)}) async-start(bf16[4,288,1024]{2,1,0:T(8,128)(2,1)} %bitcast.105), calls=%async_computation.1 | async-start | bytes 4718592 | tf_op jit(solution)/shard_map/all_to_all | solution.py:117
  109.2 5.1 %copy-start.4 = (bf16[1,2048,512]{2,1,0:T(8,128)(2,1)S(1)}, bf16[1,2048,512]{2,1,0:T(8,128)(2,1)}, u32[]{:S(2)}) copy-start(bf16[1,2048,512]{2,1,0:T(8,128)(2,1)} %param.12) | copy-start | bytes 6291460
  114.3 4.7 %copy-start.6 = (bf16[1,2048,512]{2,1,0:T(8,128)(2,1)S(1)}, bf16[1,2048,512]{2,1,0:T(8,128)(2,1)}, u32[]{:S(2)}) copy-start(bf16[1,2048,512]{2,1,0:T(8,128)(2,1)} %param.13) | copy-start | bytes 6291460
  134.6 5.8 %copy-start.5 = (bf16[1,2048,512]{2,1,0:T(8,128)(2,1)S(1)}, bf16[1,2048,512]{2,1,0:T(8,128)(2,1)}, u32[]{:S(2)}) copy-start(bf16[1,2048,512]{2,1,0:T(8,128)(2,1)} %param.12) | copy-start | bytes 6291460
  134.6 5.8 %copy-start.12 = (f32[1152,512]{1,0:T(8,128)S(1)}, f32[1152,512]{1,0:T(8,128)}, u32[]{:S(2)}) copy-start(f32[1152,512]{1,0:T(8,128)} %fusion.26) | copy-start | bytes 7077892
  160.9 6.3 %copy-start.7 = (bf16[1,2048,512]{2,1,0:T(8,128)(2,1)S(1)}, bf16[1,2048,512]{2,1,0:T(8,128)(2,1)}, u32[]{:S(2)}) copy-start(bf16[1,2048,512]{2,1,0:T(8,128)(2,1)} %param.13) | copy-start | bytes 6291460
  160.9 6.2 %copy-start.8 = (f32[1152,512]{1,0:T(8,128)S(1)}, f32[1152,512]{1,0:T(8,128)}, u32[]{:S(2)}) copy-start(f32[1152,512]{1,0:T(8,128)} %convolution_add_fusion) | copy-start | bytes 7077892
  161.0 6.2 %copy-start.10 = (f32[1152,512]{1,0:T(8,128)S(1)}, f32[1152,512]{1,0:T(8,128)}, u32[]{:S(2)}) copy-start(f32[1152,512]{1,0:T(8,128)} %convolution_add_fusion.1) | copy-start | bytes 7077892
  161.0 6.6 %copy-start.13 = (f32[1152,512]{1,0:T(8,128)S(1)}, f32[1152,512]{1,0:T(8,128)}, u32[]{:S(2)}) copy-start(f32[1152,512]{1,0:T(8,128)} %fusion.29) | copy-start | bytes 7077892
  163.0 10.1 %copy-start.1 = (bf16[4,288,2048]{2,1,0:T(8,128)(2,1)}, bf16[4,288,2048]{2,1,0:T(8,128)(2,1)S(1)}, u32[]{:S(2)}) copy-start(bf16[4,288,2048]{2,1,0:T(8,128)(2,1)S(1)} %get-tuple-element.12) | copy-start | bytes 14155780
  163.0 29.4 %collective-permute-start = (bf16[288,2048]{1,0:T(8,128)(2,1)}, bf16[288,2048]{1,0:T(8,128)(2,1)}, u32[]{:S(2)}, u32[]{:S(2)}) collective-permute-start(bf16[288,2048]{1,0:T(8,128)(2,1)} %get-tuple-element.11), channel_id=1, source_target_pairs={{0,1},{1,2},{2,3},{3,0},{4,5},{5,6},{6,7},{7,4},{8,9},{9,10},{10,1... | collective-permute-start | bytes 3538952 | tf_op jit(solution)/shard_map/ppermute | solution.py:66
  164.5 75.5 %collective-permute-start.1 = (bf16[288,2048]{1,0:T(8,128)(2,1)}, bf16[288,2048]{1,0:T(8,128)(2,1)}, u32[]{:S(2)}, u32[]{:S(2)}) collective-permute-start(bf16[288,2048]{1,0:T(8,128)(2,1)} %get-tuple-element.10), channel_id=1, source_target_pairs={{0,2},{1,3},{2,0},{3,1},{4,6},{5,7},{6,4},{7,5},{8,10},{9,11},{10,... | collective-permute-start | bytes 3538952 | tf_op jit(solution)/shard_map/ppermute | solution.py:66
  175.2 67.2 %collective-permute-start.2 = (bf16[288,2048]{1,0:T(8,128)(2,1)}, bf16[288,2048]{1,0:T(8,128)(2,1)}, u32[]{:S(2)}, u32[]{:S(2)}) collective-permute-start(bf16[288,2048]{1,0:T(8,128)(2,1)} %get-tuple-element.9), channel_id=1, source_target_pairs={{0,3},{1,0},{2,1},{3,2},{4,7},{5,4},{6,5},{7,6},{8,11},{9,8},{10,9... | collective-permute-start | bytes 3538952 | tf_op jit(solution)/shard_map/ppermute | solution.py:66
  182.9 124.8 %all-to-all-start.2 = ((bf16[32,36,2048]{2,1,0:T(8,128)(2,1)}), bf16[32,36,2048]{2,1,0:T(8,128)(2,1)}, u32[]{:S(2)}, u32[]{:S(2)}) async-start(bf16[32,36,2048]{2,1,0:T(8,128)(2,1)} %convolution_convert_fusion), calls=%async_computation.3 | async-start | bytes 10485760 | tf_op jit(solution)/shard_map/all_to_all | solution.py:124
  190.0 128.8 %reduce-scatter.2.cloned.1.call-start = ((), (), s32[]{:S(2)}) async-start(), calls=%async_computation.7 | async-start | bytes 4718592 | tf_op jit(solution)/shard_map/reduce_scatter | solution.py:135
  192.4 52.5 %copy-start.14 = (f32[1152,512]{1,0:T(8,128)S(1)}, f32[1152,512]{1,0:T(8,128)}, u32[]{:S(2)}) copy-start(f32[1152,512]{1,0:T(8,128)} %get-tuple-element.26) | copy-start | bytes 7077892
  195.0 49.9 %copy-start.9 = (f32[1152,512]{1,0:T(8,128)S(1)}, f32[1152,512]{1,0:T(8,128)}, u32[]{:S(2)}) copy-start(f32[1152,512]{1,0:T(8,128)} %convolution_add_fusion) | copy-start | bytes 7077892
  195.0 49.9 %copy-start.11 = (f32[1152,512]{1,0:T(8,128)S(1)}, f32[1152,512]{1,0:T(8,128)}, u32[]{:S(2)}) copy-start(f32[1152,512]{1,0:T(8,128)} %convolution_add_fusion.1) | copy-start | bytes 7077892
  259.9 0.7 copy-start.3
  259.9 0.8 copy-start.2
Sparse Core Ops, SparseCore 0:
  12.6 43.7 all-gather.3
  58.7 39.9 all-gather.5
  100.5 52.0 all-gather.7
  260.1 52.9 reduce-scatter.1

commit v6 on v4

--- a/solution.py
+++ b/solution.py
@@ -13,10 +13,12 @@
     return (first, second)
 
 
-def forward_part(rows_flat, gate_e, up_e, down_e, tangent_e, blocks):
-    gate_act = jnp.dot(rows_flat, gate_e, preferred_element_type=jnp.float32)
-    up_act = jnp.dot(rows_flat, up_e, preferred_element_type=jnp.float32)
-    gate_dot = jnp.dot(rows_flat, tangent_e, preferred_element_type=jnp.float32)
+def forward_part(rows_flat, joined_e, down_e, blocks):
+    hidden = down_e.shape[0]
+    acts = jnp.dot(rows_flat, joined_e, preferred_element_type=jnp.float32)
+    gate_act = acts[:, :hidden]
+    up_act = acts[:, hidden : 2 * hidden]
+    gate_dot = acts[:, 2 * hidden :]
     first, second = silu_derivs(gate_act)
     lifted = (first * gate_dot * up_act).astype(jnp.bfloat16)
     term = lax.dot_general(
@@ -107,7 +109,8 @@
     down_e = w_down[0]
     tangent_e = tangent_gate[0]
     send_scaled = (src_w.reshape(-1)[:, None] * select_rows(at_cot, cot_g)).astype(jnp.bfloat16)
-    term, factor = forward_part(rows_flat, gate_e, up_e, down_e, tangent_e, (expert_count, capacity))
+    joined_e = jnp.concatenate([gate_e, up_e, tangent_e], axis=1)
+    term, factor = forward_part(rows_flat, joined_e, down_e, (expert_count, capacity))
     returned = lax.all_to_all(term, ("ey", "ez"), split_axis=0, concat_axis=0, tiled=True)
     _, send_scaled = lax.optimization_barrier((rows_flat, send_scaled))
     scaled_flat = shift_along_y(send_scaled, n_y)
@@ -118,15 +121,16 @@
     hvp_gate = lax.psum_scatter(partial_hvp, "dp", scatter_dimension=0, tiled=True)
     back_at = ((expert_ids % n_y) * n_z + expert_ids // n_y) * capacity + slot_pos
     at_slot = back_at[:, :, None] == jnp.arange(slots, dtype=jnp.int32)[None, None, :]
-    output_tangent = jnp.zeros((rows_dev, model_width), jnp.float32)
-    for piece in split3(combine):
-        spread = jnp.sum(jnp.where(at_slot, piece[:, :, None], 0.0), axis=1).astype(jnp.bfloat16)
-        output_tangent = output_tangent + lax.dot_general(
-            spread.reshape(rows_dev, expert_count, capacity),
-            returned,
-            (((1, 2), (0, 1)), ((), ())),
-            preferred_element_type=jnp.float32,
-        )
+    spread = jnp.concatenate(
+        [jnp.sum(jnp.where(at_slot, piece[:, :, None], 0.0), axis=1) for piece in split3(combine)], axis=0
+    ).astype(jnp.bfloat16)
+    by_piece = lax.dot_general(
+        spread.reshape(3 * rows_dev, expert_count, capacity),
+        returned,
+        (((1, 2), (0, 1)), ((), ())),
+        preferred_element_type=jnp.float32,
+    ).reshape(3, rows_dev, model_width)
+    output_tangent = (by_piece[0] + by_piece[1]) + by_piece[2]
     return (hvp_gate[None], output_tangent.astype(jnp.bfloat16))
 
 

time: 321 us -> 312 us (0.972)
  matrix products: 67.4 us -> 54.5 us
    dot_general x6 -> x2, matrix products: 29.1 us -> 14.9 us  [the longest x1 9.92 us: forward_part(): acts = jnp.dot(rows_flat, joined_e, preferred_element_type=jnp.float32)]
    all_to_all x1, waiting for transfers between devices: 58.4 us -> 54.1 us  [per_device(): lax.all_to_all(term, ('ey', 'ez'), split_axis=0, concat_axis=0, tiled=True)]
    ppermute x3, waiting for transfers between devices: 27.8 us -> 32 us  [shift_along_y(): lax.ppermute(out, 'ey', perm=[(i, (i + shift) % n_y) for i in range(n_y)])]
    unnamed x22, local copies, waits for them, and re-layouts: 3.82 us -> 7.32 us
  transfers between devices with their start and end apart: 8 -> 8, of which waited for: 7 -> 7; matrix products, arithmetic and copies ran while one was open for 27% -> 24% of each run, Pallas kernels for 0% -> 0%
where the time goes in v6:
time: 312 us
  waiting for transfers between devices  192 us (62%)
  matrix products  54.5 us (17%)
  local copies, waits for them, and re-layouts  23.5 us (8%)
  starting transfers between devices  17.2 us (6%)
  between operations  14 us (4%)
  other arithmetic  10.9 us (3%)
    all_gather x1, waiting for transfers between devices, per_device(): tok_g = lax.all_gather(packed, 'ez', axis=0, tiled=True)  59.6 us
    all_to_all x1, waiting for transfers between devices, per_device(): lax.all_to_all(term, ('ey', 'ez'), split_axis=0, concat_axis=0, tiled=True)  54.1 us
    all_gather x1, waiting for transfers between devices, per_device(): cot_g = lax.all_gather(cotangent, 'ez', axis=0, tiled=True)  37.5 us
    ppermute x3, waiting for transfers between devices, shift_along_y(): lax.ppermute(out, 'ey', perm=[(i, (i + shift) % n_y) for i in range(n_y)])  32 us
    dot_general x2, matrix products, select_rows(): return jnp.dot(picks, source, preferred_element_type=jnp.float32)  19.6 us
    dot_general x1, matrix products, per_device(): lax.dot_general(rows_flat, coeff, (((0,), (0,)), ((), ())), preferred_ele...  14.1 us
    dot_general x1, matrix products, forward_part(): acts = jnp.dot(rows_flat, joined_e, preferred_element_type=jnp.float32)  9.92 us
    all_to_all x1, starting transfers between devices, per_device(): lax.all_to_all(term, ('ey', 'ez'), split_axis=0, concat_axis=0, tiled=True)  8.6 us
  transfers between devices with their start and end apart: 8, of which 7 were waited for; matrix products, arithmetic and copies ran while one was open for 24% of the time, Pallas kernels for 0%

profile of v6, /device:TPU:32, one launch (start us, length us, event | category | flops | bytes accessed | tf_op | source)
XLA Modules:
  0.0 311.8 jit_solution(1604940516161903092)
XLA Ops:
  7.2 0.8 convert_reduce_fusion
  8.2 0.2 reduce_window_sum.11
  8.4 0.8 select_reduce_fusion.6
  9.2 0.4 select_reduce_fusion.4
  9.8 0.1 convert_element_type.47
  9.9 1.9 pad_maximum_fusion
  11.9 0.7 all-gather.5.cloned.1.call-update
  13.0 59.6 %all-gather.3.cloned.1.call-done = bf16[1152,2048]{1,0:T(8,128)(2,1)} async-done(((bf16[144,2048]{1,0:T(8,128)(2,1)}), bf16[1152,2048]{1,0:T(8,128)(2,1)}) %all-gather.3.cloned.1.call-update) | async-done | bytes 4718608 | tf_op jit(solution)/shard_map/all_gather | solution.py:91
  72.6 1.1 slice_bitcast_fusion
  73.7 0.3 copy.71
  74.0 0.6 reshape.159
  74.8 10.4 %convolution_convert_fusion = bf16[1152,2048]{1,0:T(8,128)(2,1)} fusion(bf16[1152,2048]{1,0:T(8,128)(2,1)} %all-gather.3.cloned.1.call-done, s32[1152]{0:T(1024)S(1)} %get-tuple-element.19), kind=kOutput, calls=%fused_computation.1 | convolution fusion | flops 5439504384 | bytes 9441792 | tf_op jit(solution)/shard_map/dot_general | solution.py:49
  85.2 5.0 %all-to-all-start = ((bf16[4,288,2048]{2,1,0:T(8,128)(2,1)}), bf16[4,288,2048]{2,1,0:T(8,128)(2,1)}, u32[]{:S(2)}, u32[]{:S(2)}) async-start(bf16[4,288,2048]{2,1,0:T(8,128)(2,1)} %bitcast.63), calls=%async_computation | async-start | bytes 9437184 | tf_op jit(solution)/shard_map/all_to_all | solution.py:106
  90.3 37.5 %all-gather.5.cloned.1.call-done = bf16[1024,2048]{1,0:T(8,128)(2,1)} async-done(((bf16[128,2048]{1,0:T(8,128)(2,1)}), bf16[1024,2048]{1,0:T(8,128)(2,1)}) %all-gather.5.cloned.1.call-update) | async-done | bytes 4194320 | tf_op jit(solution)/shard_map/all_gather | solution.py:92
  127.8 9.2 %fusion = bf16[1152,2048]{1,0:T(8,128)(2,1)} fusion(bf16[1024,2048]{1,0:T(8,128)(2,1)} %all-gather.5.cloned.1.call-done, f32[1152]{0:T(1024)S(1)} %add.159, s32[1152]{0:T(1024)S(1)} %get-tuple-element.18), kind=kOutput, calls=%fused_computation.2 | convolution fusion | flops 4837736448 | bytes 8922112 | tf_op jit(solution)/shard_map/dot_general | solution.py:49
  137.0 7.9 %all-to-all-done = bf16[4,288,2048]{2,1,0:T(8,128)(2,1)} async-done(((bf16[4,288,2048]{2,1,0:T(8,128)(2,1)}), bf16[4,288,2048]{2,1,0:T(8,128)(2,1)}, u32[]{:S(2)}, u32[]{:S(2)}) %all-to-all-start) | async-done | bytes 4718624 | tf_op jit(solution)/shard_map/all_to_all | solution.py:106
  144.9 0.6 broadcast_in_dim.103
  145.5 1.7 copy-done.2
  147.3 2.0 dynamic-slice_bitcast_fusion
  149.3 0.6 collective-permute-start
  149.8 2.1 collective-permute-start.1
  151.9 0.6 collective-permute-start.2
  152.5 0.6 copy-done.9
  153.1 9.9 %fusion.1 = f32[1152,1536]{1,0:T(8,128)S(1)} fusion(bf16[1152,2048]{1,0:T(8,128)(2,1)} %bitcast.5, bf16[2048,512]{1,0:T(8,128)(2,1)S(1)} %bitcast.67, bf16[2048,512]{1,0:T(8,128)(2,1)S(1)} %bitcast.68, bf16[2048,512]{1,0:T(8,128)(2,1)S(1)} %bitcast.69), kind=kOutput, calls=%fused_computation.3 | convolution fusion | flops 7266631680 | bytes 18087936 | tf_op jit(solution)/shard_map/dot_general | solution.py:18
  163.1 2.9 copy-done.1
  166.0 1.0 fusion.16
  167.0 1.2 reshape.162
  168.2 5.9 %convolution_convert_fusion.1 = bf16[32,36,2048]{2,1,0:T(8,128)(2,1)} fusion(bf16[32,36,512]{2,1,0:T(8,128)(2,1)} %reshape.162, bf16[1,512,2048]{2,1,0:T(8,128)(2,1)S(1)} %copy-done), kind=kOutput, calls=%fused_computation.15 | convolution fusion | flops 2418278400 | bytes 7995392 | tf_op jit(solution)/shard_map/dot_general | solution.py:24
  174.1 8.6 %all-to-all-start.1 = ((bf16[32,36,2048]{2,1,0:T(8,128)(2,1)}), bf16[32,36,2048]{2,1,0:T(8,128)(2,1)}, u32[]{:S(2)}, u32[]{:S(2)}) async-start(bf16[32,36,2048]{2,1,0:T(8,128)(2,1)} %convolution_convert_fusion.1), calls=%async_computation.2 | async-start | bytes 10485760 | tf_op jit(solution)/shard_map/all_to_all | solution.py:114
  182.7 0.3 reduce-scatter.2.cloned.1.call-start
  183.0 30.3 %collective-permute-done = bf16[288,2048]{1,0:T(8,128)(2,1)} collective-permute-done((bf16[288,2048]{1,0:T(8,128)(2,1)}, bf16[288,2048]{1,0:T(8,128)(2,1)}, u32[]{:S(2)}, u32[]{:S(2)}) %collective-permute-start) | collective-permute-done | bytes 1179680 | tf_op jit(solution)/shard_map/ppermute | solution.py:59
  213.3 2.4 bitcast_dynamic-update-slice_fusion.2
  215.7 0.6 collective-permute-done.1
  216.3 2.5 bitcast_dynamic-update-slice_fusion.1
  218.8 1.1 collective-permute-done.2
  219.9 2.4 bitcast_dynamic-update-slice_fusion
  222.3 14.1 %fusion.38 = f32[2048,512]{1,0:T(8,128)} fusion(bf16[1152,2048]{1,0:T(8,128)(2,1)} %bitcast.5, bf16[1152,2048]{1,0:T(8,128)(2,1)} %bitcast.64, f32[1152,1536]{1,0:T(8,128)} %copy-done.1, bf16[1,512,2048]{2,1,0:T(8,128)(2,1)S(1)} %copy-done), kind=kOutput, calls=%fused_computation.89 | convolution fusion | flops 4840095744 | bytes 22806528 | tf_op jit(solution)/shard_map/dot_general | solution.py:118
  236.4 0.7 copy-done.5
  237.5 4.7 %select_reduce_fusion.2 = (bf16[128,1152]{1,0:T(8,128)(2,1)S(1)}, bf16[128,1152]{1,0:T(8,128)(2,1)S(1)}, bf16[128,1152]{1,0:T(8,128)(2,1)S(1)}) fusion(f32[128,8]{1,0:T(8,128)S(1)} %copy.64, s32[128,8]{1,0:T(8,128)S(1)} %copy.63, f32[128,8]{1,0:T(8,128)S(1)} %copy.68, f32[128,8]{1,0:T(8,128)S(1)} %copy.66), kind=kLoop, calls=%fused_computation.12 | loop fusion | flops 7815168 | bytes 901120 | tf_op jit(solution)/shard_map/reduce_sum | solution.py:125
  242.2 0.2 copy.65
  242.5 0.8 concatenate.19
  243.2 0.2 copy.67
  243.5 0.8 concatenate.20
  244.2 0.2 copy.69
  244.4 0.8 concatenate.21
  245.2 54.1 %all-to-all-done.1 = bf16[32,36,2048]{2,1,0:T(8,128)(2,1)} async-done(((bf16[32,36,2048]{2,1,0:T(8,128)(2,1)}), bf16[32,36,2048]{2,1,0:T(8,128)(2,1)}, u32[]{:S(2)}, u32[]{:S(2)}) %all-to-all-start.1) | async-done | bytes 4718624 | tf_op jit(solution)/shard_map/all_to_all | solution.py:114
  299.3 5.0 %convolution_bitcast_fusion = f32[384,2048]{1,0:T(8,128)S(1)} fusion(bf16[32,36,2048]{2,1,0:T(8,128)(2,1)} %all-to-all-done.1, bf16[128,32,36]{0,2,1:T(8,128)(2,1)} %concatenate.21, bf16[128,32,36]{0,2,1:T(8,128)(2,1)} %concatenate.20, bf16[128,32,36]{0,2,1:T(8,128)(2,1)S(1)} %copy-done.4), kind=kOutput, calls=%fused_computation.20 | convolution fusion | flops 1814593536 | bytes 8749056 | tf_op jit(solution)/shard_map/dot_general | solution.py:127
  304.3 1.0 fusion.20
  (52 shorter events, 1.6 us)
Async XLA Ops:
  7.2 161.0 %copy-start = (bf16[1,512,2048]{2,1,0:T(8,128)(2,1)S(1)}, bf16[1,512,2048]{2,1,0:T(8,128)(2,1)}, u32[]{:S(2)}) copy-start(bf16[1,512,2048]{2,1,0:T(8,128)(2,1)} %param.14) | copy-start | bytes 6291460
  7.2 65.4 %all-gather.3.cloned.1.call-start = ((), (), s32[]{:S(2)}) async-start(), calls=%async_computation.3 | async-start | bytes 5308416 | tf_op jit(solution)/shard_map/all_gather | solution.py:91
  11.9 115.9 %all-gather.5.cloned.1.call-start = ((), (), s32[]{:S(2)}) async-start(), calls=%async_computation.4 | async-start | bytes 4718592 | tf_op jit(solution)/shard_map/all_gather | solution.py:92
  85.2 59.7 %all-to-all-start = ((bf16[4,288,2048]{2,1,0:T(8,128)(2,1)}), bf16[4,288,2048]{2,1,0:T(8,128)(2,1)}, u32[]{:S(2)}, u32[]{:S(2)}) async-start(bf16[4,288,2048]{2,1,0:T(8,128)(2,1)} %bitcast.63), calls=%async_computation | async-start | bytes 9437184 | tf_op jit(solution)/shard_map/all_to_all | solution.py:106
  144.9 2.3 copy-start.2
  147.3 5.2 %copy-start.7 = (bf16[1,2048,512]{2,1,0:T(8,128)(2,1)S(1)}, bf16[1,2048,512]{2,1,0:T(8,128)(2,1)}, u32[]{:S(2)}) copy-start(bf16[1,2048,512]{2,1,0:T(8,128)(2,1)} %param.15) | copy-start | bytes 6291460
  147.3 5.2 %copy-start.8 = (bf16[1,2048,512]{2,1,0:T(8,128)(2,1)S(1)}, bf16[1,2048,512]{2,1,0:T(8,128)(2,1)}, u32[]{:S(2)}) copy-start(bf16[1,2048,512]{2,1,0:T(8,128)(2,1)} %param.13) | copy-start | bytes 6291460
  147.3 5.8 %copy-start.9 = (bf16[1,2048,512]{2,1,0:T(8,128)(2,1)S(1)}, bf16[1,2048,512]{2,1,0:T(8,128)(2,1)}, u32[]{:S(2)}) copy-start(bf16[1,2048,512]{2,1,0:T(8,128)(2,1)} %param.12) | copy-start | bytes 6291460
  149.3 3.2 %copy-start.3 = (bf16[4,288,2048]{2,1,0:T(8,128)(2,1)}, bf16[4,288,2048]{2,1,0:T(8,128)(2,1)S(1)}, u32[]{:S(2)}) copy-start(bf16[4,288,2048]{2,1,0:T(8,128)(2,1)S(1)} %get-tuple-element.12) | copy-start | bytes 14155780
  149.3 64.0 %collective-permute-start = (bf16[288,2048]{1,0:T(8,128)(2,1)}, bf16[288,2048]{1,0:T(8,128)(2,1)}, u32[]{:S(2)}, u32[]{:S(2)}) collective-permute-start(bf16[288,2048]{1,0:T(8,128)(2,1)} %get-tuple-element.11), channel_id=1, source_target_pairs={{0,1},{1,2},{2,3},{3,0},{4,5},{5,6},{6,7},{7,4},{8,9},{9,10},{10,1... | collective-permute-start | bytes 3538952 | tf_op jit(solution)/shard_map/ppermute | solution.py:59
  149.8 66.5 %collective-permute-start.1 = (bf16[288,2048]{1,0:T(8,128)(2,1)}, bf16[288,2048]{1,0:T(8,128)(2,1)}, u32[]{:S(2)}, u32[]{:S(2)}) collective-permute-start(bf16[288,2048]{1,0:T(8,128)(2,1)} %get-tuple-element.10), channel_id=1, source_target_pairs={{0,2},{1,3},{2,0},{3,1},{4,6},{5,7},{6,4},{7,5},{8,10},{9,11},{10,... | collective-permute-start | bytes 3538952 | tf_op jit(solution)/shard_map/ppermute | solution.py:59
  151.9 68.0 %collective-permute-start.2 = (bf16[288,2048]{1,0:T(8,128)(2,1)}, bf16[288,2048]{1,0:T(8,128)(2,1)}, u32[]{:S(2)}, u32[]{:S(2)}) collective-permute-start(bf16[288,2048]{1,0:T(8,128)(2,1)} %get-tuple-element.9), channel_id=1, source_target_pairs={{0,3},{1,0},{2,1},{3,2},{4,7},{5,4},{6,5},{7,6},{8,11},{9,8},{10,9... | collective-permute-start | bytes 3538952 | tf_op jit(solution)/shard_map/ppermute | solution.py:59
  163.0 2.9 copy-start.1
  174.1 125.2 %all-to-all-start.1 = ((bf16[32,36,2048]{2,1,0:T(8,128)(2,1)}), bf16[32,36,2048]{2,1,0:T(8,128)(2,1)}, u32[]{:S(2)}, u32[]{:S(2)}) async-start(bf16[32,36,2048]{2,1,0:T(8,128)(2,1)} %convolution_convert_fusion.1), calls=%async_computation.2 | async-start | bytes 10485760 | tf_op jit(solution)/shard_map/all_to_all | solution.py:114
  182.7 122.6 %reduce-scatter.2.cloned.1.call-start = ((), (), s32[]{:S(2)}) async-start(), calls=%async_computation.5 | async-start | bytes 4718592 | tf_op jit(solution)/shard_map/reduce_scatter | solution.py:121
  236.4 0.7 copy-start.5
  236.4 0.8 copy-start.6
  243.2 56.1 %copy-start.4 = (bf16[128,32,36]{0,2,1:T(8,128)(2,1)S(1)}, bf16[128,32,36]{0,2,1:T(8,128)(2,1)}, u32[]{:S(2)}) copy-start(bf16[128,32,36]{0,2,1:T(8,128)(2,1)} %concatenate.19) | copy-start | bytes 884740
Sparse Core Ops, SparseCore 0:
  12.0 60.5 all-gather.2
  74.4 53.4 all-gather.4
  236.5 48.1 reduce-scatter.1

commit v7 on v6

--- a/solution.py
+++ b/solution.py
@@ -53,10 +53,9 @@
     chunks = send.reshape(n_y, -1, send.shape[-1])
     me = lax.axis_index("ey")
     got = jnp.zeros_like(chunks)
-    got = lax.dynamic_update_index_in_dim(got, lax.dynamic_index_in_dim(chunks, me, 0, False), me, 0)
+    got = lax.dynamic_update_index_in_dim(got, chunks[0], me, 0)
     for shift in range(1, n_y):
-        out = lax.dynamic_index_in_dim(chunks, (me + shift) % n_y, 0, False)
-        moved = lax.ppermute(out, "ey", perm=[(i, (i + shift) % n_y) for i in range(n_y)])
+        moved = lax.ppermute(chunks[shift], "ey", perm=[(i, (i + shift) % n_y) for i in range(n_y)])
         got = lax.dynamic_update_index_in_dim(got, moved, (me + n_y - shift) % n_y, 0)
     return got.reshape(send.shape)
 
@@ -108,7 +107,10 @@
     up_e = w_up[0]
     down_e = w_down[0]
     tangent_e = tangent_gate[0]
-    send_scaled = (src_w.reshape(-1)[:, None] * select_rows(at_cot, cot_g)).astype(jnp.bfloat16)
+    rolled = (lax.axis_index("ey") + jnp.arange(n_y, dtype=jnp.int32)) % n_y
+    at_rolled = jnp.take(at_cot.reshape(n_y, -1), rolled, axis=0).reshape(-1)
+    w_rolled = jnp.take(src_w.reshape(n_y, -1), rolled, axis=0).reshape(-1)
+    send_scaled = (w_rolled[:, None] * select_rows(at_rolled, cot_g)).astype(jnp.bfloat16)
     joined_e = jnp.concatenate([gate_e, up_e, tangent_e], axis=1)
     term, factor = forward_part(rows_flat, joined_e, down_e, (expert_count, capacity))
     returned = lax.all_to_all(term, ("ey", "ez"), split_axis=0, concat_axis=0, tiled=True)

time: 312 us -> 312 us (level)
  waiting for transfers between devices: 192 us -> 185 us
  local copies, waits for them, and re-layouts: 23.5 us -> 29.2 us
    ppermute x3, waiting for transfers between devices: 32 us -> 26.7 us  [shift_along_y(): lax.ppermute(chunks[shift], 'ey', perm=[(i, (i + shift) % n_y) for i in r...]
    slice x0 -> x1, local copies, waits for them, and re-layouts: none -> 4.07 us  [shift_along_y(): chunks[shift]]
    unnamed x22 -> x18, local copies, waits for them, and re-layouts: 7.32 us -> 4.96 us
  transfers between devices with their start and end apart: 8 -> 8, of which waited for: 7 -> 7; matrix products, arithmetic and copies ran while one was open for 24% -> 26% of each run, Pallas kernels for 0% -> 0%
where the time goes in v7:
time: 312 us
  waiting for transfers between devices  185 us (59%)
  matrix products  54.4 us (17%)
  local copies, waits for them, and re-layouts  29.2 us (9%)
  starting transfers between devices  17.7 us (6%)
  between operations  14 us (4%)
  other arithmetic  11.1 us (4%)
    all_gather x1, waiting for transfers between devices, per_device(): tok_g = lax.all_gather(packed, 'ez', axis=0, tiled=True)  59.8 us
    all_to_all x1, waiting for transfers between devices, per_device(): lax.all_to_all(term, ('ey', 'ez'), split_axis=0, concat_axis=0, tiled=True)  54.2 us
    all_gather x1, waiting for transfers between devices, per_device(): cot_g = lax.all_gather(cotangent, 'ez', axis=0, tiled=True)  35.8 us
    ppermute x3, waiting for transfers between devices, shift_along_y(): lax.ppermute(chunks[shift], 'ey', perm=[(i, (i + shift) % n_y) for i in r...  26.7 us
    dot_general x2, matrix products, select_rows(): return jnp.dot(picks, source, preferred_element_type=jnp.float32)  19.6 us
    dot_general x1, matrix products, per_device(): lax.dot_general(rows_flat, coeff, (((0,), (0,)), ((), ())), preferred_ele...  14 us
    dot_general x1, matrix products, forward_part(): acts = jnp.dot(rows_flat, joined_e, preferred_element_type=jnp.float32)  9.92 us
    all_to_all x1, starting transfers between devices, per_device(): lax.all_to_all(term, ('ey', 'ez'), split_axis=0, concat_axis=0, tiled=True)  9.2 us
  transfers between devices with their start and end apart: 8, of which 7 were waited for; matrix products, arithmetic and copies ran while one was open for 26% of the time, Pallas kernels for 0%

profile of v7, /device:TPU:32, one launch (start us, length us, event | category | flops | bytes accessed | tf_op | source)
XLA Modules:
  0.0 311.6 jit_solution(2884344649521418942)
XLA Ops:
  7.2 0.8 convert_reduce_fusion
  8.2 0.2 reduce_window_sum.11
  8.4 0.7 select_reduce_fusion.6
  9.2 0.4 select_reduce_fusion.4
  9.9 1.9 pad_maximum_fusion
  11.9 0.7 all-gather.5.cloned.1.call-update
  12.8 59.8 %all-gather.3.cloned.1.call-done = bf16[1152,2048]{1,0:T(8,128)(2,1)} async-done(((bf16[144,2048]{1,0:T(8,128)(2,1)}), bf16[1152,2048]{1,0:T(8,128)(2,1)}) %all-gather.3.cloned.1.call-update) | async-done | bytes 4718608 | tf_op jit(solution)/shard_map/all_gather | solution.py:90
  72.6 1.1 slice_bitcast_fusion
  73.6 0.3 copy.76
  74.0 0.6 reshape.226
  74.8 10.4 %convolution_convert_fusion = bf16[1152,2048]{1,0:T(8,128)(2,1)} fusion(bf16[1152,2048]{1,0:T(8,128)(2,1)} %all-gather.3.cloned.1.call-done, s32[1152]{0:T(1024)S(1)} %add_select_fusion), kind=kOutput, calls=%fused_computation.3 | convolution fusion | flops 5439504384 | bytes 9441792 | tf_op jit(solution)/shard_map/dot_general | solution.py:49
  85.2 5.0 %all-to-all-start = ((bf16[4,288,2048]{2,1,0:T(8,128)(2,1)}), bf16[4,288,2048]{2,1,0:T(8,128)(2,1)}, u32[]{:S(2)}, u32[]{:S(2)}) async-start(bf16[4,288,2048]{2,1,0:T(8,128)(2,1)} %bitcast.61), calls=%async_computation | async-start | bytes 9437184 | tf_op jit(solution)/shard_map/all_to_all | solution.py:105
  90.6 0.6 gather_fusion
  91.3 0.6 gather_fusion.1
  92.0 35.8 %all-gather.5.cloned.1.call-done = bf16[1024,2048]{1,0:T(8,128)(2,1)} async-done(((bf16[128,2048]{1,0:T(8,128)(2,1)}), bf16[1024,2048]{1,0:T(8,128)(2,1)}) %all-gather.5.cloned.1.call-update) | async-done | bytes 4194320 | tf_op jit(solution)/shard_map/all_gather | solution.py:91
  127.8 9.2 %fusion = bf16[1152,2048]{1,0:T(8,128)(2,1)} fusion(bf16[1024,2048]{1,0:T(8,128)(2,1)} %all-gather.5.cloned.1.call-done, f32[1152]{0:T(1024)S(1)} %select_n.143, s32[1152]{0:T(1024)S(1)} %select_n.146), kind=kOutput, calls=%fused_computation.4 | convolution fusion | flops 4837736448 | bytes 8922112 | tf_op jit(solution)/shard_map/dot_general | solution.py:49
  137.0 7.9 %all-to-all-done = bf16[4,288,2048]{2,1,0:T(8,128)(2,1)} async-done(((bf16[4,288,2048]{2,1,0:T(8,128)(2,1)}), bf16[4,288,2048]{2,1,0:T(8,128)(2,1)}, u32[]{:S(2)}, u32[]{:S(2)}) %all-to-all-start) | async-done | bytes 4718624 | tf_op jit(solution)/shard_map/all_to_all | solution.py:105
  144.9 4.1 %fusion.47 = (bf16[288,2048]{1,0:T(8,128)(2,1)}, bf16[288,2048]{1,0:T(8,128)(2,1)}, bf16[288,2048]{1,0:T(8,128)(2,1)}) fusion(bf16[1152,2048]{1,0:T(8,128)(2,1)} %fusion), kind=kLoop, calls=%fused_computation.113 | loop fusion | bytes 7077888 | tf_op jit(solution)/shard_map/slice | solution.py:58
  149.0 0.6 collective-permute-start
  149.5 2.1 collective-permute-start.1
  151.6 0.6 collective-permute-start.2
  152.2 9.9 %fusion.1 = f32[1152,1536]{1,0:T(8,128)S(1)} fusion(bf16[1152,2048]{1,0:T(8,128)(2,1)} %bitcast.5, bf16[2048,512]{1,0:T(8,128)(2,1)S(1)} %bitcast.64, bf16[2048,512]{1,0:T(8,128)(2,1)S(1)} %bitcast.65, bf16[2048,512]{1,0:T(8,128)(2,1)S(1)} %bitcast.66), kind=kOutput, calls=%fused_computation.5 | convolution fusion | flops 7266631680 | bytes 18087936 | tf_op jit(solution)/shard_map/dot_general | solution.py:18
  162.2 2.9 copy-done.1
  165.1 1.0 fusion.16
  166.1 1.3 reshape.228
  167.4 5.9 %convolution_convert_fusion.1 = bf16[32,36,2048]{2,1,0:T(8,128)(2,1)} fusion(bf16[32,36,512]{2,1,0:T(8,128)(2,1)} %reshape.228, bf16[1,512,2048]{2,1,0:T(8,128)(2,1)S(1)} %copy-done), kind=kOutput, calls=%fused_computation.17 | convolution fusion | flops 2418278400 | bytes 7995392 | tf_op jit(solution)/shard_map/dot_general | solution.py:24
  173.3 9.2 %all-to-all-start.1 = ((bf16[32,36,2048]{2,1,0:T(8,128)(2,1)}), bf16[32,36,2048]{2,1,0:T(8,128)(2,1)}, u32[]{:S(2)}, u32[]{:S(2)}) async-start(bf16[32,36,2048]{2,1,0:T(8,128)(2,1)} %convolution_convert_fusion.1), calls=%async_computation.2 | async-start | bytes 10485760 | tf_op jit(solution)/shard_map/all_to_all | solution.py:116
  182.5 0.3 reduce-scatter.2.cloned.1.call-start
  182.8 2.8 broadcast_in_dim.123
  185.6 2.4 bitcast_dynamic-update-slice_fusion.3
  188.0 25.0 %collective-permute-done = bf16[288,2048]{1,0:T(8,128)(2,1)} collective-permute-done((bf16[288,2048]{1,0:T(8,128)(2,1)}, bf16[288,2048]{1,0:T(8,128)(2,1)}, u32[]{:S(2)}, u32[]{:S(2)}) %collective-permute-start) | collective-permute-done | bytes 1179680 | tf_op jit(solution)/shard_map/ppermute | solution.py:58
  213.0 2.4 bitcast_dynamic-update-slice_fusion.2
  215.4 0.5 collective-permute-done.1
  215.9 2.5 bitcast_dynamic-update-slice_fusion.1
  218.4 1.2 collective-permute-done.2
  219.6 2.4 bitcast_dynamic-update-slice_fusion
  222.0 14.0 %fusion.38 = f32[2048,512]{1,0:T(8,128)} fusion(bf16[1152,2048]{1,0:T(8,128)(2,1)} %bitcast.5, bf16[1152,2048]{1,0:T(8,128)(2,1)} %bitcast.11, f32[1152,1536]{1,0:T(8,128)} %copy-done.1, bf16[1,512,2048]{2,1,0:T(8,128)(2,1)S(1)} %copy-done), kind=kOutput, calls=%fused_computation.92 | convolution fusion | flops 4840095744 | bytes 22806528 | tf_op jit(solution)/shard_map/dot_general | solution.py:120
  236.1 0.7 copy-done.4
  237.2 4.7 %select_reduce_fusion.2 = (bf16[128,1152]{1,0:T(8,128)(2,1)S(1)}, bf16[128,1152]{1,0:T(8,128)(2,1)S(1)}, bf16[128,1152]{1,0:T(8,128)(2,1)S(1)}) fusion(f32[128,8]{1,0:T(8,128)S(1)} %copy.69, s32[128,8]{1,0:T(8,128)S(1)} %copy.68, f32[128,8]{1,0:T(8,128)S(1)} %copy.73, f32[128,8]{1,0:T(8,128)S(1)} %copy.71), kind=kLoop, calls=%fused_computation.14 | loop fusion | flops 7815168 | bytes 901120 | tf_op jit(solution)/shard_map/reduce_sum | solution.py:127
  241.9 0.2 copy.74
  242.1 0.8 concatenate.21
  242.9 0.2 copy.72
  243.1 0.8 concatenate.20
  243.9 0.2 copy.70
  244.1 0.8 concatenate.19
  244.9 54.2 %all-to-all-done.1 = bf16[32,36,2048]{2,1,0:T(8,128)(2,1)} async-done(((bf16[32,36,2048]{2,1,0:T(8,128)(2,1)}), bf16[32,36,2048]{2,1,0:T(8,128)(2,1)}, u32[]{:S(2)}, u32[]{:S(2)}) %all-to-all-start.1) | async-done | bytes 4718624 | tf_op jit(solution)/shard_map/all_to_all | solution.py:116
  299.1 5.0 %convolution_bitcast_fusion = f32[384,2048]{1,0:T(8,128)S(1)} fusion(bf16[32,36,2048]{2,1,0:T(8,128)(2,1)} %all-to-all-done.1, bf16[128,32,36]{0,2,1:T(8,128)(2,1)S(1)} %copy-done.2, bf16[128,32,36]{0,2,1:T(8,128)(2,1)} %concatenate.20, bf16[128,32,36]{0,2,1:T(8,128)(2,1)} %concatenate.19), kind=kOutput, calls=%fused_computation.22 | convolution fusion | flops 1814593536 | bytes 8749056 | tf_op jit(solution)/shard_map/dot_general | solution.py:129
  304.1 1.0 fusion.20
  (60 shorter events, 2.1 us)
Async XLA Ops:
  7.2 160.2 %copy-start = (bf16[1,512,2048]{2,1,0:T(8,128)(2,1)S(1)}, bf16[1,512,2048]{2,1,0:T(8,128)(2,1)}, u32[]{:S(2)}) copy-start(bf16[1,512,2048]{2,1,0:T(8,128)(2,1)} %param.14) | copy-start | bytes 6291460
  7.2 65.4 %all-gather.3.cloned.1.call-start = ((), (), s32[]{:S(2)}) async-start(), calls=%async_computation.3 | async-start | bytes 5308416 | tf_op jit(solution)/shard_map/all_gather | solution.py:90
  11.9 115.9 %all-gather.5.cloned.1.call-start = ((), (), s32[]{:S(2)}) async-start(), calls=%async_computation.4 | async-start | bytes 4718592 | tf_op jit(solution)/shard_map/all_gather | solution.py:91
  85.2 59.7 %all-to-all-start = ((bf16[4,288,2048]{2,1,0:T(8,128)(2,1)}), bf16[4,288,2048]{2,1,0:T(8,128)(2,1)}, u32[]{:S(2)}, u32[]{:S(2)}) async-start(bf16[4,288,2048]{2,1,0:T(8,128)(2,1)} %bitcast.61), calls=%async_computation | async-start | bytes 9437184 | tf_op jit(solution)/shard_map/all_to_all | solution.py:105
  144.9 7.3 %copy-start.5 = (bf16[1,2048,512]{2,1,0:T(8,128)(2,1)S(1)}, bf16[1,2048,512]{2,1,0:T(8,128)(2,1)}, u32[]{:S(2)}) copy-start(bf16[1,2048,512]{2,1,0:T(8,128)(2,1)} %param.15) | copy-start | bytes 6291460
  144.9 7.3 %copy-start.6 = (bf16[1,2048,512]{2,1,0:T(8,128)(2,1)S(1)}, bf16[1,2048,512]{2,1,0:T(8,128)(2,1)}, u32[]{:S(2)}) copy-start(bf16[1,2048,512]{2,1,0:T(8,128)(2,1)} %param.13) | copy-start | bytes 6291460
  144.9 7.3 %copy-start.7 = (bf16[1,2048,512]{2,1,0:T(8,128)(2,1)S(1)}, bf16[1,2048,512]{2,1,0:T(8,128)(2,1)}, u32[]{:S(2)}) copy-start(bf16[1,2048,512]{2,1,0:T(8,128)(2,1)} %param.12) | copy-start | bytes 6291460
  149.0 64.0 %collective-permute-start = (bf16[288,2048]{1,0:T(8,128)(2,1)}, bf16[288,2048]{1,0:T(8,128)(2,1)}, u32[]{:S(2)}, u32[]{:S(2)}) collective-permute-start(bf16[288,2048]{1,0:T(8,128)(2,1)} %get-tuple-element.11), channel_id=1, source_target_pairs={{0,1},{1,2},{2,3},{3,0},{4,5},{5,6},{6,7},{7,4},{8,9},{9,10},{10,1... | collective-permute-start | bytes 3538952 | tf_op jit(solution)/shard_map/ppermute | solution.py:58
  149.5 66.4 %collective-permute-start.1 = (bf16[288,2048]{1,0:T(8,128)(2,1)}, bf16[288,2048]{1,0:T(8,128)(2,1)}, u32[]{:S(2)}, u32[]{:S(2)}) collective-permute-start(bf16[288,2048]{1,0:T(8,128)(2,1)} %get-tuple-element.10), channel_id=1, source_target_pairs={{0,2},{1,3},{2,0},{3,1},{4,6},{5,7},{6,4},{7,5},{8,10},{9,11},{10,... | collective-permute-start | bytes 3538952 | tf_op jit(solution)/shard_map/ppermute | solution.py:58
  151.6 68.0 %collective-permute-start.2 = (bf16[288,2048]{1,0:T(8,128)(2,1)}, bf16[288,2048]{1,0:T(8,128)(2,1)}, u32[]{:S(2)}, u32[]{:S(2)}) collective-permute-start(bf16[288,2048]{1,0:T(8,128)(2,1)} %get-tuple-element.9), channel_id=1, source_target_pairs={{0,3},{1,0},{2,1},{3,2},{4,7},{5,4},{6,5},{7,6},{8,11},{9,8},{10,9... | collective-permute-start | bytes 3538952 | tf_op jit(solution)/shard_map/ppermute | solution.py:58
  162.2 2.9 copy-start.1
  173.3 125.8 %all-to-all-start.1 = ((bf16[32,36,2048]{2,1,0:T(8,128)(2,1)}), bf16[32,36,2048]{2,1,0:T(8,128)(2,1)}, u32[]{:S(2)}, u32[]{:S(2)}) async-start(bf16[32,36,2048]{2,1,0:T(8,128)(2,1)} %convolution_convert_fusion.1), calls=%async_computation.2 | async-start | bytes 10485760 | tf_op jit(solution)/shard_map/all_to_all | solution.py:116
  182.5 122.6 %reduce-scatter.2.cloned.1.call-start = ((), (), s32[]{:S(2)}) async-start(), calls=%async_computation.5 | async-start | bytes 4718592 | tf_op jit(solution)/shard_map/reduce_scatter | solution.py:123
  236.0 0.7 copy-start.4
  236.0 0.8 copy-start.3
  242.9 56.2 %copy-start.2 = (bf16[128,32,36]{0,2,1:T(8,128)(2,1)S(1)}, bf16[128,32,36]{0,2,1:T(8,128)(2,1)}, u32[]{:S(2)}) copy-start(bf16[128,32,36]{0,2,1:T(8,128)(2,1)} %concatenate.21) | copy-start | bytes 884740
Sparse Core Ops, SparseCore 0:
  12.0 60.5 all-gather.2
  74.3 53.4 all-gather.4
  236.2 48.0 reduce-scatter.1

commit v8 on v7

--- a/solution.py
+++ b/solution.py
@@ -100,14 +100,15 @@
     z_of = jnp.arange(n_z, dtype=jnp.int32)[None, :, None]
     at_packed = jnp.where(valid, src_tok + z_of * block, -1).reshape(-1)
     at_cot = jnp.where(valid, src_tok + z_of * rows_dev, -1).reshape(-1)
-    send_rows = select_rows(at_packed, tok_g).astype(jnp.bfloat16)
+    rolled = (lax.axis_index("ey") + jnp.arange(n_y, dtype=jnp.int32)) % n_y
+    send_rows = select_rows(jnp.take(at_packed.reshape(n_y, -1), rolled, axis=0).reshape(-1), tok_g)
+    send_rows = send_rows.astype(jnp.bfloat16)
 
-    rows_flat = lax.all_to_all(send_rows, "ey", split_axis=0, concat_axis=0, tiled=True)
+    rows_flat = shift_along_y(send_rows, n_y)
     gate_e = w_gate[0]
     up_e = w_up[0]
     down_e = w_down[0]
     tangent_e = tangent_gate[0]
-    rolled = (lax.axis_index("ey") + jnp.arange(n_y, dtype=jnp.int32)) % n_y
     at_rolled = jnp.take(at_cot.reshape(n_y, -1), rolled, axis=0).reshape(-1)
     w_rolled = jnp.take(src_w.reshape(n_y, -1), rolled, axis=0).reshape(-1)
     send_scaled = (w_rolled[:, None] * select_rows(at_rolled, cot_g)).astype(jnp.bfloat16)

time: 312 us -> 315 us (level)
  local copies, waits for them, and re-layouts: 29.2 us -> 37.6 us
  matrix products: 54.4 us -> 49.3 us
    all_to_all x1 -> x0, waiting for transfers between devices: 7.89 us -> none  [per_device(): lax.all_to_all(send_rows, 'ey', split_axis=0, concat_axis=0, tiled=True)]
    ppermute x3 -> x6, starting transfers between devices: 3.24 us -> 9.52 us  [shift_along_y(): lax.ppermute(chunks[shift], 'ey', perm=[(i, (i + shift) % n_y) for i in r...]
    ppermute x3 -> x6, waiting for transfers between devices: 26.7 us -> 32.6 us  [shift_along_y(): lax.ppermute(chunks[shift], 'ey', perm=[(i, (i + shift) % n_y) for i in r...]
    all_to_all x1 -> x0, starting transfers between devices: 4.96 us -> none  [per_device(): lax.all_to_all(send_rows, 'ey', split_axis=0, concat_axis=0, tiled=True)]
    dynamic_update_slice x3 -> x6, local copies, waits for them, and re-layouts: 7.29 us -> 11.5 us  [shift_along_y(): lax.dynamic_update_index_in_dim(got, moved, (me + n_y - shift) % n_y, 0)]
    another operation x3 -> x5, local copies, waits for them, and re-layouts: 0.63 us -> 3.98 us
  transfers between devices with their start and end apart: 8 -> 10, of which waited for: 7 -> 6; matrix products, arithmetic and copies ran while one was open for 26% -> 27% of each run, Pallas kernels for 0% -> 0%
where the time goes in v8:
time: 315 us; the launch traced here: 314 us
  waiting for transfers between devices  183 us (58%)
  matrix products  49.3 us (16%)
  local copies, waits for them, and re-layouts  37.6 us (12%)
  starting transfers between devices  18.4 us (6%)
  between operations  14.2 us (5%)
  other arithmetic  11.2 us (4%)
    all_gather x1, waiting for transfers between devices, per_device(): tok_g = lax.all_gather(packed, 'ez', axis=0, tiled=True)  59.5 us
    all_to_all x1, waiting for transfers between devices, per_device(): lax.all_to_all(term, ('ey', 'ez'), split_axis=0, concat_axis=0, tiled=True)  57.1 us
    all_gather x1, waiting for transfers between devices, per_device(): cot_g = lax.all_gather(cotangent, 'ez', axis=0, tiled=True)  33.3 us
    ppermute x6, waiting for transfers between devices, shift_along_y(): lax.ppermute(chunks[shift], 'ey', perm=[(i, (i + shift) % n_y) for i in r...  32.6 us
    dot_general x2, matrix products, select_rows(): return jnp.dot(picks, source, preferred_element_type=jnp.float32)  16.7 us
    dot_general x1, matrix products, per_device(): lax.dot_general(rows_flat, coeff, (((0,), (0,)), ((), ())), preferred_ele...  14.1 us
    dynamic_update_slice x6, local copies, waits for them, and re-layouts, shift_along_y(): lax.dynamic_update_index_in_dim(got, moved, (me + n_y - shift) % n_y, 0)  11.5 us
    ppermute x6, starting transfers between devices, shift_along_y(): lax.ppermute(chunks[shift], 'ey', perm=[(i, (i + shift) % n_y) for i in r...  9.52 us
  transfers between devices with their start and end apart: 10, of which 6 were waited for; matrix products, arithmetic and copies ran while one was open for 27% of the time, Pallas kernels for 0%

profile of v8, /device:TPU:32, one launch (start us, length us, event | category | flops | bytes accessed | tf_op | source)
XLA Modules:
  0.0 313.9 jit_solution(5317456555672792408)
XLA Ops:
  7.2 0.8 convert_reduce_fusion
  8.4 0.7 select_reduce_fusion.6
  9.9 2.0 pad_maximum_fusion
  12.0 0.7 all-gather.5.cloned.1.call-update
  13.1 59.5 %all-gather.3.cloned.1.call-done = bf16[1152,2048]{1,0:T(8,128)(2,1)} async-done(((bf16[144,2048]{1,0:T(8,128)(2,1)}), bf16[1152,2048]{1,0:T(8,128)(2,1)}) %all-gather.3.cloned.1.call-update) | async-done | bytes 4718608 | tf_op jit(solution)/shard_map/all_gather | solution.py:90
  72.7 1.1 slice_bitcast_fusion.1
  74.0 0.6 reshape.216
  74.9 0.6 gather_fusion.2
  76.1 9.0 %convolution_convert_fusion = bf16[1152,2048]{1,0:T(8,128)(2,1)S(1)} fusion(bf16[1152,2048]{1,0:T(8,128)(2,1)} %all-gather.3.cloned.1.call-done, s32[1152]{0:T(1024)S(1)} %eq.86), kind=kOutput, calls=%fused_computation.4 | convolution fusion | flops 5439504384 | bytes 9441792 | tf_op jit(solution)/shard_map/dot_general | solution.py:49
  85.1 2.0 fusion.49
  87.1 0.9 copy-done.3
  88.1 1.5 collective-permute-start
  89.5 2.7 collective-permute-start.1
  92.3 1.4 collective-permute-start.2
  93.8 0.6 gather_fusion
  94.6 33.3 %all-gather.5.cloned.1.call-done = bf16[1024,2048]{1,0:T(8,128)(2,1)} async-done(((bf16[128,2048]{1,0:T(8,128)(2,1)}), bf16[1024,2048]{1,0:T(8,128)(2,1)}) %all-gather.5.cloned.1.call-update) | async-done | bytes 4194320 | tf_op jit(solution)/shard_map/all_gather | solution.py:91
  127.9 7.8 %fusion = bf16[1152,2048]{1,0:T(8,128)(2,1)S(1)} fusion(bf16[1024,2048]{1,0:T(8,128)(2,1)} %all-gather.5.cloned.1.call-done, f32[1152]{0:T(1024)S(1)} %select_n.150, s32[1152]{0:T(1024)S(1)} %eq.90), kind=kOutput, calls=%fused_computation.5 | convolution fusion | flops 4837736448 | bytes 8922112 | tf_op jit(solution)/shard_map/dot_general | solution.py:49
  135.7 0.6 broadcast.197.clone
  136.3 2.3 fusion.20
  138.6 1.4 bitcast_dynamic-update-slice_fusion.6
  140.0 3.5 %collective-permute-done.1 = bf16[288,2048]{1,0:T(8,128)(2,1)} collective-permute-done((bf16[288,2048]{1,0:T(8,128)(2,1)}, bf16[288,2048]{1,0:T(8,128)(2,1)}, u32[]{:S(2)}, u32[]{:S(2)}) %collective-permute-start.1) | collective-permute-done | bytes 1179680 | tf_op jit(solution)/shard_map/ppermute | solution.py:58
  143.5 1.4 bitcast_dynamic-update-slice_fusion.5
  145.0 1.4 bitcast_dynamic-update-slice_fusion.4
  146.4 1.9 fusion.48
  148.3 2.3 collective-permute-start.4
  150.6 1.6 collective-permute-start.5
  152.2 7.5 %fusion.1 = f32[1152,1536]{1,0:T(8,128)S(1)} fusion(bf16[1152,2048]{1,0:T(8,128)(2,1)S(1)} %bitcast.68, bf16[2048,512]{1,0:T(8,128)(2,1)S(1)} %bitcast.72, bf16[2048,512]{1,0:T(8,128)(2,1)S(1)} %bitcast.73, bf16[2048,512]{1,0:T(8,128)(2,1)S(1)} %bitcast.74), kind=kOutput, calls=%fused_computation.6 | convolution fusion | flops 7266631680 | bytes 18087936 | tf_op jit(solution)/shard_map/dot_general | solution.py:18
  159.8 2.9 copy-done.1
  162.7 1.0 fusion.16
  163.7 1.2 reshape.219
  164.9 5.9 %convolution_convert_fusion.1 = bf16[32,36,2048]{2,1,0:T(8,128)(2,1)} fusion(bf16[32,36,512]{2,1,0:T(8,128)(2,1)} %reshape.219, bf16[1,512,2048]{2,1,0:T(8,128)(2,1)S(1)} %copy-done), kind=kOutput, calls=%fused_computation.18 | convolution fusion | flops 2418278400 | bytes 7995392 | tf_op jit(solution)/shard_map/dot_general | solution.py:24
  170.9 2.8 broadcast.197
  173.6 2.4 bitcast_dynamic-update-slice_fusion.3
  176.1 8.6 %all-to-all-start = ((bf16[32,36,2048]{2,1,0:T(8,128)(2,1)}), bf16[32,36,2048]{2,1,0:T(8,128)(2,1)}, u32[]{:S(2)}, u32[]{:S(2)}) async-start(bf16[32,36,2048]{2,1,0:T(8,128)(2,1)} %convolution_convert_fusion.1), calls=%async_computation.1 | async-start | bytes 10485760 | tf_op jit(solution)/shard_map/all_to_all | solution.py:117
  185.0 2.4 bitcast_dynamic-update-slice_fusion.2
  187.4 26.4 %collective-permute-done.4 = bf16[288,2048]{1,0:T(8,128)(2,1)} collective-permute-done((bf16[288,2048]{1,0:T(8,128)(2,1)}, bf16[288,2048]{1,0:T(8,128)(2,1)}, u32[]{:S(2)}, u32[]{:S(2)}) %collective-permute-start.4) | collective-permute-done | bytes 1179680 | tf_op jit(solution)/shard_map/ppermute | solution.py:58
  213.8 2.5 bitcast_dynamic-update-slice_fusion.1
  216.3 2.7 collective-permute-done.5
  218.9 2.4 bitcast_dynamic-update-slice_fusion
  221.3 14.1 %fusion.39 = f32[2048,512]{1,0:T(8,128)} fusion(bf16[1152,2048]{1,0:T(8,128)(2,1)} %bitcast.69, bf16[1152,2048]{1,0:T(8,128)(2,1)} %bitcast.14, f32[1152,1536]{1,0:T(8,128)} %copy-done.1, bf16[1,512,2048]{2,1,0:T(8,128)(2,1)S(1)} %copy-done), kind=kOutput, calls=%fused_computation.101 | convolution fusion | flops 4840095744 | bytes 22806528 | tf_op jit(solution)/shard_map/dot_general | solution.py:121
  235.4 0.7 copy-done.7
  236.6 4.7 %select_reduce_fusion.2 = (bf16[128,1152]{1,0:T(8,128)(2,1)S(1)}, bf16[128,1152]{1,0:T(8,128)(2,1)S(1)}, bf16[128,1152]{1,0:T(8,128)(2,1)S(1)}) fusion(f32[128,8]{1,0:T(8,128)S(1)} %copy.58, s32[128,8]{1,0:T(8,128)S(1)} %copy.57, f32[128,8]{1,0:T(8,128)S(1)} %copy.62, f32[128,8]{1,0:T(8,128)S(1)} %copy.60), kind=kLoop, calls=%fused_computation.15 | loop fusion | flops 7815168 | bytes 901120 | tf_op jit(solution)/shard_map/reduce_sum | solution.py:128
  241.5 0.8 concatenate.21
  242.5 0.8 concatenate.20
  243.5 0.8 concatenate.19
  244.3 57.1 %all-to-all-done = bf16[32,36,2048]{2,1,0:T(8,128)(2,1)} async-done(((bf16[32,36,2048]{2,1,0:T(8,128)(2,1)}), bf16[32,36,2048]{2,1,0:T(8,128)(2,1)}, u32[]{:S(2)}, u32[]{:S(2)}) %all-to-all-start) | async-done | bytes 4718624 | tf_op jit(solution)/shard_map/all_to_all | solution.py:117
  301.4 5.0 %convolution_bitcast_fusion = f32[384,2048]{1,0:T(8,128)S(1)} fusion(bf16[32,36,2048]{2,1,0:T(8,128)(2,1)} %all-to-all-done, bf16[128,32,36]{0,2,1:T(8,128)(2,1)S(1)} %copy-done.5, bf16[128,32,36]{0,2,1:T(8,128)(2,1)} %concatenate.20, bf16[128,32,36]{0,2,1:T(8,128)(2,1)} %concatenate.19), kind=kOutput, calls=%fused_computation.23 | convolution fusion | flops 1814593536 | bytes 8749056 | tf_op jit(solution)/shard_map/dot_general | solution.py:130
  306.4 1.0 fusion.21
  (78 shorter events, 4.4 us)
Async XLA Ops:
  7.2 157.8 %copy-start = (bf16[1,512,2048]{2,1,0:T(8,128)(2,1)S(1)}, bf16[1,512,2048]{2,1,0:T(8,128)(2,1)}, u32[]{:S(2)}) copy-start(bf16[1,512,2048]{2,1,0:T(8,128)(2,1)} %param.16) | copy-start | bytes 6291460
  7.2 65.5 %all-gather.3.cloned.1.call-start = ((), (), s32[]{:S(2)}) async-start(), calls=%async_computation.2 | async-start | bytes 5308416 | tf_op jit(solution)/shard_map/all_gather | solution.py:90
  11.9 116.0 %all-gather.5.cloned.1.call-start = ((), (), s32[]{:S(2)}) async-start(), calls=%async_computation.3 | async-start | bytes 4718592 | tf_op jit(solution)/shard_map/all_gather | solution.py:91
  85.1 2.9 copy-start.3
  88.1 50.5 %collective-permute-start = (bf16[288,2048]{1,0:T(8,128)(2,1)}, bf16[288,2048]{1,0:T(8,128)(2,1)}, u32[]{:S(2)}, u32[]{:S(2)}) collective-permute-start(bf16[288,2048]{1,0:T(8,128)(2,1)} %get-tuple-element.15), channel_id=1, source_target_pairs={{0,1},{1,2},{2,3},{3,0},{4,5},{5,6},{6,7},{7,4},{8,9},{9,10},{10,1... | collective-permute-start | bytes 3538952 | tf_op jit(solution)/shard_map/ppermute | solution.py:58
  89.5 54.0 %collective-permute-start.1 = (bf16[288,2048]{1,0:T(8,128)(2,1)}, bf16[288,2048]{1,0:T(8,128)(2,1)}, u32[]{:S(2)}, u32[]{:S(2)}) collective-permute-start(bf16[288,2048]{1,0:T(8,128)(2,1)} %get-tuple-element.14), channel_id=1, source_target_pairs={{0,2},{1,3},{2,0},{3,1},{4,6},{5,7},{6,4},{7,5},{8,10},{9,11},{10,... | collective-permute-start | bytes 3538952 | tf_op jit(solution)/shard_map/ppermute | solution.py:58
  92.3 52.7 %collective-permute-start.2 = (bf16[288,2048]{1,0:T(8,128)(2,1)S(1)}, bf16[288,2048]{1,0:T(8,128)(2,1)}, u32[]{:S(2)}, u32[]{:S(2)}) collective-permute-start(bf16[288,2048]{1,0:T(8,128)(2,1)S(1)} %get-tuple-element.13), channel_id=1, source_target_pairs={{0,3},{1,0},{2,1},{3,2},{4,7},{5,4},{6,5},{7,6},{8,11},{9,8},{10,9... | collective-permute-start | bytes 3538952 | tf_op jit(solution)/shard_map/ppermute | solution.py:58
  135.7 10.7 %copy-start.2 = (bf16[1152,2048]{1,0:T(8,128)(2,1)}, bf16[1152,2048]{1,0:T(8,128)(2,1)S(1)}, u32[]{:S(2)}) copy-start(bf16[1152,2048]{1,0:T(8,128)(2,1)S(1)} %fusion) | copy-start | bytes 14155780
  146.4 5.8 %copy-start.4 = (bf16[4,288,2048]{2,1,0:T(8,128)(2,1)}, bf16[4,288,2048]{2,1,0:T(8,128)(2,1)S(1)}, u32[]{:S(2)}) copy-start(bf16[4,288,2048]{2,1,0:T(8,128)(2,1)S(1)} %bitcast_dynamic-update-slice_fusion.4) | copy-start | bytes 14155780
  146.4 5.8 %copy-start.8 = (bf16[1,2048,512]{2,1,0:T(8,128)(2,1)S(1)}, bf16[1,2048,512]{2,1,0:T(8,128)(2,1)}, u32[]{:S(2)}) copy-start(bf16[1,2048,512]{2,1,0:T(8,128)(2,1)} %param.17) | copy-start | bytes 6291460
  146.4 5.8 %copy-start.9 = (bf16[1,2048,512]{2,1,0:T(8,128)(2,1)S(1)}, bf16[1,2048,512]{2,1,0:T(8,128)(2,1)}, u32[]{:S(2)}) copy-start(bf16[1,2048,512]{2,1,0:T(8,128)(2,1)} %param.15) | copy-start | bytes 6291460
  146.4 5.8 %copy-start.10 = (bf16[1,2048,512]{2,1,0:T(8,128)(2,1)S(1)}, bf16[1,2048,512]{2,1,0:T(8,128)(2,1)}, u32[]{:S(2)}) copy-start(bf16[1,2048,512]{2,1,0:T(8,128)(2,1)} %param.14) | copy-start | bytes 6291460
  148.3 36.6 %collective-permute-start.3 = (bf16[288,2048]{1,0:T(8,128)(2,1)}, bf16[288,2048]{1,0:T(8,128)(2,1)}, u32[]{:S(2)}, u32[]{:S(2)}) collective-permute-start(bf16[288,2048]{1,0:T(8,128)(2,1)} %get-tuple-element.12), channel_id=1, source_target_pairs={{0,1},{1,2},{2,3},{3,0},{4,5},{5,6},{6,7},{7,4},{8,9},{9,10},{10,1... | collective-permute-start | bytes 3538952 | tf_op jit(solution)/shard_map/ppermute | solution.py:58
  148.3 65.4 %collective-permute-start.4 = (bf16[288,2048]{1,0:T(8,128)(2,1)}, bf16[288,2048]{1,0:T(8,128)(2,1)}, u32[]{:S(2)}, u32[]{:S(2)}) collective-permute-start(bf16[288,2048]{1,0:T(8,128)(2,1)} %get-tuple-element.11), channel_id=1, source_target_pairs={{0,2},{1,3},{2,0},{3,1},{4,6},{5,7},{6,4},{7,5},{8,10},{9,11},{10,... | collective-permute-start | bytes 3538952 | tf_op jit(solution)/shard_map/ppermute | solution.py:58
  150.6 68.3 %collective-permute-start.5 = (bf16[288,2048]{1,0:T(8,128)(2,1)}, bf16[288,2048]{1,0:T(8,128)(2,1)}, u32[]{:S(2)}, u32[]{:S(2)}) collective-permute-start(bf16[288,2048]{1,0:T(8,128)(2,1)} %get-tuple-element.10), channel_id=1, source_target_pairs={{0,3},{1,0},{2,1},{3,2},{4,7},{5,4},{6,5},{7,6},{8,11},{9,8},{10,9... | collective-permute-start | bytes 3538952 | tf_op jit(solution)/shard_map/ppermute | solution.py:58
  159.8 2.9 copy-start.1
  176.1 125.4 %all-to-all-start = ((bf16[32,36,2048]{2,1,0:T(8,128)(2,1)}), bf16[32,36,2048]{2,1,0:T(8,128)(2,1)}, u32[]{:S(2)}, u32[]{:S(2)}) async-start(bf16[32,36,2048]{2,1,0:T(8,128)(2,1)} %convolution_convert_fusion.1), calls=%async_computation.1 | async-start | bytes 10485760 | tf_op jit(solution)/shard_map/all_to_all | solution.py:117
  184.7 122.7 %reduce-scatter.2.cloned.1.call-start = ((), (), s32[]{:S(2)}) async-start(), calls=%async_computation.4 | async-start | bytes 4718592 | tf_op jit(solution)/shard_map/reduce_scatter | solution.py:124
  235.4 0.7 copy-start.7
  235.4 0.8 copy-start.6
  242.3 59.1 %copy-start.5 = (bf16[128,32,36]{0,2,1:T(8,128)(2,1)S(1)}, bf16[128,32,36]{0,2,1:T(8,128)(2,1)}, u32[]{:S(2)}) copy-start(bf16[128,32,36]{0,2,1:T(8,128)(2,1)} %concatenate.21) | copy-start | bytes 884740
Sparse Core Ops, SparseCore 0:
  12.0 60.5 all-gather.2
  74.4 53.4 all-gather.4
  235.6 43.2 reduce-scatter.1

commit v9 on v6

--- a/solution.py
+++ b/solution.py
@@ -61,6 +61,17 @@
     return got.reshape(send.shape)
 
 
+def shift_along_z(recv, n_y, n_z):
+    chunks = recv.reshape(n_y, n_z, -1, recv.shape[-1])
+    me = lax.axis_index("ez")
+    got = jnp.zeros_like(chunks)
+    got = lax.dynamic_update_index_in_dim(got, chunks[:, 0], me, 1)
+    for shift in range(1, n_z):
+        moved = lax.ppermute(chunks[:, shift], "ez", perm=[(i, (i + shift) % n_z) for i in range(n_z)])
+        got = lax.dynamic_update_index_in_dim(got, moved, (me + n_z - shift) % n_z, 1)
+    return got.reshape(recv.shape)
+
+
 def per_device(tokens, cotangent, expert_ids, combine, w_gate, w_up, w_down, tangent_gate):
     n_z = lax.axis_size("ez")
     n_y = lax.axis_size("ey")
@@ -82,6 +93,13 @@
     src_of = jnp.sum(jnp.where(in_slot, token_no + 1.0, 0.0), axis=0) - 1.0
     weight_te = jnp.sum(jnp.where(chosen, combine[:, :, None], 0.0), axis=1)
     w_of = jnp.sum(jnp.where(in_slot, weight_te[:, :, None], 0.0), axis=0)
+    z_here = lax.axis_index("ez")
+    by_y = lambda t: t.reshape(n_z, n_y, capacity).transpose(1, 0, 2)
+    z_roll = (z_here + jnp.arange(n_z, dtype=jnp.int32)) % n_z
+    own_tok = jnp.take(by_y(src_of), z_roll, axis=1).reshape(-1).astype(jnp.int32)
+    own_w = jnp.take(by_y(w_of), z_roll, axis=1).reshape(-1)
+    send_c = (own_w[:, None] * select_rows(own_tok, cotangent)).astype(jnp.bfloat16)
+    recv_c = lax.all_to_all(send_c, "ey", split_axis=0, concat_axis=0, tiled=True)
     table = jnp.stack((src_of,) + split3(w_of)).astype(jnp.bfloat16)
     extra = 16
     table = jnp.pad(table.reshape(-1), (0, extra * model_width - 4 * slots))
@@ -89,7 +107,6 @@
     block = rows_dev + extra
 
     tok_g = lax.all_gather(packed, "ez", axis=0, tiled=True)
-    cot_g = lax.all_gather(cotangent, "ez", axis=0, tiled=True)
     table_g = tok_g.reshape(n_z, block, model_width)[:, rows_dev:].reshape(n_z, -1)
     table_g = table_g[:, : 4 * slots].reshape(n_z, 4, expert_count, capacity)
     z_me = lax.axis_index("ez")
@@ -100,7 +117,6 @@
     valid = src_tok >= 0
     z_of = jnp.arange(n_z, dtype=jnp.int32)[None, :, None]
     at_packed = jnp.where(valid, src_tok + z_of * block, -1).reshape(-1)
-    at_cot = jnp.where(valid, src_tok + z_of * rows_dev, -1).reshape(-1)
     send_rows = select_rows(at_packed, tok_g).astype(jnp.bfloat16)
 
     rows_flat = lax.all_to_all(send_rows, "ey", split_axis=0, concat_axis=0, tiled=True)
@@ -108,12 +124,10 @@
     up_e = w_up[0]
     down_e = w_down[0]
     tangent_e = tangent_gate[0]
-    send_scaled = (src_w.reshape(-1)[:, None] * select_rows(at_cot, cot_g)).astype(jnp.bfloat16)
     joined_e = jnp.concatenate([gate_e, up_e, tangent_e], axis=1)
     term, factor = forward_part(rows_flat, joined_e, down_e, (expert_count, capacity))
     returned = lax.all_to_all(term, ("ey", "ez"), split_axis=0, concat_axis=0, tiled=True)
-    _, send_scaled = lax.optimization_barrier((rows_flat, send_scaled))
-    scaled_flat = shift_along_y(send_scaled, n_y)
+    scaled_flat = shift_along_z(recv_c, n_y, n_z)
     coeff = backward_part(scaled_flat, down_e, factor)
     partial_hvp = lax.dot_general(
         rows_flat, coeff, (((0,), (0,)), ((), ())), preferred_element_type=jnp.float32

time: 312 us -> 380 us (1.22)
  starting transfers between devices: 17.2 us -> 45.1 us
  local copies, waits for them, and re-layouts: 23.5 us -> 47.5 us
  waiting for transfers between devices: 192 us -> 208 us
    all_gather x1, waiting for transfers between devices: 59.6 us -> 0.01 us  [per_device(): tok_g = lax.all_gather(packed, 'ez', axis=0, tiled=True)]
    all_to_all x0 -> x1, waiting for transfers between devices: none -> 54.6 us  [per_device(): lax.all_to_all(send_c, 'ey', split_axis=0, concat_axis=0, tiled=True)]
    ppermute x3 -> x7, waiting for transfers between devices: 32 us -> 73.1 us  [shift_along_z(): lax.ppermute(chunks[:, shift], 'ez', perm=[(i, (i + shift) % n_z) for i i...]
    all_gather x1 -> x0, waiting for transfers between devices: 37.5 us -> none  [per_device(): cot_g = lax.all_gather(cotangent, 'ez', axis=0, tiled=True)]
    all_to_all x1, waiting for transfers between devices: 54.1 us -> 80.1 us  [per_device(): lax.all_to_all(term, ('ey', 'ez'), split_axis=0, concat_axis=0, tiled=True)]
    ppermute x3 -> x7, starting transfers between devices: 3.24 us -> 16.5 us  [shift_along_z(): lax.ppermute(chunks[:, shift], 'ez', perm=[(i, (i + shift) % n_z) for i i...]
    all_to_all x1, starting transfers between devices: 8.6 us -> 18.4 us  [per_device(): lax.all_to_all(term, ('ey', 'ez'), split_axis=0, concat_axis=0, tiled=True)]
    all_to_all x0 -> x1, local copies, waits for them, and re-layouts: none -> 8.15 us  [per_device(): lax.all_to_all(send_c, 'ey', split_axis=0, concat_axis=0, tiled=True)]
  transfers between devices with their start and end apart: 8 -> 12, of which waited for: 7 -> 5; matrix products, arithmetic and copies ran while one was open for 24% -> 24% of each run, Pallas kernels for 0% -> 0%
where the time goes in v9:
time: 380 us; the launch traced here: 377 us
  waiting for transfers between devices  208 us (55%)
  matrix products  51.2 us (13%)
  local copies, waits for them, and re-layouts  47.5 us (12%)
  starting transfers between devices  45.1 us (12%)
  between operations  14.3 us (4%)
  other arithmetic  11.1 us (3%)
    all_to_all x1, waiting for transfers between devices, per_device(): lax.all_to_all(term, ('ey', 'ez'), split_axis=0, concat_axis=0, tiled=True)  80.1 us
    ppermute x7, waiting for transfers between devices, shift_along_z(): lax.ppermute(chunks[:, shift], 'ez', perm=[(i, (i + shift) % n_z) for i i...  73.1 us
    all_to_all x1, waiting for transfers between devices, per_device(): lax.all_to_all(send_c, 'ey', split_axis=0, concat_axis=0, tiled=True)  54.6 us
    all_to_all x1, starting transfers between devices, per_device(): lax.all_to_all(term, ('ey', 'ez'), split_axis=0, concat_axis=0, tiled=True)  18.4 us
    ppermute x7, starting transfers between devices, shift_along_z(): lax.ppermute(chunks[:, shift], 'ez', perm=[(i, (i + shift) % n_z) for i i...  16.5 us
    dot_general x2, matrix products, select_rows(): return jnp.dot(picks, source, preferred_element_type=jnp.float32)  14.9 us
    dot_general x1, matrix products, per_device(): lax.dot_general(rows_flat, coeff, (((0,), (0,)), ((), ())), preferred_ele...  14 us
    dynamic_update_slice x7, local copies, waits for them, and re-layouts, shift_along_z(): lax.dynamic_update_index_in_dim(got, moved, (me + n_z - shift) % n_z, 1)  11.5 us
  transfers between devices with their start and end apart: 12, of which 5 were waited for; matrix products, arithmetic and copies ran while one was open for 24% of the time, Pallas kernels for 0%

profile of v9, /device:TPU:32, one launch (start us, length us, event | category | flops | bytes accessed | tf_op | source)
XLA Modules:
  0.0 377.0 jit_solution(10250232533351527304)
XLA Ops:
  7.2 0.8 convert_reduce_fusion
  8.4 0.8 select_reduce_fusion.6
  9.2 0.4 select_reduce_fusion.4
  9.9 1.9 pad_maximum_fusion
  12.0 0.6 gather_fusion.1
  12.8 0.6 gather_fusion
  13.6 4.6 %fusion = bf16[1152,2048]{1,0:T(8,128)(2,1)} fusion(bf16[128,2048]{1,0:T(8,128)(2,1)} %param.11, f32[1152]{0:T(1024)S(1)} %mul.76, s32[1152]{0:T(1024)S(1)} %convert_element_type.59), kind=kOutput, calls=%fused_computation.4 | convolution fusion | flops 608845824 | bytes 5252096 | tf_op jit(solution)/shard_map/dot_general | solution.py:49
  18.2 4.9 %all-to-all-start.1 = ((bf16[4,288,2048]{2,1,0:T(8,128)(2,1)}), bf16[4,288,2048]{2,1,0:T(8,128)(2,1)}, u32[]{:S(2)}, u32[]{:S(2)}) async-start(bf16[4,288,2048]{2,1,0:T(8,128)(2,1)} %bitcast.80), calls=%async_computation.1 | async-start | bytes 9437184 | tf_op jit(solution)/shard_map/all_to_all | solution.py:102
  23.3 54.6 %all-to-all-done.1 = bf16[4,288,2048]{2,1,0:T(8,128)(2,1)} async-done(((bf16[4,288,2048]{2,1,0:T(8,128)(2,1)}), bf16[4,288,2048]{2,1,0:T(8,128)(2,1)}, u32[]{:S(2)}, u32[]{:S(2)}) %all-to-all-start.1) | async-done | bytes 4718624 | tf_op jit(solution)/shard_map/all_to_all | solution.py:102
  77.9 8.1 %copy.128 = bf16[4,288,2048]{2,0,1:T(4,128)(2,1)} copy(bf16[4,288,2048]{2,1,0:T(8,128)(2,1)} %all-to-all-done.1) | data formatting | bytes 9437184 | tf_op jit(solution)/shard_map/all_to_all | solution.py:102
  86.0 1.1 slice_bitcast_fusion.7
  87.4 0.6 reshape.150
  88.2 10.4 %convolution_convert_fusion = bf16[1152,2048]{1,0:T(8,128)(2,1)} fusion(bf16[1152,2048]{1,0:T(8,128)(2,1)} %all-gather.2.cloned.1.call-done, s32[1152]{0:T(1024)S(1)} %add_select_fusion), kind=kOutput, calls=%fused_computation.3 | convolution fusion | flops 5439504384 | bytes 9441792 | tf_op jit(solution)/shard_map/dot_general | solution.py:49
  98.6 5.0 %all-to-all-start = ((bf16[4,288,2048]{2,1,0:T(8,128)(2,1)}), bf16[4,288,2048]{2,1,0:T(8,128)(2,1)}, u32[]{:S(2)}, u32[]{:S(2)}) async-start(bf16[4,288,2048]{2,1,0:T(8,128)(2,1)} %bitcast.82), calls=%async_computation | async-start | bytes 9437184 | tf_op jit(solution)/shard_map/all_to_all | solution.py:122
  103.6 5.3 %slice_bitcast_fusion = (bf16[4,36,2048]{2,0,1:T(4,128)(2,1)}, bf16[4,36,2048]{2,0,1:T(4,128)(2,1)}, bf16[4,36,2048]{2,0,1:T(4,128)(2,1)S(1)}, bf16[4,36,2048]{2...) fusion(bf16[4,8,36,2048]{3,0,2,1:T(4,128)(2,1)} %bitcast.81), kind=kLoop, calls=%fused_computation.50 | loop fusion | bytes 9437184 | tf_op jit(solution)/shard_map/squeeze | solution.py:70
  108.8 2.0 collective-permute-start
  110.8 4.5 %collective-permute-start.1 = (bf16[4,36,2048]{2,0,1:T(4,128)(2,1)}, bf16[4,36,2048]{2,0,1:T(4,128)(2,1)S(1)}, u32[]{:S(2)}, u32[]{:S(2)}) collective-permute-start(bf16[4,36,2048]{2,0,1:T(4,128)(2,1)} %get-tuple-element.13), channel_id=1, source_target_pairs={{0,8},{4,12},{8,16},{12,20},{16,24},{20,28},{24,0},{28,4},{1,9},{5... | collective-permute-start | bytes 1769480 | tf_op jit(solution)/shard_map/ppermute | solution.py:70
  115.3 1.9 collective-permute-start.2
  117.2 1.4 collective-permute-start.3
  118.7 3.4 collective-permute-start.4
  122.1 3.0 broadcast_in_dim.124
  125.1 1.2 copy_dynamic-update-slice_fusion.7
  126.3 3.9 %collective-permute-done = bf16[4,36,2048]{2,0,1:T(4,128)(2,1)} collective-permute-done((bf16[4,36,2048]{2,0,1:T(4,128)(2,1)}, bf16[4,36,2048]{2,0,1:T(4,128)(2,1)}, u32[]{:S(2)}, u32[]{:S(2)}) %collective-permute-start) | collective-permute-done | bytes 589856 | tf_op jit(solution)/shard_map/ppermute | solution.py:70
  130.2 2.3 collective-permute-start.5
  132.5 2.2 copy_dynamic-update-slice_fusion.6
  134.8 24.4 %collective-permute-done.1 = bf16[4,36,2048]{2,0,1:T(4,128)(2,1)S(1)} collective-permute-done((bf16[4,36,2048]{2,0,1:T(4,128)(2,1)}, bf16[4,36,2048]{2,0,1:T(4,128)(2,1)S(1)}, u32[]{:S(2)}, u32[]{:S(2)}) %collective-permute-start.1) | collective-permute-done | bytes 589856 | tf_op jit(solution)/shard_map/ppermute | solution.py:70
  159.2 0.9 collective-permute-start.6
  160.1 1.2 copy_dynamic-update-slice_fusion.5
  161.3 44.8 %collective-permute-done.2 = bf16[4,36,2048]{2,0,1:T(4,128)(2,1)S(1)} collective-permute-done((bf16[4,36,2048]{2,0,1:T(4,128)(2,1)}, bf16[4,36,2048]{2,0,1:T(4,128)(2,1)S(1)}, u32[]{:S(2)}, u32[]{:S(2)}) %collective-permute-start.2) | collective-permute-done | bytes 589856 | tf_op jit(solution)/shard_map/ppermute | solution.py:70
  206.1 1.2 copy_dynamic-update-slice_fusion.4
  207.2 1.2 copy_dynamic-update-slice_fusion.3
  208.5 1.2 copy_dynamic-update-slice_fusion.2
  209.7 11.3 %fusion.1 = f32[1152,1536]{1,0:T(8,128)S(1)} fusion(bf16[1152,2048]{1,0:T(8,128)(2,1)} %bitcast.5, bf16[2048,512]{1,0:T(8,128)(2,1)} %bitcast.92, bf16[2048,512]{1,0:T(8,128)(2,1)} %bitcast.93, bf16[2048,512]{1,0:T(8,128)(2,1)} %bitcast.94), kind=kOutput, calls=%fused_computation.5 | convolution fusion | flops 7266631680 | bytes 18087936 | tf_op jit(solution)/shard_map/dot_general | solution.py:18
  221.0 2.9 copy-done.1
  223.9 1.0 fusion.16
  224.9 1.3 reshape.154
  226.2 5.9 %convolution_convert_fusion.1 = bf16[32,36,2048]{2,1,0:T(8,128)(2,1)} fusion(bf16[32,36,512]{2,1,0:T(8,128)(2,1)} %reshape.154, bf16[1,512,2048]{2,1,0:T(8,128)(2,1)S(1)} %copy-done), kind=kOutput, calls=%fused_computation.16 | convolution fusion | flops 2418278400 | bytes 7995392 | tf_op jit(solution)/shard_map/dot_general | solution.py:24
  232.1 18.4 %all-to-all-start.2 = ((bf16[32,36,2048]{2,1,0:T(8,128)(2,1)}), bf16[32,36,2048]{2,1,0:T(8,128)(2,1)}, u32[]{:S(2)}, u32[]{:S(2)}) async-start(bf16[32,36,2048]{2,1,0:T(8,128)(2,1)} %convolution_convert_fusion.1), calls=%async_computation.3 | async-start | bytes 10485760 | tf_op jit(solution)/shard_map/all_to_all | solution.py:129
  250.8 2.3 copy_dynamic-update-slice_fusion.1
  253.1 2.3 copy_dynamic-update-slice_fusion
  255.3 7.3 %reshape.153 = bf16[1152,2048]{1,0:T(8,128)(2,1)} reshape(bf16[4,8,36,2048]{3,2,1,0:T(8,128)(2,1)} %copy_dynamic-update-slice_fusion) | data formatting | bytes 9437184 | tf_op jit(solution)/shard_map/reshape | solution.py:72
  262.6 14.0 %fusion.37 = f32[2048,512]{1,0:T(8,128)} fusion(bf16[1152,2048]{1,0:T(8,128)(2,1)} %bitcast.5, bf16[1152,2048]{1,0:T(8,128)(2,1)} %reshape.153, f32[1152,1536]{1,0:T(8,128)} %copy-done.1, bf16[1,512,2048]{2,1,0:T(8,128)(2,1)S(1)} %copy-done), kind=kOutput, calls=%fused_computation.100 | convolution fusion | flops 4840095744 | bytes 22806528 | tf_op jit(solution)/shard_map/dot_general | solution.py:132
  277.1 4.7 %select_reduce_fusion.2 = (bf16[128,1152]{1,0:T(8,128)(2,1)S(1)}, bf16[128,1152]{1,0:T(8,128)(2,1)S(1)}, bf16[128,1152]{1,0:T(8,128)(2,1)S(1)}) fusion(f32[128,8]{1,0:T(8,128)S(1)} %copy.139, s32[128,8]{1,0:T(8,128)S(1)} %copy.138, f32[128,8]{1,0:T(8,128)S(1)} %copy.143, f32[128,8]{1,0:T(8,128)S(1)} %copy.141), kind=kLoop, calls=%fused_computation.14 | loop fusion | flops 7815168 | bytes 901120 | tf_op jit(solution)/shard_map/reduce_sum | solution.py:139
  282.0 0.8 concatenate.19
  283.3 0.8 concatenate.21
  284.1 80.1 %all-to-all-done.2 = bf16[32,36,2048]{2,1,0:T(8,128)(2,1)} async-done(((bf16[32,36,2048]{2,1,0:T(8,128)(2,1)}), bf16[32,36,2048]{2,1,0:T(8,128)(2,1)}, u32[]{:S(2)}, u32[]{:S(2)}) %all-to-all-start.2) | async-done | bytes 4718624 | tf_op jit(solution)/shard_map/all_to_all | solution.py:129
  364.2 5.0 %convolution_bitcast_fusion = f32[384,2048]{1,0:T(8,128)S(1)} fusion(bf16[32,36,2048]{2,1,0:T(8,128)(2,1)} %all-to-all-done.2, bf16[128,32,36]{0,2,1:T(8,128)(2,1)} %concatenate.21, bf16[128,32,36]{0,2,1:T(8,128)(2,1)S(1)} %concatenate.20, bf16[128,32,36]{0,2,1:T(8,128)(2,1)} %concatenate.19), kind=kOutput, calls=%fused_computation.21 | convolution fusion | flops 1814593536 | bytes 8749056 | tf_op jit(solution)/shard_map/dot_general | solution.py:141
  369.2 1.0 fusion.19
  (62 shorter events, 3.4 us)
Async XLA Ops:
  7.2 219.0 %copy-start = (bf16[1,512,2048]{2,1,0:T(8,128)(2,1)S(1)}, bf16[1,512,2048]{2,1,0:T(8,128)(2,1)}, u32[]{:S(2)}) copy-start(bf16[1,512,2048]{2,1,0:T(8,128)(2,1)} %param.16) | copy-start | bytes 6291460
  7.2 78.8 %all-gather.2.cloned.1.call-start = ((), (), s32[]{:S(2)}) async-start(), calls=%async_computation.4 | async-start | bytes 5308416 | tf_op jit(solution)/shard_map/all_gather | solution.py:109
  18.2 59.7 %all-to-all-start.1 = ((bf16[4,288,2048]{2,1,0:T(8,128)(2,1)}), bf16[4,288,2048]{2,1,0:T(8,128)(2,1)}, u32[]{:S(2)}, u32[]{:S(2)}) async-start(bf16[4,288,2048]{2,1,0:T(8,128)(2,1)} %bitcast.80), calls=%async_computation.1 | async-start | bytes 9437184 | tf_op jit(solution)/shard_map/all_to_all | solution.py:102
  98.6 111.0 %all-to-all-start = ((bf16[4,288,2048]{2,1,0:T(8,128)(2,1)}), bf16[4,288,2048]{2,1,0:T(8,128)(2,1)}, u32[]{:S(2)}, u32[]{:S(2)}) async-start(bf16[4,288,2048]{2,1,0:T(8,128)(2,1)} %bitcast.82), calls=%async_computation | async-start | bytes 9437184 | tf_op jit(solution)/shard_map/all_to_all | solution.py:122
  108.8 21.4 %collective-permute-start = (bf16[4,36,2048]{2,0,1:T(4,128)(2,1)}, bf16[4,36,2048]{2,0,1:T(4,128)(2,1)}, u32[]{:S(2)}, u32[]{:S(2)}) collective-permute-start(bf16[4,36,2048]{2,0,1:T(4,128)(2,1)} %get-tuple-element.14), channel_id=1, source_target_pairs={{0,4},{4,8},{8,12},{12,16},{16,20},{20,24},{24,28},{28,0},{1,5},{5... | collective-permute-start | bytes 1769480 | tf_op jit(solution)/shard_map/ppermute | solution.py:70
  110.8 48.3 %collective-permute-start.1 = (bf16[4,36,2048]{2,0,1:T(4,128)(2,1)}, bf16[4,36,2048]{2,0,1:T(4,128)(2,1)S(1)}, u32[]{:S(2)}, u32[]{:S(2)}) collective-permute-start(bf16[4,36,2048]{2,0,1:T(4,128)(2,1)} %get-tuple-element.13), channel_id=1, source_target_pairs={{0,8},{4,12},{8,16},{12,20},{16,24},{20,28},{24,0},{28,4},{1,9},{5... | collective-permute-start | bytes 1769480 | tf_op jit(solution)/shard_map/ppermute | solution.py:70
  115.3 90.8 %collective-permute-start.2 = (bf16[4,36,2048]{2,0,1:T(4,128)(2,1)}, bf16[4,36,2048]{2,0,1:T(4,128)(2,1)S(1)}, u32[]{:S(2)}, u32[]{:S(2)}) collective-permute-start(bf16[4,36,2048]{2,0,1:T(4,128)(2,1)} %get-tuple-element.12), channel_id=1, source_target_pairs={{0,12},{4,16},{8,20},{12,24},{16,28},{20,0},{24,4},{28,8},{1,13},{... | collective-permute-start | bytes 1769480 | tf_op jit(solution)/shard_map/ppermute | solution.py:70
  117.2 90.0 %collective-permute-start.3 = (bf16[4,36,2048]{2,0,1:T(4,128)(2,1)}, bf16[4,36,2048]{2,0,1:T(4,128)(2,1)S(1)}, u32[]{:S(2)}, u32[]{:S(2)}) collective-permute-start(bf16[4,36,2048]{2,0,1:T(4,128)(2,1)} %get-tuple-element.11), channel_id=1, source_target_pairs={{0,16},{4,20},{8,24},{12,28},{16,0},{20,4},{24,8},{28,12},{1,17},{... | collective-permute-start | bytes 1769480 | tf_op jit(solution)/shard_map/ppermute | solution.py:70
  118.7 89.8 %collective-permute-start.4 = (bf16[4,36,2048]{2,0,1:T(4,128)(2,1)S(1)}, bf16[4,36,2048]{2,0,1:T(4,128)(2,1)S(1)}, u32[]{:S(2)}, u32[]{:S(2)}) collective-permute-start(bf16[4,36,2048]{2,0,1:T(4,128)(2,1)S(1)} %get-tuple-element.10), channel_id=1, source_target_pairs={{0,20},{4,24},{8,28},{12,0},{16,4},{20,8},{24,12},{28,16},{1,21},{... | collective-permute-start | bytes 1769480 | tf_op jit(solution)/shard_map/ppermute | solution.py:70
  130.2 120.6 %collective-permute-start.5 = (bf16[4,36,2048]{2,0,1:T(4,128)(2,1)}, bf16[4,36,2048]{2,0,1:T(4,128)(2,1)}, u32[]{:S(2)}, u32[]{:S(2)}) collective-permute-start(bf16[4,36,2048]{2,0,1:T(4,128)(2,1)} %get-tuple-element.9), channel_id=1, source_target_pairs={{0,24},{4,28},{8,0},{12,4},{16,8},{20,12},{24,16},{28,20},{1,25},{... | collective-permute-start | bytes 1769480 | tf_op jit(solution)/shard_map/ppermute | solution.py:70
  159.2 93.9 %collective-permute-start.6 = (bf16[4,36,2048]{2,0,1:T(4,128)(2,1)}, bf16[4,36,2048]{2,0,1:T(4,128)(2,1)}, u32[]{:S(2)}, u32[]{:S(2)}) collective-permute-start(bf16[4,36,2048]{2,0,1:T(4,128)(2,1)} %get-tuple-element.8), channel_id=1, source_target_pairs={{0,28},{4,0},{8,4},{12,8},{16,12},{20,16},{24,20},{28,24},{1,29},{... | collective-permute-start | bytes 1769480 | tf_op jit(solution)/shard_map/ppermute | solution.py:70
  221.0 2.9 copy-start.1
  232.1 132.1 %all-to-all-start.2 = ((bf16[32,36,2048]{2,1,0:T(8,128)(2,1)}), bf16[32,36,2048]{2,1,0:T(8,128)(2,1)}, u32[]{:S(2)}, u32[]{:S(2)}) async-start(bf16[32,36,2048]{2,1,0:T(8,128)(2,1)} %convolution_convert_fusion.1), calls=%async_computation.3 | async-start | bytes 10485760 | tf_op jit(solution)/shard_map/all_to_all | solution.py:129
  250.5 119.6 %reduce-scatter.2.cloned.1.call-start = ((), (), s32[]{:S(2)}) async-start(), calls=%async_computation.5 | async-start | bytes 4718592 | tf_op jit(solution)/shard_map/reduce_scatter | solution.py:135
  262.6 14.0 %copy-start.2 = (s32[128,8]{0,1:T(8,128)S(1)}, s32[128,8]{0,1:T(8,128)}, u32[]{:S(2)}) copy-start(s32[128,8]{0,1:T(8,128)} %param.12) | copy-start | bytes 12292
  262.6 14.2 %copy-start.3 = (f32[128,8]{0,1:T(8,128)S(1)}, f32[128,8]{0,1:T(8,128)}, u32[]{:S(2)}) copy-start(f32[128,8]{0,1:T(8,128)} %param.13) | copy-start | bytes 12292
Sparse Core Ops, SparseCore 0:
  12.0 60.5 all-gather.1
  276.7 42.2 reduce-scatter.1

commit v10 on v6

--- a/solution.py
+++ b/solution.py
@@ -52,13 +52,12 @@
 def shift_along_y(send, n_y):
     chunks = send.reshape(n_y, -1, send.shape[-1])
     me = lax.axis_index("ey")
-    got = jnp.zeros_like(chunks)
-    got = lax.dynamic_update_index_in_dim(got, lax.dynamic_index_in_dim(chunks, me, 0, False), me, 0)
+    arrived = [lax.dynamic_index_in_dim(chunks, me, 0, False)]
     for shift in range(1, n_y):
         out = lax.dynamic_index_in_dim(chunks, (me + shift) % n_y, 0, False)
-        moved = lax.ppermute(out, "ey", perm=[(i, (i + shift) % n_y) for i in range(n_y)])
-        got = lax.dynamic_update_index_in_dim(got, moved, (me + n_y - shift) % n_y, 0)
-    return got.reshape(send.shape)
+        arrived.append(lax.ppermute(out, "ey", perm=[(i, (i + shift) % n_y) for i in range(n_y)]))
+    got = [lax.select_n((me + n_y - p) % n_y, *arrived) for p in range(n_y)]
+    return jnp.stack(got).reshape(send.shape)
 
 
 def per_device(tokens, cotangent, expert_ids, combine, w_gate, w_up, w_down, tangent_gate):

time: 312 us -> 312 us (level)
  local copies, waits for them, and re-layouts: 23.5 us -> 15.3 us
  other arithmetic: 10.9 us -> 16 us
    dynamic_update_slice x3 -> x0, local copies, waits for them, and re-layouts: 7.35 us -> none  [shift_along_y(): lax.dynamic_update_index_in_dim(got, moved, (me + n_y - shift) % n_y, 0)]
    another operation x1 -> x3, other arithmetic: 0.01 us -> 5.08 us  [the longest x2 5.07 us: shift_along_y(): return jnp.stack(got).reshape(send.shape)]
    ppermute x3, waiting for transfers between devices: 32 us -> 36.9 us  [shift_along_y(): lax.ppermute(out, 'ey', perm=[(i, (i + shift) % n_y) for i in range(n_y)])]
    unnamed x22 -> x18, local copies, waits for them, and re-layouts: 7.32 us -> 4.97 us
where the time goes in v10:
time: 312 us
  waiting for transfers between devices  194 us (62%)
  matrix products  54.5 us (17%)
  starting transfers between devices  17.8 us (6%)
  other arithmetic  16 us (5%)
  local copies, waits for them, and re-layouts  15.3 us (5%)
  between operations  14.1 us (5%)
    all_gather x1, waiting for transfers between devices, per_device(): tok_g = lax.all_gather(packed, 'ez', axis=0, tiled=True)  59.6 us
    all_to_all x1, waiting for transfers between devices, per_device(): lax.all_to_all(term, ('ey', 'ez'), split_axis=0, concat_axis=0, tiled=True)  51.4 us
    all_gather x1, waiting for transfers between devices, per_device(): cot_g = lax.all_gather(cotangent, 'ez', axis=0, tiled=True)  37.5 us
    ppermute x3, waiting for transfers between devices, shift_along_y(): lax.ppermute(out, 'ey', perm=[(i, (i + shift) % n_y) for i in range(n_y)])  36.9 us
    dot_general x2, matrix products, select_rows(): return jnp.dot(picks, source, preferred_element_type=jnp.float32)  19.6 us
    dot_general x1, matrix products, per_device(): lax.dot_general(rows_flat, coeff, (((0,), (0,)), ((), ())), preferred_ele...  14.1 us
    dot_general x1, matrix products, forward_part(): acts = jnp.dot(rows_flat, joined_e, preferred_element_type=jnp.float32)  9.92 us
    all_to_all x1, starting transfers between devices, per_device(): lax.all_to_all(term, ('ey', 'ez'), split_axis=0, concat_axis=0, tiled=True)  9.2 us
  transfers between devices with their start and end apart: 8, of which 7 were waited for; matrix products, arithmetic and copies ran while one was open for 24% of the time, Pallas kernels for 0%

profile of v10, /device:TPU:32, one launch (start us, length us, event | category | flops | bytes accessed | tf_op | source)
XLA Modules:
  0.0 311.6 jit_solution(17858314937653101592)
XLA Ops:
  7.2 0.8 convert_reduce_fusion
  8.2 0.2 reduce_window_sum.11
  8.4 0.8 select_reduce_fusion.6
  9.2 0.4 select_reduce_fusion.4
  9.6 0.1 copy.60
  9.8 0.1 convert_element_type.47
  9.9 1.9 pad_maximum_fusion.1
  11.9 0.7 all-gather.5.cloned.1.call-update
  13.0 59.6 %all-gather.3.cloned.1.call-done = bf16[1152,2048]{1,0:T(8,128)(2,1)} async-done(((bf16[144,2048]{1,0:T(8,128)(2,1)}), bf16[1152,2048]{1,0:T(8,128)(2,1)}) %all-gather.3.cloned.1.call-update) | async-done | bytes 4718608 | tf_op jit(solution)/shard_map/all_gather | solution.py:90
  72.6 1.1 slice_bitcast_fusion
  73.7 0.3 copy.71
  74.0 0.6 reshape.159
  74.8 10.4 %convolution_convert_fusion = bf16[1152,2048]{1,0:T(8,128)(2,1)} fusion(bf16[1152,2048]{1,0:T(8,128)(2,1)} %all-gather.3.cloned.1.call-done, s32[1152]{0:T(1024)S(1)} %get-tuple-element.22), kind=kOutput, calls=%fused_computation.1 | convolution fusion | flops 5439504384 | bytes 9441792 | tf_op jit(solution)/shard_map/dot_general | solution.py:49
  85.2 5.0 %all-to-all-start = ((bf16[4,288,2048]{2,1,0:T(8,128)(2,1)}), bf16[4,288,2048]{2,1,0:T(8,128)(2,1)}, u32[]{:S(2)}, u32[]{:S(2)}) async-start(bf16[4,288,2048]{2,1,0:T(8,128)(2,1)} %bitcast.87), calls=%async_computation | async-start | bytes 9437184 | tf_op jit(solution)/shard_map/all_to_all | solution.py:105
  90.4 37.5 %all-gather.5.cloned.1.call-done = bf16[1024,2048]{1,0:T(8,128)(2,1)} async-done(((bf16[128,2048]{1,0:T(8,128)(2,1)}), bf16[1024,2048]{1,0:T(8,128)(2,1)}) %all-gather.5.cloned.1.call-update) | async-done | bytes 4194320 | tf_op jit(solution)/shard_map/all_gather | solution.py:91
  127.8 9.2 %fusion = bf16[1152,2048]{1,0:T(8,128)(2,1)} fusion(bf16[1024,2048]{1,0:T(8,128)(2,1)} %all-gather.5.cloned.1.call-done, f32[1152]{0:T(1024)S(1)} %add.162, s32[1152]{0:T(1024)S(1)} %get-tuple-element.21), kind=kOutput, calls=%fused_computation.2 | convolution fusion | flops 4837736448 | bytes 8922112 | tf_op jit(solution)/shard_map/dot_general | solution.py:49
  137.0 7.9 %all-to-all-done = bf16[4,288,2048]{2,1,0:T(8,128)(2,1)} async-done(((bf16[4,288,2048]{2,1,0:T(8,128)(2,1)}), bf16[4,288,2048]{2,1,0:T(8,128)(2,1)}, u32[]{:S(2)}, u32[]{:S(2)}) %all-to-all-start) | async-done | bytes 4718624 | tf_op jit(solution)/shard_map/all_to_all | solution.py:105
  144.9 4.1 %dynamic-slice_bitcast_fusion = (bf16[288,2048]{1,0:T(8,128)(2,1)}, bf16[288,2048]{1,0:T(8,128)(2,1)}, bf16[288,2048]{1,0:T(8,128)(2,1)}) fusion(bf16[4,288,2048]{2,1,0:T(8,128)(2,1)} %bitcast.85, s32[]{:T(128)S(6)} %select_n.217, s32[]{:T(128)S(6)} %select_n.215, s32[]{:T(128)S(6)} %select_n.210), kind=kLoop, calls=%fused_computation.47 | loop fusion | bytes 7077900 | tf_op jit(solution)/shard_map/jit(dynamic_index_in_dim)/squeeze | solution.py:57
  149.0 0.6 collective-permute-start
  149.6 2.1 collective-permute-start.1
  151.6 0.6 collective-permute-start.2
  152.3 9.9 %fusion.1 = f32[1152,1536]{1,0:T(8,128)S(1)} fusion(bf16[1152,2048]{1,0:T(8,128)(2,1)} %bitcast.5, bf16[2048,512]{1,0:T(8,128)(2,1)S(1)} %bitcast.91, bf16[2048,512]{1,0:T(8,128)(2,1)S(1)} %bitcast.92, bf16[2048,512]{1,0:T(8,128)(2,1)S(1)} %bitcast.93), kind=kOutput, calls=%fused_computation.3 | convolution fusion | flops 7266631680 | bytes 18087936 | tf_op jit(solution)/shard_map/dot_general | solution.py:18
  162.2 2.9 copy-done.1
  165.1 1.0 fusion.16
  166.1 1.2 reshape.162
  167.3 5.9 %convolution_convert_fusion.1 = bf16[32,36,2048]{2,1,0:T(8,128)(2,1)} fusion(bf16[32,36,512]{2,1,0:T(8,128)(2,1)} %reshape.162, bf16[1,512,2048]{2,1,0:T(8,128)(2,1)S(1)} %copy-done), kind=kOutput, calls=%fused_computation.16 | convolution fusion | flops 2418278400 | bytes 7995392 | tf_op jit(solution)/shard_map/dot_general | solution.py:24
  173.3 9.2 %all-to-all-start.1 = ((bf16[32,36,2048]{2,1,0:T(8,128)(2,1)}), bf16[32,36,2048]{2,1,0:T(8,128)(2,1)}, u32[]{:S(2)}, u32[]{:S(2)}) async-start(bf16[32,36,2048]{2,1,0:T(8,128)(2,1)} %convolution_convert_fusion.1), calls=%async_computation.2 | async-start | bytes 10485760 | tf_op jit(solution)/shard_map/all_to_all | solution.py:113
  182.5 0.3 reduce-scatter.2.cloned.1.call-start
  182.8 30.3 %collective-permute-done = bf16[288,2048]{1,0:T(8,128)(2,1)} collective-permute-done((bf16[288,2048]{1,0:T(8,128)(2,1)}, bf16[288,2048]{1,0:T(8,128)(2,1)}, u32[]{:S(2)}, u32[]{:S(2)}) %collective-permute-start) | collective-permute-done | bytes 1179680 | tf_op jit(solution)/shard_map/ppermute | solution.py:58
  213.0 3.0 collective-permute-done.1
  216.0 3.6 %collective-permute-done.2 = bf16[288,2048]{1,0:T(8,128)(2,1)} collective-permute-done((bf16[288,2048]{1,0:T(8,128)(2,1)}, bf16[288,2048]{1,0:T(8,128)(2,1)}, u32[]{:S(2)}, u32[]{:S(2)}) %collective-permute-start.2) | collective-permute-done | bytes 1179680 | tf_op jit(solution)/shard_map/ppermute | solution.py:58
  219.6 2.6 fusion.21
  222.2 2.5 pad_maximum_fusion
  224.7 14.1 %fusion.46 = f32[2048,512]{1,0:T(8,128)} fusion(bf16[1152,2048]{1,0:T(8,128)(2,1)} %bitcast.5, bf16[1152,2048]{1,0:T(8,128)(2,1)} %bitcast.88, f32[1152,1536]{1,0:T(8,128)} %copy-done.1, bf16[1,512,2048]{2,1,0:T(8,128)(2,1)S(1)} %copy-done), kind=kOutput, calls=%fused_computation.98 | convolution fusion | flops 4840095744 | bytes 22806528 | tf_op jit(solution)/shard_map/dot_general | solution.py:117
  238.8 0.7 copy-done.3
  239.5 0.1 copy.63
  239.7 0.1 copy.64
  239.9 0.1 copy.68
  240.0 4.7 %select_reduce_fusion.2 = (bf16[128,1152]{1,0:T(8,128)(2,1)S(1)}, bf16[128,1152]{1,0:T(8,128)(2,1)S(1)}, bf16[128,1152]{1,0:T(8,128)(2,1)S(1)}) fusion(f32[128,8]{1,0:T(8,128)S(1)} %copy.64, s32[128,8]{1,0:T(8,128)S(1)} %copy.63, f32[128,8]{1,0:T(8,128)S(1)} %copy.68, f32[128,8]{1,0:T(8,128)S(1)} %copy.66), kind=kLoop, calls=%fused_computation.13 | loop fusion | flops 7815168 | bytes 901120 | tf_op jit(solution)/shard_map/reduce_sum | solution.py:124
  244.7 0.2 copy.65
  244.9 0.8 concatenate.19
  245.7 0.2 copy.67
  245.9 0.8 concatenate.20
  246.7 0.2 copy.69
  246.9 0.8 concatenate.21
  247.7 51.4 %all-to-all-done.1 = bf16[32,36,2048]{2,1,0:T(8,128)(2,1)} async-done(((bf16[32,36,2048]{2,1,0:T(8,128)(2,1)}), bf16[32,36,2048]{2,1,0:T(8,128)(2,1)}, u32[]{:S(2)}, u32[]{:S(2)}) %all-to-all-start.1) | async-done | bytes 4718624 | tf_op jit(solution)/shard_map/all_to_all | solution.py:113
  299.1 5.0 %convolution_bitcast_fusion = f32[384,2048]{1,0:T(8,128)S(1)} fusion(bf16[32,36,2048]{2,1,0:T(8,128)(2,1)} %all-to-all-done.1, bf16[128,32,36]{0,2,1:T(8,128)(2,1)} %concatenate.21, bf16[128,32,36]{0,2,1:T(8,128)(2,1)} %concatenate.20, bf16[128,32,36]{0,2,1:T(8,128)(2,1)S(1)} %copy-done.2), kind=kOutput, calls=%fused_computation.21 | convolution fusion | flops 1814593536 | bytes 8749056 | tf_op jit(solution)/shard_map/dot_general | solution.py:126
  304.1 1.0 fusion.28
  (46 shorter events, 1.2 us)
Async XLA Ops:
  7.2 160.2 %copy-start = (bf16[1,512,2048]{2,1,0:T(8,128)(2,1)S(1)}, bf16[1,512,2048]{2,1,0:T(8,128)(2,1)}, u32[]{:S(2)}) copy-start(bf16[1,512,2048]{2,1,0:T(8,128)(2,1)} %param.14) | copy-start | bytes 6291460
  7.2 65.4 %all-gather.3.cloned.1.call-start = ((), (), s32[]{:S(2)}) async-start(), calls=%async_computation.3 | async-start | bytes 5308416 | tf_op jit(solution)/shard_map/all_gather | solution.py:90
  11.9 115.9 %all-gather.5.cloned.1.call-start = ((), (), s32[]{:S(2)}) async-start(), calls=%async_computation.4 | async-start | bytes 4718592 | tf_op jit(solution)/shard_map/all_gather | solution.py:91
  85.2 59.8 %all-to-all-start = ((bf16[4,288,2048]{2,1,0:T(8,128)(2,1)}), bf16[4,288,2048]{2,1,0:T(8,128)(2,1)}, u32[]{:S(2)}, u32[]{:S(2)}) async-start(bf16[4,288,2048]{2,1,0:T(8,128)(2,1)} %bitcast.87), calls=%async_computation | async-start | bytes 9437184 | tf_op jit(solution)/shard_map/all_to_all | solution.py:105
  144.9 7.3 %copy-start.5 = (bf16[1,2048,512]{2,1,0:T(8,128)(2,1)S(1)}, bf16[1,2048,512]{2,1,0:T(8,128)(2,1)}, u32[]{:S(2)}) copy-start(bf16[1,2048,512]{2,1,0:T(8,128)(2,1)} %param.15) | copy-start | bytes 6291460
  144.9 7.3 %copy-start.6 = (bf16[1,2048,512]{2,1,0:T(8,128)(2,1)S(1)}, bf16[1,2048,512]{2,1,0:T(8,128)(2,1)}, u32[]{:S(2)}) copy-start(bf16[1,2048,512]{2,1,0:T(8,128)(2,1)} %param.13) | copy-start | bytes 6291460
  144.9 7.3 %copy-start.7 = (bf16[1,2048,512]{2,1,0:T(8,128)(2,1)S(1)}, bf16[1,2048,512]{2,1,0:T(8,128)(2,1)}, u32[]{:S(2)}) copy-start(bf16[1,2048,512]{2,1,0:T(8,128)(2,1)} %param.12) | copy-start | bytes 6291460
  149.0 64.0 %collective-permute-start = (bf16[288,2048]{1,0:T(8,128)(2,1)}, bf16[288,2048]{1,0:T(8,128)(2,1)}, u32[]{:S(2)}, u32[]{:S(2)}) collective-permute-start(bf16[288,2048]{1,0:T(8,128)(2,1)} %get-tuple-element.15), channel_id=1, source_target_pairs={{0,1},{1,2},{2,3},{3,0},{4,5},{5,6},{6,7},{7,4},{8,9},{9,10},{10,1... | collective-permute-start | bytes 3538952 | tf_op jit(solution)/shard_map/ppermute | solution.py:58
  149.6 66.4 %collective-permute-start.1 = (bf16[288,2048]{1,0:T(8,128)(2,1)}, bf16[288,2048]{1,0:T(8,128)(2,1)}, u32[]{:S(2)}, u32[]{:S(2)}) collective-permute-start(bf16[288,2048]{1,0:T(8,128)(2,1)} %get-tuple-element.14), channel_id=1, source_target_pairs={{0,2},{1,3},{2,0},{3,1},{4,6},{5,7},{6,4},{7,5},{8,10},{9,11},{10,... | collective-permute-start | bytes 3538952 | tf_op jit(solution)/shard_map/ppermute | solution.py:58
  151.6 68.0 %collective-permute-start.2 = (bf16[288,2048]{1,0:T(8,128)(2,1)}, bf16[288,2048]{1,0:T(8,128)(2,1)}, u32[]{:S(2)}, u32[]{:S(2)}) collective-permute-start(bf16[288,2048]{1,0:T(8,128)(2,1)} %get-tuple-element.13), channel_id=1, source_target_pairs={{0,3},{1,0},{2,1},{3,2},{4,7},{5,4},{6,5},{7,6},{8,11},{9,8},{10,9... | collective-permute-start | bytes 3538952 | tf_op jit(solution)/shard_map/ppermute | solution.py:58
  162.2 2.9 copy-start.1
  173.3 125.8 %all-to-all-start.1 = ((bf16[32,36,2048]{2,1,0:T(8,128)(2,1)}), bf16[32,36,2048]{2,1,0:T(8,128)(2,1)}, u32[]{:S(2)}, u32[]{:S(2)}) async-start(bf16[32,36,2048]{2,1,0:T(8,128)(2,1)} %convolution_convert_fusion.1), calls=%async_computation.2 | async-start | bytes 10485760 | tf_op jit(solution)/shard_map/all_to_all | solution.py:113
  182.5 122.6 %reduce-scatter.2.cloned.1.call-start = ((), (), s32[]{:S(2)}) async-start(), calls=%async_computation.5 | async-start | bytes 4718592 | tf_op jit(solution)/shard_map/reduce_scatter | solution.py:120
  238.8 0.7 copy-start.3
  238.8 0.8 copy-start.4
  245.7 53.4 %copy-start.2 = (bf16[128,32,36]{0,2,1:T(8,128)(2,1)S(1)}, bf16[128,32,36]{0,2,1:T(8,128)(2,1)}, u32[]{:S(2)}) copy-start(bf16[128,32,36]{0,2,1:T(8,128)(2,1)} %concatenate.19) | copy-start | bytes 884740
Sparse Core Ops, SparseCore 0:
  12.0 60.5 all-gather.2
  74.4 53.4 all-gather.4
  239.0 45.7 reduce-scatter.1
